TPU v7x, 256 devices: a whole 4x4x8 slice. The times are simulated.
256 devices in a mesh: dp: 32 (over x, y, core), mp: 8 (over z).
Axes of the slice: x: 4, y: 4, z: 8, core: 2. Of those that a mesh axis runs over, the one named last changes fastest.
Arguments:
- hidden: bfloat16 [512, 1024], P('dp'), may hold values from -6 to 6
- attn_gain: float32 [1024], replicated, may hold values from 0.25 to 1.75
- w_qkv: bfloat16 [1024, 3, 1024], P(None, None, 'mp'), may hold values from -2 to 2
- w_out: bfloat16 [1024, 1024], P('mp'), may hold values from -0.1875 to 0.1875
- mlp_gain: float32 [1024], replicated, may hold values from 0.25 to 1.75
- w_gate_up: bfloat16 [1024, 2, 4096], P(None, None, 'mp'), may hold values from -0.1875 to 0.1875
- w_down: bfloat16 [4096, 1024], P('mp'), may hold values from -0.09375 to 0.09375
- kv_cache: bfloat16 [2, 4096, 128, 1024], P(None, 'dp', None, 'mp'), may hold values from -9 to 9
- lengths: int32 [512], replicated, may hold values from 1 to 16384, as said below
- page_request: int32 [4096], P('dp'), may hold values from -1 to 511, as said below
- page_index: int32 [4096], P('dp'), may hold values from 0 to 127, as said below
Outputs:
- appended: bfloat16 [2, 512, 1024], P(None, 'dp', 'mp')
- hidden_out: bfloat16 [512, 1024], P('dp')
Inputs may be any that keep to these rules, and one draw needn't show every extreme that they name: `lengths`: 4 requests hold exactly 16384 tokens, the others fewer than 512. `page_request`: each request owns exactly ceil(lengths / 128) pool pages, which may lie on any data devices; -1 marks an empty page. `page_index`: the pages of a request carry the places 0 to ceil(lengths / 128) - 1, each once; empty pages carry 0.
All inputs are finite; a program needn't handle non-finite values.
Results may differ from a plain program's by a relative error of at most 0.0085.
Values may be sent and summed in bfloat16 or wider, within the bound.
No kernel may reach another device: no remote copies, remote signals or barrier semaphores. Data moves between devices by JAX's collectives and lax.ppermute only.
A program may use at most 128 MiB of HBM per device.

v0:
```python
import jax
import jax.numpy as jnp
from jax import lax
from jax.sharding import PartitionSpec as P

HEAD_DIM = 64
PAGE_BLOCK = 8


EPSILON = 1e-05
NEGATIVE = -1e30


def merged_2(value, axis, join):
    pieces = jax.tree.map(lambda part: lax.all_gather(part, axis), value)
    head = jax.tree.map(lambda part: part[0], pieces)
    tail = jax.tree.map(lambda part: part[1:], pieces)
    running, _ = lax.scan(lambda running, piece: (join(running, piece), None), head, tail)
    return running


def rms_norm(values, gain):
    widened = values.astype(jnp.float32)
    mean_square = jnp.mean(widened * widened, axis=-1, keepdims=True)
    return (widened * lax.rsqrt(mean_square + EPSILON) * gain).astype(jnp.bfloat16)


def combine(first, second):
    largest = jnp.maximum(first[0], second[0])
    shrink_first = jnp.exp(first[0] - largest)
    shrink_second = jnp.exp(second[0] - largest)
    totals = first[1] * shrink_first + second[1] * shrink_second
    weighted = first[2] * shrink_first[:, :, None] + second[2] * shrink_second[:, :, None]
    return (largest, totals, weighted)


def body(
    hidden,
    attn_gain,
    w_qkv,
    w_out,
    mlp_gain,
    w_gate_up,
    w_down,
    kv_cache,
    lengths,
    page_request,
    page_index,
):
    local_rows = hidden.shape[0]
    head_cols = w_qkv.shape[2]
    local_heads = head_cols // HEAD_DIM
    pool_pages = kv_cache.shape[1]
    page_len = kv_cache.shape[2]
    data_devices = lax.axis_size("dp")
    requests = local_rows * data_devices
    score_scale = HEAD_DIM ** (-0.5)
    normed = rms_norm(hidden, attn_gain)
    projected = jnp.dot(
        normed, w_qkv.reshape(w_qkv.shape[0], 3 * head_cols), preferred_element_type=jnp.float32
    )
    projected = lax.optimization_barrier(projected.astype(jnp.bfloat16)).reshape(
        local_rows, 3, head_cols
    )
    appended = jnp.stack([projected[:, 1], projected[:, 2]])
    every_query = lax.all_gather(projected[:, 0], "dp", axis=0, tiled=True)
    own_queries = projected[:, 0].reshape(local_rows, local_heads, HEAD_DIM).astype(jnp.float32)
    own_keys = projected[:, 1].reshape(local_rows, local_heads, HEAD_DIM).astype(jnp.float32)
    own_values = projected[:, 2].reshape(local_rows, local_heads, HEAD_DIM).astype(jnp.float32)
    self_scores = jnp.sum(own_queries * own_keys, axis=-1) * score_scale
    home_row = lax.axis_index("dp") * local_rows
    start_max = lax.dynamic_update_slice(
        jnp.full((requests, local_heads), NEGATIVE, jnp.float32), self_scores, (home_row, 0)
    )
    start_totals = lax.dynamic_update_slice(
        jnp.zeros((requests, local_heads), jnp.float32),
        jnp.ones((local_rows, local_heads), jnp.float32),
        (home_row, 0),
    )
    start_weighted = lax.dynamic_update_slice(
        jnp.zeros((requests, local_heads, HEAD_DIM), jnp.float32), own_values, (home_row, 0, 0)
    )
    visit_order = jnp.arange(pool_pages, dtype=jnp.int32)
    trip_count = pool_pages // PAGE_BLOCK
    request_ids = jnp.arange(requests, dtype=jnp.int32)
    offsets = jnp.arange(page_len, dtype=jnp.int32)

    def visit(step_index, carry):
        running_max, totals, weighted = carry
        picked = lax.dynamic_slice_in_dim(visit_order, step_index * PAGE_BLOCK, PAGE_BLOCK, 0)
        fetched = jnp.take(kv_cache, picked, axis=1)
        owners = page_request[picked]
        page_pos = page_index[picked]
        clamped = jnp.maximum(owners, 0)
        chosen_queries = every_query[clamped].reshape(PAGE_BLOCK, local_heads, HEAD_DIM)
        key_rows = fetched[0].reshape(PAGE_BLOCK, page_len, local_heads, HEAD_DIM)
        value_rows = fetched[1].reshape(PAGE_BLOCK, page_len, local_heads, HEAD_DIM)
        scores = (
            jnp.einsum(
                "phd,pthd->pht", chosen_queries, key_rows, preferred_element_type=jnp.float32
            )
            * score_scale
        )
        position = page_pos[:, None] * page_len + offsets[None, :]
        usable = (owners[:, None] >= 0) & (position < lengths[clamped][:, None])
        page_max = jnp.max(jnp.where(usable[:, None, :], scores, NEGATIVE), axis=2)
        raw = jnp.where(usable[:, None, :], jnp.exp(scores - page_max[:, :, None]), 0.0)
        page_total = jnp.sum(raw, axis=2)
        page_sum = jnp.einsum(
            "pht,pthd->phd",
            raw.astype(jnp.bfloat16),
            value_rows,
            preferred_element_type=jnp.float32,
        )
        member = owners[:, None] == request_ids[None, :]
        candidate = jnp.max(jnp.where(member[:, :, None], page_max[:, None, :], NEGATIVE), axis=0)
        new_max = jnp.maximum(running_max, candidate)
        factors = jnp.where(owners[:, None] >= 0, jnp.exp(page_max - new_max[clamped]), 0.0)
        rescale = jnp.exp(running_max - new_max)
        onehot = member.astype(jnp.float32)
        totals = totals * rescale + jnp.einsum(
            "pr,ph->rh", onehot, page_total * factors, precision=lax.Precision.HIGHEST
        )
        weighted = weighted * rescale[:, :, None] + jnp.einsum(
            "pr,phd->rhd", onehot, page_sum * factors[:, :, None], precision=lax.Precision.HIGHEST
        )
        return (new_max, totals, weighted)

    running_max, totals, weighted = lax.fori_loop(
        0, trip_count, visit, (start_max, start_totals, start_weighted)
    )
    merged = merged_2((running_max, totals, weighted), "dp", combine)
    own_totals = lax.dynamic_slice_in_dim(merged[1], home_row, local_rows, 0)
    own_weighted = lax.dynamic_slice_in_dim(merged[2], home_row, local_rows, 0)
    context = (
        (own_weighted / own_totals[:, :, None]).reshape(local_rows, head_cols).astype(jnp.bfloat16)
    )
    attended = lax.psum(jnp.dot(context, w_out, preferred_element_type=jnp.float32), "mp")
    residual = lax.optimization_barrier(
        (hidden.astype(jnp.float32) + attended).astype(jnp.bfloat16)
    )
    normed_mlp = rms_norm(residual, mlp_gain)
    hidden_cols = w_gate_up.shape[2]
    gate_up = jnp.dot(
        normed_mlp,
        w_gate_up.reshape(w_gate_up.shape[0], 2 * hidden_cols),
        preferred_element_type=jnp.float32,
    ).reshape(local_rows, 2, hidden_cols)
    activated = (jax.nn.silu(gate_up[:, 0]) * gate_up[:, 1]).astype(jnp.bfloat16)
    lowered = lax.psum(jnp.dot(activated, w_down, preferred_element_type=jnp.float32), "mp")
    hidden_out = (residual.astype(jnp.float32) + lowered).astype(jnp.bfloat16)
    return (appended, hidden_out)


def solution(mesh):
    return jax.shard_map(
        body,
        mesh=mesh,
        in_specs=(
            P("dp", None),
            P(),
            P(None, None, "mp"),
            P("mp", None),
            P(),
            P(None, None, "mp"),
            P("mp", None),
            P(None, "dp", None, "mp"),
            P(),
            P("dp"),
            P("dp"),
        ),
        out_specs=(P(None, "dp", "mp"), P("dp", None)),
        check_vma=False,
    )
```

profile of v0, /device:TPU:2, one launch (start us, length us, event | category | flops | bytes accessed | tf_op | source)
XLA Modules:
  0.0 589.8 jit_solution(4555764252407409945)
XLA Ops:
  11.2 24.7 %all-gather = bf16[512,1,128]{2,0,1:T(8,128)(2,1)S(1)} all-gather(bf16[16,1,128]{2,0,1:T(8,128)(2,1)S(1)} %copy.113), channel_id=2, replica_groups=mesh['dp'=32,'mp'=8] {'dp'}, dimensions={0}, use_global_device_ids=true | all-gather | bytes 135168 | tf_op jit(solution)/shard_map/all_gather | solution.py:66
  36.7 190.9 %while.35 = (s32[]{:T(128)}, f32[512,2]{0,1:T(2,128)S(1)}, f32[512,2]{0,1:T(2,128)S(1)}, f32[512,2,64]{0,2,1:T(8,128)S(1)}, s32[128]{0:T(128)S(1)}, /*index=5*/s...) while((s32[]{:T(128)}, f32[512,2]{0,1:T(2,128)S(1)}, ...), condition=%wide.region_6.7_spmd.clone.clone, body=%wide.region_2.6_spmd.clone.clone.sunk | while | flops 7361630 | bytes 5361311 | solution.py:129
  41.5 4.0 gather_fusion.2
  53.5 4.0 gather_fusion.2
  65.4 4.0 gather_fusion.2
  77.3 4.0 gather_fusion.2
  89.3 4.0 gather_fusion.2
  101.2 4.0 gather_fusion.2
  113.1 4.0 gather_fusion.2
  125.1 4.0 gather_fusion.2
  137.0 4.0 gather_fusion.2
  148.9 4.0 gather_fusion.2
  160.9 4.0 gather_fusion.2
  172.8 4.0 gather_fusion.2
  184.7 4.0 gather_fusion.2
  196.7 4.0 gather_fusion.2
  208.6 4.0 gather_fusion.2
  220.5 4.0 gather_fusion.2
  228.4 22.8 %all-gather.1 = f32[16384,2]{0,1:T(2,128)S(1)} all-gather(f32[512,2]{0,1:T(2,128)S(1)} %get-tuple-element.259), channel_id=3, replica_groups=mesh['dp'=32,'mp'=8] {'dp'}, dimensions={0}, use_global_device_ids=true | all-gather | bytes 135168 | tf_op jit(solution)/shard_map/all_gather | solution.py:15
  251.2 24.6 %all-gather.2 = f32[16384,2]{0,1:T(2,128)S(1)} all-gather(f32[512,2]{0,1:T(2,128)S(1)} %get-tuple-element.260), channel_id=4, replica_groups=mesh['dp'=32,'mp'=8] {'dp'}, dimensions={0}, use_global_device_ids=true | all-gather | bytes 135168 | tf_op jit(solution)/shard_map/all_gather | solution.py:15
  275.8 12.0 %all-gather.6.cloned.1.call-done = f32[16384,2,64]{0,2,1:T(8,128)} async-done(((f32[512,2,64]{0,2,1:T(8,128)}), f32[16384,2,64]{0,2,1:T(8,128)}) %all-gather.6.cloned.1.call-update) | async-done | bytes 8388624 | tf_op jit(solution)/shard_map/all_gather | solution.py:15
  289.0 7.1 %slice.95 = f32[15872,2,64]{0,2,1:T(8,128)} slice(f32[16384,2,64]{0,2,1:T(8,128)} %all-gather.6.cloned.1.call-done), slice={[512:16384], [0:2], [0:64]} | slice | bytes 16252928 | tf_op jit(solution)/shard_map/slice | solution.py:17
  296.1 19.6 %copy.125 = f32[15872,2,64]{2,1,0:T(2,128)} copy(f32[15872,2,64]{0,2,1:T(8,128)} %slice.95) | data formatting | bytes 16252928 | tf_op jit(solution)/shard_map/while | solution.py:18
  315.7 119.1 %while.34 = (s32[]{:T(128)}, f32[512,2]{0,1:T(2,128)S(1)}, f32[512,2]{0,1:T(2,128)S(1)}, f32[512,2,64]{2,1,0:T(2,128)S(1)}, f32[31,512,2]{1,2,0:T(2,128)S(1)}, /...) while((s32[]{:T(128)}, f32[512,2]{0,1:T(2,128)S(1)}, f32[512,2]{0,1:T(2,128)S(1)}, ...), condition=%wide.region_8.9_spmd, body=%wide.region_7.8_spmd.sunk | while | flops 202754 | bytes 843877 | solution.py:18
  316.0 3.5 fusion.67
  319.8 3.5 fusion.67
  323.7 3.5 fusion.67
  327.5 3.5 fusion.67
  331.4 3.5 fusion.67
  335.2 3.5 fusion.67
  339.1 3.5 fusion.67
  342.9 3.5 fusion.67
  346.8 3.5 fusion.67
  350.6 3.5 fusion.67
  354.4 3.5 fusion.67
  358.3 3.5 fusion.67
  362.1 3.5 fusion.67
  366.0 3.5 fusion.67
  369.8 3.5 fusion.67
  373.7 3.5 fusion.67
  377.5 3.5 fusion.67
  381.3 3.5 fusion.67
  385.2 3.5 fusion.67
  389.0 3.5 fusion.67
  392.9 3.5 fusion.67
  436.0 3.5 copy.128
  442.4 65.8 %all-reduce.3.cloned.1.call-done = f32[16,1024]{1,0:T(8,128)} async-done(((f32[16,1024]{1,0:T(8,128)}), f32[16,1024]{1,0:T(8,128)}) %all-reduce.3.cloned.1.call-update) | async-done | bytes 65552 | tf_op jit(solution)/shard_map/psum | solution.py:138
  511.4 70.4 %all-reduce.5.cloned.1.call-done = f32[16,1024]{1,0:T(8,128)} async-done(((f32[16,1024]{1,0:T(8,128)}), f32[16,1024]{1,0:T(8,128)}) %all-reduce.5.cloned.1.call-update) | async-done | bytes 65552 | tf_op jit(solution)/shard_map/psum | solution.py:150
  (656 shorter events, 184.9 us)
Async XLA Ops:
  7.2 502.7 %copy-start = (bf16[512,1024]{1,0:T(8,128)(2,1)S(1)}, bf16[512,1024]{1,0:T(8,128)(2,1)}, u32[]{:S(2)}) copy-start(bf16[512,1024]{1,0:T(8,128)(2,1)} %param.21) | copy-start | bytes 3145732
  7.2 280.6 %all-gather.6.cloned.1.call-start = ((), (), s32[]{:S(2)}) async-start(), calls=%async_computation.2 | async-start | bytes 8650752 | tf_op jit(solution)/shard_map/all_gather | solution.py:15
  227.6 0.7 copy-start.1
  228.3 279.9 %all-reduce.3.cloned.1.call-start = ((), (), s32[]{:S(2)}) async-start(), calls=%async_computation | async-start | bytes 131072 | tf_op jit(solution)/shard_map/psum | solution.py:138
  315.6 119.5 %copy-start.3 = (bf16[128,1024]{1,0:T(8,128)(2,1)S(1)}, bf16[128,1024]{1,0:T(8,128)(2,1)}, u32[]{:S(2)}) copy-start(bf16[128,1024]{1,0:T(8,128)(2,1)} %param.18) | copy-start | bytes 786436
  315.7 192.6 %copy-start.2 = (bf16[16,1024]{1,0:T(8,128)(2,1)S(1)}, bf16[16,1024]{1,0:T(8,128)(2,1)}, u32[]{:S(2)}) copy-start(bf16[16,1024]{1,0:T(8,128)(2,1)} %param.15) | copy-start | bytes 98308
  315.7 193.5 %copy-start.4 = (f32[1024]{0:T(1024)S(1)}, f32[1024]{0:T(1024)}, u32[]{:S(2)}) copy-start(f32[1024]{0:T(1024)} %param.19) | copy-start | bytes 12292
  436.0 145.8 %all-reduce.5.cloned.1.call-start = ((), (), s32[]{:S(2)}) async-start(), calls=%async_computation.1 | async-start | bytes 131072 | tf_op jit(solution)/shard_map/psum | solution.py:150
Sparse Core Ops, SparseCore 0:
  228.4 59.3 all-gather.5
  436.1 72.0 all-reduce.2
  510.9 70.8 all-reduce.4
where the time goes:
time: 593 us; the launch traced here: 590 us
  local copies, waits for them, and re-layouts  206 us (35%)
  waiting for transfers between devices  148 us (25%)
  other arithmetic  126 us (21%)
  blocking collectives  72.1 us (12%)
  matrix products  20.3 us (3%)
  between operations  13.9 us (2%)
    add x31, other arithmetic, combine(): first[2] * shrink_first[:, :, None] + second[2] * shrink_second[:, :, None]  108 us
    psum x1, waiting for transfers between devices, body(): lax.psum(jnp.dot(activated, w_down, preferred_element_type=jnp.float32),...  70.4 us
    psum x1, waiting for transfers between devices, body(): lax.psum(jnp.dot(context, w_out, preferred_element_type=jnp.float32), 'mp')  65.8 us
    gather x16, local copies, waits for them, and re-layouts, visit(): fetched = jnp.take(kv_cache, picked, axis=1)  64.4 us
    all_gather x2, blocking collectives, merged_2(): pieces = jax.tree.map(lambda part: lax.all_gather(part, axis), value)  47.4 us
    all_gather x1, blocking collectives, body(): every_query = lax.all_gather(projected[:, 0], 'dp', axis=0, tiled=True)  24.7 us
    gather x16, local copies, waits for them, and re-layouts, visit(): usable = (owners[:, None] >= 0) & (position < lengths[clamped][:, None])  21.2 us
    gather x16, local copies, waits for them, and re-layouts, visit(): owners = page_request[picked]  20.8 us
  transfers between devices with their start and end apart: 3, of which 3 were waited for; matrix products, arithmetic and copies ran while one was open for 1% of the time, Pallas kernels for 0%

commit v1 on v0

v1 whole, which is shorter than its diff:
```python
import jax
import jax.numpy as jnp
from jax import lax
from jax.sharding import PartitionSpec as P

HEAD_DIM = 64


EPSILON = 1e-05
NEGATIVE = -1e30


def rms_norm(values, gain):
    widened = values.astype(jnp.float32)
    mean_square = jnp.mean(widened * widened, axis=-1, keepdims=True)
    return (widened * lax.rsqrt(mean_square + EPSILON) * gain).astype(jnp.bfloat16)


def body(
    hidden,
    attn_gain,
    w_qkv,
    w_out,
    mlp_gain,
    w_gate_up,
    w_down,
    kv_cache,
    lengths,
    page_request,
    page_index,
):
    local_rows = hidden.shape[0]
    head_cols = w_qkv.shape[2]
    local_heads = head_cols // HEAD_DIM
    pool_pages = kv_cache.shape[1]
    page_len = kv_cache.shape[2]
    data_devices = lax.axis_size("dp")
    requests = local_rows * data_devices
    score_scale = HEAD_DIM ** (-0.5)
    normed = rms_norm(hidden, attn_gain)
    projected = jnp.dot(
        normed, w_qkv.reshape(w_qkv.shape[0], 3 * head_cols), preferred_element_type=jnp.float32
    )
    projected = lax.optimization_barrier(projected.astype(jnp.bfloat16)).reshape(
        local_rows, 3, head_cols
    )
    appended = jnp.stack([projected[:, 1], projected[:, 2]])
    every_query = lax.all_gather(projected[:, 0], "dp", axis=0, tiled=True)
    own_queries = projected[:, 0].reshape(local_rows, local_heads, HEAD_DIM).astype(jnp.float32)
    own_keys = projected[:, 1].reshape(local_rows, local_heads, HEAD_DIM).astype(jnp.float32)
    own_values = projected[:, 2].reshape(local_rows, local_heads, HEAD_DIM).astype(jnp.float32)
    self_scores = jnp.sum(own_queries * own_keys, axis=-1) * score_scale
    home_row = lax.axis_index("dp") * local_rows
    request_ids = jnp.arange(requests, dtype=jnp.int32)
    offsets = jnp.arange(page_len, dtype=jnp.int32)

    owners = page_request
    clamped = jnp.maximum(owners, 0)
    chosen_queries = every_query[clamped].reshape(pool_pages, local_heads, HEAD_DIM)
    key_rows = kv_cache[0].reshape(pool_pages, page_len, local_heads, HEAD_DIM)
    value_rows = kv_cache[1].reshape(pool_pages, page_len, local_heads, HEAD_DIM)
    scores = (
        jnp.einsum("phd,pthd->pht", chosen_queries, key_rows, preferred_element_type=jnp.float32)
        * score_scale
    )
    position = page_index[:, None] * page_len + offsets[None, :]
    usable = (owners[:, None] >= 0) & (position < lengths[clamped][:, None])
    page_max = jnp.max(jnp.where(usable[:, None, :], scores, NEGATIVE), axis=2)
    raw = jnp.where(usable[:, None, :], jnp.exp(scores - page_max[:, :, None]), 0.0)
    page_total = jnp.sum(raw, axis=2)
    page_sum = jnp.einsum(
        "pht,pthd->phd", raw.astype(jnp.bfloat16), value_rows, preferred_element_type=jnp.float32
    )

    member = owners[:, None] == request_ids[None, :]
    seg_max = jnp.max(jnp.where(member[:, :, None], page_max[:, None, :], NEGATIVE), axis=0)
    self_full = lax.dynamic_update_slice(
        jnp.full((requests, local_heads), NEGATIVE, jnp.float32), self_scores, (home_row, 0)
    )
    local_max = jnp.maximum(seg_max, self_full)
    factors = jnp.where(owners[:, None] >= 0, jnp.exp(page_max - local_max[clamped]), 0.0)
    payload = jnp.concatenate(
        [(page_sum * factors[:, :, None]).reshape(pool_pages, head_cols), page_total * factors],
        axis=1,
    )
    onehot = member.astype(jnp.float32)
    local_sums = jnp.einsum("pr,pc->rc", onehot, payload, precision=lax.Precision.HIGHEST)
    home_max = lax.dynamic_slice_in_dim(local_max, home_row, local_rows, 0)
    self_weight = jnp.exp(self_scores - home_max)
    self_payload = jnp.concatenate(
        [(self_weight[:, :, None] * own_values).reshape(local_rows, head_cols), self_weight],
        axis=1,
    )
    local_sums = local_sums + lax.dynamic_update_slice(
        jnp.zeros_like(local_sums), self_payload, (home_row, 0)
    )

    global_max = lax.pmax(local_max, "dp")
    shrink = jnp.exp(local_max - global_max)
    shrink_cols = jnp.concatenate([jnp.repeat(shrink, HEAD_DIM, axis=1), shrink], axis=1)
    mine = lax.psum_scatter(local_sums * shrink_cols, "dp", scatter_dimension=0, tiled=True)
    own_weighted = mine[:, :head_cols].reshape(local_rows, local_heads, HEAD_DIM)
    own_totals = mine[:, head_cols:]
    context = (
        (own_weighted / own_totals[:, :, None]).reshape(local_rows, head_cols).astype(jnp.bfloat16)
    )
    attended = lax.psum(jnp.dot(context, w_out, preferred_element_type=jnp.float32), "mp")
    residual = lax.optimization_barrier(
        (hidden.astype(jnp.float32) + attended).astype(jnp.bfloat16)
    )
    normed_mlp = rms_norm(residual, mlp_gain)
    hidden_cols = w_gate_up.shape[2]
    gate_up = jnp.dot(
        normed_mlp,
        w_gate_up.reshape(w_gate_up.shape[0], 2 * hidden_cols),
        preferred_element_type=jnp.float32,
    ).reshape(local_rows, 2, hidden_cols)
    activated = (jax.nn.silu(gate_up[:, 0]) * gate_up[:, 1]).astype(jnp.bfloat16)
    lowered = lax.psum(jnp.dot(activated, w_down, preferred_element_type=jnp.float32), "mp")
    hidden_out = (residual.astype(jnp.float32) + lowered).astype(jnp.bfloat16)
    return (appended, hidden_out)


def solution(mesh):
    return jax.shard_map(
        body,
        mesh=mesh,
        in_specs=(
            P("dp", None),
            P(),
            P(None, None, "mp"),
            P("mp", None),
            P(),
            P(None, None, "mp"),
            P("mp", None),
            P(None, "dp", None, "mp"),
            P(),
            P("dp"),
            P("dp"),
        ),
        out_specs=(P(None, "dp", "mp"), P("dp", None)),
        check_vma=False,
    )
```

time: 593 us -> 379 us (0.64)
  local copies, waits for them, and re-layouts: 206 us -> 32.9 us
  other arithmetic: 126 us -> 7.77 us
  waiting for transfers between devices: 148 us -> 230 us
  blocking collectives: 72.1 us -> 80.4 us
  matrix products: 20.3 us -> 12.7 us
    gather x96 -> x5, local copies, waits for them, and re-layouts: 145 us -> 2.79 us  [the longest x1 1.26 us: body(): usable = (owners[:, None] >= 0) & (position < lengths[clamped][:, None])]
    add x62 -> x0, other arithmetic: 109 us -> none  [the longest x31 108 us: combine(): first[2] * shrink_first[:, :, None] + second[2] * shrink_second[:, :, None]]
    unnamed x3 -> x4, waiting for transfers between devices: 0.05 us -> 92.7 us
    pmax x0 -> x1, blocking collectives: none -> 55.7 us  [body(): global_max = lax.pmax(local_max, 'dp')]
    all_gather x2 -> x0, blocking collectives: 47.4 us -> none  [merged_2(): pieces = jax.tree.map(lambda part: lax.all_gather(part, axis), value)]
    while x2 -> x0, local copies, waits for them, and re-layouts: 19.8 us -> none  [merged_2(): lax.scan(lambda running, piece: (join(running, piece), None), head, tail)]
    unnamed x13 -> x22, local copies, waits for them, and re-layouts: 5.65 us -> 18.4 us
    all_gather x1 -> x0, waiting for transfers between devices: 12 us -> none  [merged_2(): pieces = jax.tree.map(lambda part: lax.all_gather(part, axis), value)]
where the time goes in v1:
time: 379 us; the launch traced here: 378 us
  waiting for transfers between devices  230 us (61%)
  blocking collectives  80.4 us (21%)
  local copies, waits for them, and re-layouts  32.9 us (9%)
  between operations  14 us (4%)
  matrix products  12.7 us (3%)
  other arithmetic  7.77 us (2%)
    unnamed x4, waiting for transfers between devices  92.7 us
    psum x1, waiting for transfers between devices, body(): lax.psum(jnp.dot(activated, w_down, preferred_element_type=jnp.float32),...  70.4 us
    psum x1, waiting for transfers between devices, body(): lax.psum(jnp.dot(context, w_out, preferred_element_type=jnp.float32), 'mp')  67.3 us
    pmax x1, blocking collectives, body(): global_max = lax.pmax(local_max, 'dp')  55.7 us
    all_gather x1, blocking collectives, body(): every_query = lax.all_gather(projected[:, 0], 'dp', axis=0, tiled=True)  24.7 us
    unnamed x22, local copies, waits for them, and re-layouts  18.4 us
  transfers between devices with their start and end apart: 3, of which 3 were waited for; matrix products, arithmetic and copies ran while one was open for 1% of the time, Pallas kernels for 0%

profile of v1, /device:TPU:2, one launch (start us, length us, event | category | flops | bytes accessed | tf_op | source)
XLA Modules:
  0.0 378.3 jit_solution(6640743451332159533)
XLA Ops:
  7.2 0.7 broadcast_maximum_fusion
  8.0 0.7 broadcast_compare_fusion
  8.6 0.8 iota_compare_fusion
  9.4 1.4 copy.92
  10.8 0.9 fusion.9
  11.7 1.1 convolution_convert_fusion
  12.9 24.7 %all-gather = bf16[512,1,128]{2,0,1:T(8,128)(2,1)S(1)} all-gather(bf16[16,1,128]{2,0,1:T(8,128)(2,1)S(1)} %copy.95), channel_id=2, replica_groups=mesh['dp'=32,'mp'=8] {'dp'}, dimensions={0}, use_global_device_ids=true | all-gather | bytes 135168 | tf_op jit(solution)/shard_map/all_gather | solution.py:48
  37.6 0.7 gather_fusion.1
  38.3 0.1 copy.96
  38.4 0.1 copy.103
  38.6 6.0 %fusion.35 = (bf16[1,128,128,128]{3,2,1,0:T(8,128)(2,1)}, bf16[1,128,128,128]{3,2,1,0:T(8,128)(2,1)}) fusion(bf16[2,128,128,128]{3,2,1,0:T(8,128)(2,1)} %param.18), kind=kLoop, calls=%fused_computation.69 | loop fusion | bytes 16777216 | tf_op jit(solution)/shard_map/slice | solution.py:61
  44.6 6.4 %copy.111 = bf16[1,128,128,128]{2,3,1,0:T(8,128)(2,1)} copy(bf16[1,128,128,128]{3,2,1,0:T(8,128)(2,1)} %get-tuple-element.9) | data formatting | bytes 8388608
  51.0 1.3 gather_fusion
  52.3 3.4 fusion.37
  55.7 0.1 fusion.18
  55.8 0.1 select_reduce_fusion.1
  55.9 0.2 fusion.8
  56.1 0.1 select_reduce_fusion
  56.3 0.1 reduce_sum.37
  56.5 0.1 dynamic_update_slice.6
  56.7 0.1 copy.100
  56.9 55.7 %pmax.7 = f32[512,2]{0,1:T(2,128)S(1)} all-reduce(f32[512,2]{0,1:T(2,128)S(1)} %max.9), channel_id=1, replica_groups=mesh['dp'=32,'mp'=8] {'dp'}, use_global_device_ids=true, to_apply=%region_5.6 | all-reduce | flops 1024 | bytes 8192 | tf_op jit(solution)/shard_map/pmax | solution.py:98
  112.6 0.6 gather_fusion.2
  113.3 6.4 %copy.112 = bf16[1,128,128,128]{2,3,1,0:T(8,128)(2,1)} copy(bf16[1,128,128,128]{3,2,1,0:T(8,128)(2,1)} %get-tuple-element.8) | data formatting | bytes 8388608
  119.7 4.6 %fusion = f32[128,2,1,64]{3,2,1,0:T(1,128)S(1)} fusion(bf16[128,128,2,64]{1,3,2,0:T(8,128)(2,1)} %bitcast.70, bf16[128,2,128,1]{2,0,1,3:T(8,128)(2,1)S(1)} %get-tuple-element.10), kind=kOutput, calls=%fused_computation.8 | convolution fusion | flops 4194304 | bytes 4325376 | tf_op jit(solution)/shard_map/pht,pthd->phd/dot_general | solution.py:71
  124.3 0.1 copy.106
  124.4 0.1 copy.110
  124.5 0.4 fusion.4
  124.9 0.1 maximum_add_fusion
  125.0 0.7 add.66
  125.8 0.8 maximum_multiply_fusion
  126.5 1.9 copy.107
  128.6 92.6 %reduce-scatter.4.cloned.1.call-done = f32[16,130]{1,0:T(8,128)} async-done(((f32[512,130]{1,0:T(8,128)}), f32[16,130]{1,0:T(8,128)}) %reduce-scatter.4.cloned.1.call-update) | async-done | bytes 8336
  221.2 0.7 slice.48
  221.9 0.1 copy.113
  222.0 0.7 slice.49
  222.7 0.1 copy.114
  222.8 1.8 fusion.38
  224.7 1.9 copy.116
  226.6 2.9 copy.102
  229.5 67.3 %all-reduce.3.cloned.1.call-done = f32[16,1024]{1,0:T(8,128)} async-done(((f32[16,1024]{1,0:T(8,128)}), f32[16,1024]{1,0:T(8,128)}) %all-reduce.3.cloned.1.call-update) | async-done | bytes 65552 | tf_op jit(solution)/shard_map/psum | solution.py:107
  296.8 0.8 fusion.12
  297.6 0.1 fusion.13
  297.8 0.6 fusion.20
  298.4 0.9 fusion.29
  299.3 0.6 pad_maximum_fusion
  299.9 70.4 %all-reduce.5.cloned.1.call-done = f32[16,1024]{1,0:T(8,128)} async-done(((f32[16,1024]{1,0:T(8,128)}), f32[16,1024]{1,0:T(8,128)}) %all-reduce.5.cloned.1.call-update) | async-done | bytes 65552 | tf_op jit(solution)/shard_map/psum | solution.py:119
  370.3 1.5 fusion.16
  (42 shorter events, 0.7 us)
Async XLA Ops:
  7.2 291.2 %copy-start = (bf16[512,1024]{1,0:T(8,128)(2,1)S(1)}, bf16[512,1024]{1,0:T(8,128)(2,1)}, u32[]{:S(2)}) copy-start(bf16[512,1024]{1,0:T(8,128)(2,1)} %param.17) | copy-start | bytes 3145732
  7.2 214.0 %reduce-scatter.4.cloned.1.call-start = ((), (), s32[]{:S(2)}) async-start(), calls=%async_computation.3 | async-start | bytes 540672
  44.6 6.4 %copy-start.1 = (s32[512]{0:T(512)S(1)}, s32[512]{0:T(512)}, u32[]{:S(2)}) copy-start(s32[512]{0:T(512)} %param.19) | copy-start | bytes 6148
  44.6 7.7 %copy-start.6 = (s32[128]{0:T(128)S(1)}, s32[128]{0:T(128)}, u32[]{:S(2)}) copy-start(s32[128]{0:T(128)} %param.21) | copy-start | bytes 1540
  119.7 4.9 %copy-start.5 = (s32[128]{0:T(128)S(1)}, s32[128]{0:T(128)}, u32[]{:S(2)}) copy-start(s32[128]{0:T(128)} %param.20) | copy-start | bytes 1540
  119.7 104.9 %copy-start.2 = (bf16[1024,2,512]{2,1,0:T(2,128)(2,1)S(1)}, bf16[1024,2,512]{2,1,0:T(2,128)(2,1)}, u32[]{:S(2)}) copy-start(bf16[1024,2,512]{2,1,0:T(2,128)(2,1)} %param.16) | copy-start | bytes 6291460
  128.5 168.3 %all-reduce.3.cloned.1.call-start = ((), (), s32[]{:S(2)}) async-start(), calls=%async_computation.1 | async-start | bytes 131072 | tf_op jit(solution)/shard_map/psum | solution.py:107
  224.6 145.8 %all-reduce.5.cloned.1.call-start = ((), (), s32[]{:S(2)}) async-start(), calls=%async_computation.2 | async-start | bytes 131072 | tf_op jit(solution)/shard_map/psum | solution.py:119
  224.6 72.1 %copy-start.3 = (bf16[16,1024]{1,0:T(8,128)(2,1)S(1)}, bf16[16,1024]{1,0:T(8,128)(2,1)}, u32[]{:S(2)}) copy-start(bf16[16,1024]{1,0:T(8,128)(2,1)} %param.11) | copy-start | bytes 98308
  224.6 73.1 %copy-start.4 = (f32[1024]{0:T(1024)S(1)}, f32[1024]{0:T(1024)}, u32[]{:S(2)}) copy-start(f32[1024]{0:T(1024)} %param.15) | copy-start | bytes 12292
Sparse Core Ops, SparseCore 0:
  128.6 92.5 reduce-scatter.3
  224.7 72.0 all-reduce.2
  299.4 70.8 all-reduce.4

commit v2 on v1

--- a/solution.py
+++ b/solution.py
@@ -14,6 +14,35 @@
     widened = values.astype(jnp.float32)
     mean_square = jnp.mean(widened * widened, axis=-1, keepdims=True)
     return (widened * lax.rsqrt(mean_square + EPSILON) * gain).astype(jnp.bfloat16)
+
+
+def butterfly_sum(value, axis):
+    size = lax.axis_size(axis)
+    if size & (size - 1):
+        return lax.psum(value, axis)
+    distance = 1
+    while distance < size:
+        pairs = [(j, j ^ distance) for j in range(size)]
+        value = value + lax.ppermute(value, axis, pairs)
+        distance *= 2
+    return value
+
+
+def butterfly_gather(value, axis):
+    size = lax.axis_size(axis)
+    if size & (size - 1):
+        return lax.all_gather(value, axis, axis=0, tiled=True)
+    me = lax.axis_index(axis)
+    distance = 1
+    while distance < size:
+        pairs = [(j, j ^ distance) for j in range(size)]
+        other = lax.ppermute(value, axis, pairs)
+        low = (me & distance) == 0
+        value = jnp.where(
+            low, jnp.concatenate([value, other], 0), jnp.concatenate([other, value], 0)
+        )
+        distance *= 2
+    return value
 
 
 def body(
@@ -45,7 +74,7 @@
         local_rows, 3, head_cols
     )
     appended = jnp.stack([projected[:, 1], projected[:, 2]])
-    every_query = lax.all_gather(projected[:, 0], "dp", axis=0, tiled=True)
+    every_query = butterfly_gather(projected[:, 0], "dp")
     own_queries = projected[:, 0].reshape(local_rows, local_heads, HEAD_DIM).astype(jnp.float32)
     own_keys = projected[:, 1].reshape(local_rows, local_heads, HEAD_DIM).astype(jnp.float32)
     own_values = projected[:, 2].reshape(local_rows, local_heads, HEAD_DIM).astype(jnp.float32)
@@ -95,16 +124,20 @@
         jnp.zeros_like(local_sums), self_payload, (home_row, 0)
     )
 
-    global_max = lax.pmax(local_max, "dp")
-    shrink = jnp.exp(local_max - global_max)
-    shrink_cols = jnp.concatenate([jnp.repeat(shrink, HEAD_DIM, axis=1), shrink], axis=1)
-    mine = lax.psum_scatter(local_sums * shrink_cols, "dp", scatter_dimension=0, tiled=True)
+    packed = jnp.concatenate([local_sums, local_max], axis=1)
+    packed = packed.reshape(data_devices, local_rows, packed.shape[1])
+    received = lax.all_to_all(packed, "dp", 0, 0, tiled=True)
+    source_max = received[:, :, head_cols + local_heads :]
+    global_max = jnp.max(source_max, axis=0)
+    shrink = jnp.exp(source_max - global_max[None])
+    shrink_cols = jnp.concatenate([jnp.repeat(shrink, HEAD_DIM, axis=2), shrink], axis=2)
+    mine = jnp.sum(received[:, :, : head_cols + local_heads] * shrink_cols, axis=0)
     own_weighted = mine[:, :head_cols].reshape(local_rows, local_heads, HEAD_DIM)
     own_totals = mine[:, head_cols:]
     context = (
         (own_weighted / own_totals[:, :, None]).reshape(local_rows, head_cols).astype(jnp.bfloat16)
     )
-    attended = lax.psum(jnp.dot(context, w_out, preferred_element_type=jnp.float32), "mp")
+    attended = butterfly_sum(jnp.dot(context, w_out, preferred_element_type=jnp.float32), "mp")
     residual = lax.optimization_barrier(
         (hidden.astype(jnp.float32) + attended).astype(jnp.bfloat16)
     )
@@ -116,7 +149,7 @@
         preferred_element_type=jnp.float32,
     ).reshape(local_rows, 2, hidden_cols)
     activated = (jax.nn.silu(gate_up[:, 0]) * gate_up[:, 1]).astype(jnp.bfloat16)
-    lowered = lax.psum(jnp.dot(activated, w_down, preferred_element_type=jnp.float32), "mp")
+    lowered = butterfly_sum(jnp.dot(activated, w_down, preferred_element_type=jnp.float32), "mp")
     hidden_out = (residual.astype(jnp.float32) + lowered).astype(jnp.bfloat16)
     return (appended, hidden_out)
 

time: 379 us -> 116 us (0.31)
  waiting for transfers between devices: 230 us -> 26.4 us
  blocking collectives: 80.4 us -> 16.2 us
  starting transfers between devices: 0.12 us -> 23.7 us
  between operations: 14 us -> 1.02 us
    psum x2 -> x0, waiting for transfers between devices: 138 us -> none  [the longest x1 70.4 us: body(): lax.psum(jnp.dot(activated, w_down, preferred_element_type=jnp.float32),...]
    unnamed x4 -> x0, waiting for transfers between devices: 92.7 us -> none
    pmax x1 -> x0, blocking collectives: 55.7 us -> none  [body(): global_max = lax.pmax(local_max, 'dp')]
    ppermute x0 -> x11, waiting for transfers between devices: none -> 26.4 us  [the longest x6 22.1 us: butterfly_sum(): value = value + lax.ppermute(value, axis, pairs)]
    all_gather x1 -> x0, blocking collectives: 24.7 us -> none  [body(): every_query = lax.all_gather(projected[:, 0], 'dp', axis=0, tiled=True)]
    ppermute x0 -> x11, starting transfers between devices: none -> 23.7 us  [the longest x6 14.3 us: butterfly_sum(): value = value + lax.ppermute(value, axis, pairs)]
    all_to_all x0 -> x1, blocking collectives: none -> 16.2 us  [body(): received = lax.all_to_all(packed, 'dp', 0, 0, tiled=True)]
    unnamed x22 -> x20, local copies, waits for them, and re-layouts: 18.4 us -> 17.9 us
  transfers between devices with their start and end apart: 3 -> 11, of which waited for: 3 -> 8; matrix products, arithmetic and copies ran while one was open for 1% -> 26% of each run, Pallas kernels for 0% -> 0%
where the time goes in v2:
time: 116 us
  local copies, waits for them, and re-layouts  32.4 us (28%)
  waiting for transfers between devices  26.4 us (23%)
  starting transfers between devices  23.7 us (20%)
  blocking collectives  16.2 us (14%)
  matrix products  10.3 us (9%)
  other arithmetic  5.76 us (5%)
    ppermute x6, waiting for transfers between devices, butterfly_sum(): value = value + lax.ppermute(value, axis, pairs)  22.1 us
    unnamed x20, local copies, waits for them, and re-layouts  17.9 us
    all_to_all x1, blocking collectives, body(): received = lax.all_to_all(packed, 'dp', 0, 0, tiled=True)  16.2 us
    ppermute x6, starting transfers between devices, butterfly_sum(): value = value + lax.ppermute(value, axis, pairs)  14.3 us
    ppermute x5, starting transfers between devices, butterfly_gather(): other = lax.ppermute(value, axis, pairs)  9.35 us
    slice x1, local copies, waits for them, and re-layouts, body(): kv_cache[1].reshape(pool_pages, page_len, local_heads, HEAD_DIM)  6.1 us
    dot_general x1, matrix products, body(): jnp.einsum('pht,pthd->phd', raw.astype(jnp.bfloat16), value_rows, preferr...  4.45 us
    ppermute x5, waiting for transfers between devices, butterfly_gather(): other = lax.ppermute(value, axis, pairs)  4.31 us
  transfers between devices with their start and end apart: 11, of which 8 were waited for; matrix products, arithmetic and copies ran while one was open for 26% of the time, Pallas kernels for 0%

profile of v2, /device:TPU:2, one launch (start us, length us, event | category | flops | bytes accessed | tf_op | source)
XLA Modules:
  0.0 115.7 jit_solution(4455585108568526785)
XLA Ops:
  0.6 1.5 %copy.93 = bf16[1024,3,128]{0,2,1:T(8,128)(2,1)S(1)} copy(bf16[1024,3,128]{2,0,1:T(8,128)(2,1)} %param.13) | data formatting | bytes 1572864 | tf_op args[2]
  2.1 0.9 fusion.10
  3.0 1.1 convolution_convert_fusion
  4.3 0.7 broadcast_maximum_fusion
  4.9 0.7 broadcast_compare_fusion
  5.6 0.8 iota_compare_fusion
  6.4 6.1 %fusion.38 = (bf16[1,128,128,128]{3,2,1,0:T(8,128)(2,1)}, bf16[1,128,128,128]{3,2,1,0:T(8,128)(2,1)}) fusion(bf16[2,128,128,128]{3,2,1,0:T(8,128)(2,1)} %param.18), kind=kLoop, calls=%fused_computation.79 | loop fusion | bytes 16777216 | tf_op jit(solution)/shard_map/slice | solution.py:90
  12.5 1.7 %collective-permute-start.1 = (bf16[32,128]{1,0:T(8,128)(2,1)S(1)}, bf16[32,128]{1,0:T(8,128)(2,1)S(1)}, u32[]{:S(2)}, u32[]{:S(2)}) collective-permute-start(bf16[32,128]{1,0:T(8,128)(2,1)S(1)} %maximum_select_fusion.4), channel_id=1, source_target_pairs={{0,16},{8,24},{16,0},{24,8},{32,48},{40,56},{48,32},{56,40},{64,80... | collective-permute-start | bytes 24584 | tf_op jit(solution)/shard_map/ppermute | solution.py:39
  14.2 1.3 %gather_fusion = s32[128]{0:T(128)S(1)} fusion(s32[512]{0:T(512)S(1)} %copy-done.1, s32[1024]{0:T(1024)S(1)} %pad_clamp_fusion), kind=kCustom, calls=%fused_computation | custom fusion | bytes 1536 | tf_op jit(solution)/shard_map/gather | solution.py:96
  15.5 0.8 collective-permute-done.1
  16.3 3.3 %collective-permute-start.2 = (bf16[64,128]{1,0:T(8,128)(2,1)S(1)}, bf16[64,128]{1,0:T(8,128)(2,1)S(1)}, u32[]{:S(2)}, u32[]{:S(2)}) collective-permute-start(bf16[64,128]{1,0:T(8,128)(2,1)S(1)} %maximum_select_fusion.3), channel_id=1, source_target_pairs={{0,32},{8,40},{16,48},{24,56},{32,0},{40,8},{48,16},{56,24},{64,96... | collective-permute-start | bytes 49160 | tf_op jit(solution)/shard_map/ppermute | solution.py:39
  19.7 1.9 %collective-permute-done.2 = bf16[64,128]{1,0:T(8,128)(2,1)S(1)} collective-permute-done((bf16[64,128]{1,0:T(8,128)(2,1)S(1)}, bf16[64,128]{1,0:T(8,128)(2,1)S(1)}, u32[]{:S(2)}, u32[]{:S(2)}) %collective-permute-start.2) | collective-permute-done | bytes 16416 | tf_op jit(solution)/shard_map/ppermute | solution.py:39
  21.6 2.3 %collective-permute-start.3 = (bf16[128,128]{1,0:T(8,128)(2,1)S(1)}, bf16[128,128]{1,0:T(8,128)(2,1)S(1)}, u32[]{:S(2)}, u32[]{:S(2)}) collective-permute-start(bf16[128,128]{1,0:T(8,128)(2,1)S(1)} %maximum_select_fusion.2), channel_id=1, source_target_pairs={{0,64},{8,72},{16,80},{24,88},{32,96},{40,104},{48,112},{56,120},{... | collective-permute-start | bytes 98312 | tf_op jit(solution)/shard_map/ppermute | solution.py:39
  24.2 1.6 %collective-permute-done.3 = bf16[128,128]{1,0:T(8,128)(2,1)S(1)} collective-permute-done((bf16[128,128]{1,0:T(8,128)(2,1)S(1)}, bf16[128,128]{1,0:T(8,128)(2,1)S(1)}, u32[]{:S(2)}, u32[]{:S(2)}) %collective-permute-start.3) | collective-permute-done | bytes 32800 | tf_op jit(solution)/shard_map/ppermute | solution.py:39
  25.9 2.0 %collective-permute-start.4 = (bf16[256,128]{1,0:T(8,128)(2,1)S(1)}, bf16[256,128]{1,0:T(8,128)(2,1)S(1)}, u32[]{:S(2)}, u32[]{:S(2)}) collective-permute-start(bf16[256,128]{1,0:T(8,128)(2,1)S(1)} %maximum_select_fusion.1), channel_id=1, source_target_pairs={{0,128},{8,136},{16,144},{24,152},{32,160},{40,168},{48,176},{56,1... | collective-permute-start | bytes 196616 | tf_op jit(solution)/shard_map/ppermute | solution.py:39
  27.8 6.4 %copy.111 = bf16[1,128,128,128]{2,3,1,0:T(8,128)(2,1)} copy(bf16[1,128,128,128]{3,2,1,0:T(8,128)(2,1)} %get-tuple-element.9) | data formatting | bytes 8388608
  34.2 6.3 %copy.112 = bf16[1,128,128,128]{2,3,1,0:T(8,128)(2,1)} copy(bf16[1,128,128,128]{3,2,1,0:T(8,128)(2,1)} %get-tuple-element.8) | data formatting | bytes 8388608
  40.7 0.2 dynamic_update_slice.6
  40.9 0.7 gather_fusion.1
  41.9 3.4 %fusion.40 = f32[128,2,1,128]{3,2,1,0:T(1,128)S(1)} fusion(bf16[128,2,64,1]{2,3,1,0:T(2,128)(2,1)S(1)} %copy.104, bf16[128,128,2,64]{1,3,2,0:T(8,128)(2,1)} %bitcast.66), kind=kOutput, calls=%fused_computation.81 | convolution fusion | flops 4194304 | bytes 4358144 | tf_op jit(solution)/shard_map/phd,pthd->pht/dot_general | solution.py:92
  45.4 0.2 fusion.9
  45.7 0.1 copy.100
  46.0 0.6 gather_fusion.2
  46.7 4.5 %fusion.1 = f32[128,2,1,64]{3,2,1,0:T(1,128)S(1)} fusion(bf16[128,128,2,64]{1,3,2,0:T(8,128)(2,1)} %bitcast.65, bf16[128,2,128,1]{2,0,1,3:T(8,128)(2,1)S(1)} %get-tuple-element.10), kind=kOutput, calls=%fused_computation.13 | convolution fusion | flops 4194304 | bytes 4325376 | tf_op jit(solution)/shard_map/pht,pthd->phd/dot_general | solution.py:100
  51.3 0.4 fusion.5
  51.8 0.7 add.78
  52.5 0.2 copy.102
  52.7 16.2 %all_to_all.5 = f32[32,16,132]{2,1,0:T(8,128)S(1)} all-to-all(f32[32,16,132]{2,1,0:T(8,128)S(1)} %bitcast.69), channel_id=1, replica_groups=mesh['dp'=32,'mp'=8] {'dp'}, dimensions={0} | all-to-all | bytes 540672 | tf_op jit(solution)/shard_map/all_to_all | solution.py:129
  69.1 0.1 subtract_exponential_fusion
  69.2 0.6 broadcast_in_dim.92
  69.8 0.3 reshape.149
  70.4 0.2 fusion.33
  70.6 1.9 %collective-permute-start.5 = (f32[16,1024]{1,0:T(8,128)S(1)}, f32[16,1024]{1,0:T(8,128)S(1)}, u32[]{:S(2)}, u32[]{:S(2)}) collective-permute-start(f32[16,1024]{1,0:T(8,128)S(1)} %fusion.33), channel_id=1, source_target_pairs={{0,1},{1,0},{2,3},{3,2},{4,5},{5,4},{6,7},{7,6},{8,9},{9,8},{10,11... | collective-permute-start | bytes 196616 | tf_op jit(solution)/shard_map/ppermute | solution.py:26
  72.5 3.0 %collective-permute-done.5 = f32[16,1024]{1,0:T(8,128)S(1)} collective-permute-done((f32[16,1024]{1,0:T(8,128)S(1)}, f32[16,1024]{1,0:T(8,128)S(1)}, u32[]{:S(2)}, u32[]{:S(2)}) %collective-permute-start.5) | collective-permute-done | bytes 65568 | tf_op jit(solution)/shard_map/ppermute | solution.py:26
  75.5 3.4 %collective-permute-start.6 = (f32[16,1024]{1,0:T(8,128)S(1)}, f32[16,1024]{1,0:T(8,128)S(1)}, u32[]{:S(2)}, u32[]{:S(2)}) collective-permute-start(f32[16,1024]{1,0:T(8,128)S(1)} %add.79), channel_id=1, source_target_pairs={{0,2},{1,3},{2,0},{3,1},{4,6},{5,7},{6,4},{7,5},{8,10},{9,11},{10,... | collective-permute-start | bytes 196616 | tf_op jit(solution)/shard_map/ppermute | solution.py:26
  78.8 3.7 %collective-permute-done.6 = f32[16,1024]{1,0:T(8,128)S(1)} collective-permute-done((f32[16,1024]{1,0:T(8,128)S(1)}, f32[16,1024]{1,0:T(8,128)S(1)}, u32[]{:S(2)}, u32[]{:S(2)}) %collective-permute-start.6) | collective-permute-done | bytes 65568 | tf_op jit(solution)/shard_map/ppermute | solution.py:26
  82.6 6.5 %collective-permute-start.7 = (f32[16,1024]{1,0:T(8,128)S(1)}, f32[16,1024]{1,0:T(8,128)S(1)}, u32[]{:S(2)}, u32[]{:S(2)}) collective-permute-start(f32[16,1024]{1,0:T(8,128)S(1)} %add.80), channel_id=1, source_target_pairs={{0,4},{1,5},{2,6},{3,7},{4,0},{5,1},{6,2},{7,3},{8,12},{9,13},{10,... | collective-permute-start | bytes 196616 | tf_op jit(solution)/shard_map/ppermute | solution.py:26
  89.0 3.5 %copy.114 = bf16[128,8,2,512]{3,1,2,0:T(8,128)(2,1)} copy(bf16[128,8,2,512]{3,2,1,0:T(2,128)(2,1)} %bitcast.68) | data formatting | bytes 4194304
  92.6 2.9 %copy.103 = bf16[1024,1024]{1,0:T(8,128)(2,1)S(1)} copy(bf16[1024,1024]{0,1:T(8,128)(2,1)} %bitcast.64) | data formatting | bytes 4194304 | tf_op jit(solution)/shard_map/dot_general | solution.py:146
  95.6 0.6 fusion.20
  96.3 0.3 fusion.29
  96.5 4.3 %collective-permute-done.8 = f32[16,1024]{1,0:T(8,128)S(1)} collective-permute-done((f32[16,1024]{1,0:T(8,128)S(1)}, f32[16,1024]{1,0:T(8,128)S(1)}, u32[]{:S(2)}, u32[]{:S(2)}) %collective-permute-start.8) | collective-permute-done | bytes 65568 | tf_op jit(solution)/shard_map/ppermute | solution.py:26
  100.8 0.6 collective-permute-start.9
  101.4 4.9 %collective-permute-done.9 = f32[16,1024]{1,0:T(8,128)S(1)} collective-permute-done((f32[16,1024]{1,0:T(8,128)S(1)}, f32[16,1024]{1,0:T(8,128)S(1)}, u32[]{:S(2)}, u32[]{:S(2)}) %collective-permute-start.9) | collective-permute-done | bytes 65568 | tf_op jit(solution)/shard_map/ppermute | solution.py:26
  106.3 2.0 %collective-permute-start.10 = (f32[16,1024]{1,0:T(8,128)S(1)}, f32[16,1024]{1,0:T(8,128)S(1)}, u32[]{:S(2)}, u32[]{:S(2)}) collective-permute-start(f32[16,1024]{1,0:T(8,128)S(1)} %add.86), channel_id=1, source_target_pairs={{0,4},{1,5},{2,6},{3,7},{4,0},{5,1},{6,2},{7,3},{8,12},{9,13},{10,... | collective-permute-start | bytes 196616 | tf_op jit(solution)/shard_map/ppermute | solution.py:26
  108.3 0.6 pad_maximum_fusion.1
  108.9 6.2 %collective-permute-done.10 = f32[16,1024]{1,0:T(8,128)S(1)} collective-permute-done((f32[16,1024]{1,0:T(8,128)S(1)}, f32[16,1024]{1,0:T(8,128)S(1)}, u32[]{:S(2)}, u32[]{:S(2)}) %collective-permute-start.10) | collective-permute-done | bytes 65568 | tf_op jit(solution)/shard_map/ppermute | solution.py:26
  115.1 0.6 fusion.17
  (64 shorter events, 2.3 us)
Async XLA Ops:
  0.6 95.6 %copy-start = (bf16[512,1024]{1,0:T(8,128)(2,1)S(1)}, bf16[512,1024]{1,0:T(8,128)(2,1)}, u32[]{:S(2)}) copy-start(bf16[512,1024]{1,0:T(8,128)(2,1)} %param.17) | copy-start | bytes 3145732
  4.2 8.3 %collective-permute-start = (bf16[16,128]{1,0:T(8,128)(2,1)S(1)}, bf16[16,128]{1,0:T(8,128)(2,1)S(1)}, u32[]{:S(2)}, u32[]{:S(2)}) collective-permute-start(bf16[16,128]{1,0:T(8,128)(2,1)S(1)} %bitcast.72), channel_id=1, source_target_pairs={{0,8},{8,0},{16,24},{24,16},{32,40},{40,32},{48,56},{56,48},{64,72... | collective-permute-start | bytes 12296 | tf_op jit(solution)/shard_map/ppermute | solution.py:39
  6.4 6.1 %copy-start.6 = (s32[128]{0:T(128)S(1)}, s32[128]{0:T(128)}, u32[]{:S(2)}) copy-start(s32[128]{0:T(128)} %param.21) | copy-start | bytes 1540
  6.4 7.8 %copy-start.1 = (s32[512]{0:T(512)S(1)}, s32[512]{0:T(512)}, u32[]{:S(2)}) copy-start(s32[512]{0:T(512)} %param.19) | copy-start | bytes 6148
  12.5 3.7 %collective-permute-start.1 = (bf16[32,128]{1,0:T(8,128)(2,1)S(1)}, bf16[32,128]{1,0:T(8,128)(2,1)S(1)}, u32[]{:S(2)}, u32[]{:S(2)}) collective-permute-start(bf16[32,128]{1,0:T(8,128)(2,1)S(1)} %maximum_select_fusion.4), channel_id=1, source_target_pairs={{0,16},{8,24},{16,0},{24,8},{32,48},{40,56},{48,32},{56,40},{64,80... | collective-permute-start | bytes 24584 | tf_op jit(solution)/shard_map/ppermute | solution.py:39
  16.3 5.3 %collective-permute-start.2 = (bf16[64,128]{1,0:T(8,128)(2,1)S(1)}, bf16[64,128]{1,0:T(8,128)(2,1)S(1)}, u32[]{:S(2)}, u32[]{:S(2)}) collective-permute-start(bf16[64,128]{1,0:T(8,128)(2,1)S(1)} %maximum_select_fusion.3), channel_id=1, source_target_pairs={{0,32},{8,40},{16,48},{24,56},{32,0},{40,8},{48,16},{56,24},{64,96... | collective-permute-start | bytes 49160 | tf_op jit(solution)/shard_map/ppermute | solution.py:39
  21.6 4.2 %collective-permute-start.3 = (bf16[128,128]{1,0:T(8,128)(2,1)S(1)}, bf16[128,128]{1,0:T(8,128)(2,1)S(1)}, u32[]{:S(2)}, u32[]{:S(2)}) collective-permute-start(bf16[128,128]{1,0:T(8,128)(2,1)S(1)} %maximum_select_fusion.2), channel_id=1, source_target_pairs={{0,64},{8,72},{16,80},{24,88},{32,96},{40,104},{48,112},{56,120},{... | collective-permute-start | bytes 98312 | tf_op jit(solution)/shard_map/ppermute | solution.py:39
  25.9 15.0 %collective-permute-start.4 = (bf16[256,128]{1,0:T(8,128)(2,1)S(1)}, bf16[256,128]{1,0:T(8,128)(2,1)S(1)}, u32[]{:S(2)}, u32[]{:S(2)}) collective-permute-start(bf16[256,128]{1,0:T(8,128)(2,1)S(1)} %maximum_select_fusion.1), channel_id=1, source_target_pairs={{0,128},{8,136},{16,144},{24,152},{32,160},{40,168},{48,176},{56,1... | collective-permute-start | bytes 196616 | tf_op jit(solution)/shard_map/ppermute | solution.py:39
  45.3 6.0 %copy-start.5 = (s32[128]{0:T(128)S(1)}, s32[128]{0:T(128)}, u32[]{:S(2)}) copy-start(s32[128]{0:T(128)} %param.20) | copy-start | bytes 1540
  51.1 19.3 %copy-start.3 = (bf16[128,1024]{1,0:T(8,128)(2,1)S(1)}, bf16[128,1024]{1,0:T(8,128)(2,1)}, u32[]{:S(2)}) copy-start(bf16[128,1024]{1,0:T(8,128)(2,1)} %param.14) | copy-start | bytes 786436
  70.6 4.9 %collective-permute-start.5 = (f32[16,1024]{1,0:T(8,128)S(1)}, f32[16,1024]{1,0:T(8,128)S(1)}, u32[]{:S(2)}, u32[]{:S(2)}) collective-permute-start(f32[16,1024]{1,0:T(8,128)S(1)} %fusion.33), channel_id=1, source_target_pairs={{0,1},{1,0},{2,3},{3,2},{4,5},{5,4},{6,7},{7,6},{8,9},{9,8},{10,11... | collective-permute-start | bytes 196616 | tf_op jit(solution)/shard_map/ppermute | solution.py:26
  75.5 7.1 %collective-permute-start.6 = (f32[16,1024]{1,0:T(8,128)S(1)}, f32[16,1024]{1,0:T(8,128)S(1)}, u32[]{:S(2)}, u32[]{:S(2)}) collective-permute-start(f32[16,1024]{1,0:T(8,128)S(1)} %add.79), channel_id=1, source_target_pairs={{0,2},{1,3},{2,0},{3,1},{4,6},{5,7},{6,4},{7,5},{8,10},{9,11},{10,... | collective-permute-start | bytes 196616 | tf_op jit(solution)/shard_map/ppermute | solution.py:26
  82.6 12.9 %collective-permute-start.7 = (f32[16,1024]{1,0:T(8,128)S(1)}, f32[16,1024]{1,0:T(8,128)S(1)}, u32[]{:S(2)}, u32[]{:S(2)}) collective-permute-start(f32[16,1024]{1,0:T(8,128)S(1)} %add.80), channel_id=1, source_target_pairs={{0,4},{1,5},{2,6},{3,7},{4,0},{5,1},{6,2},{7,3},{8,12},{9,13},{10,... | collective-permute-start | bytes 196616 | tf_op jit(solution)/shard_map/ppermute | solution.py:26
  89.0 6.4 %copy-start.2 = (bf16[16,1024]{1,0:T(8,128)(2,1)S(1)}, bf16[16,1024]{1,0:T(8,128)(2,1)}, u32[]{:S(2)}) copy-start(bf16[16,1024]{1,0:T(8,128)(2,1)} %param.11) | copy-start | bytes 98308
  89.0 6.6 %copy-start.4 = (f32[1024]{0:T(1024)S(1)}, f32[1024]{0:T(1024)}, u32[]{:S(2)}) copy-start(f32[1024]{0:T(1024)} %param.15) | copy-start | bytes 12292
  96.5 4.3 %collective-permute-start.8 = (f32[16,1024]{1,0:T(8,128)S(1)}, f32[16,1024]{1,0:T(8,128)S(1)}, u32[]{:S(2)}, u32[]{:S(2)}) collective-permute-start(f32[16,1024]{1,0:T(8,128)S(1)} %fusion.29), channel_id=1, source_target_pairs={{0,1},{1,0},{2,3},{3,2},{4,5},{5,4},{6,7},{7,6},{8,9},{9,8},{10,11... | collective-permute-start | bytes 196616 | tf_op jit(solution)/shard_map/ppermute | solution.py:26
  100.8 5.5 %collective-permute-start.9 = (f32[16,1024]{1,0:T(8,128)S(1)}, f32[16,1024]{1,0:T(8,128)S(1)}, u32[]{:S(2)}, u32[]{:S(2)}) collective-permute-start(f32[16,1024]{1,0:T(8,128)S(1)} %add.85), channel_id=1, source_target_pairs={{0,2},{1,3},{2,0},{3,1},{4,6},{5,7},{6,4},{7,5},{8,10},{9,11},{10,... | collective-permute-start | bytes 196616 | tf_op jit(solution)/shard_map/ppermute | solution.py:26
  106.3 8.8 %collective-permute-start.10 = (f32[16,1024]{1,0:T(8,128)S(1)}, f32[16,1024]{1,0:T(8,128)S(1)}, u32[]{:S(2)}, u32[]{:S(2)}) collective-permute-start(f32[16,1024]{1,0:T(8,128)S(1)} %add.86), channel_id=1, source_target_pairs={{0,4},{1,5},{2,6},{3,7},{4,0},{5,1},{6,2},{7,3},{8,12},{9,13},{10,... | collective-permute-start | bytes 196616 | tf_op jit(solution)/shard_map/ppermute | solution.py:26

commit v3 on v2

--- a/solution.py
+++ b/solution.py
@@ -26,6 +26,13 @@
         value = value + lax.ppermute(value, axis, pairs)
         distance *= 2
     return value
+
+
+def exchange_gather(value, axis):
+    size = lax.axis_size(axis)
+    spread = jnp.broadcast_to(value[None], (size,) + value.shape)
+    gathered = lax.all_to_all(spread, axis, 0, 0, tiled=True)
+    return gathered.reshape((size * value.shape[0],) + value.shape[1:])
 
 
 def butterfly_gather(value, axis):
@@ -74,7 +81,7 @@
         local_rows, 3, head_cols
     )
     appended = jnp.stack([projected[:, 1], projected[:, 2]])
-    every_query = butterfly_gather(projected[:, 0], "dp")
+    every_query = exchange_gather(projected[:, 0], "dp")
     own_queries = projected[:, 0].reshape(local_rows, local_heads, HEAD_DIM).astype(jnp.float32)
     own_keys = projected[:, 1].reshape(local_rows, local_heads, HEAD_DIM).astype(jnp.float32)
     own_values = projected[:, 2].reshape(local_rows, local_heads, HEAD_DIM).astype(jnp.float32)
@@ -85,21 +92,25 @@
 
     owners = page_request
     clamped = jnp.maximum(owners, 0)
-    chosen_queries = every_query[clamped].reshape(pool_pages, local_heads, HEAD_DIM)
-    key_rows = kv_cache[0].reshape(pool_pages, page_len, local_heads, HEAD_DIM)
-    value_rows = kv_cache[1].reshape(pool_pages, page_len, local_heads, HEAD_DIM)
+    chosen_queries = every_query[clamped]
+    head_of_col = jnp.arange(head_cols, dtype=jnp.int32) // HEAD_DIM
+    head_mask = head_of_col[:, None] == jnp.arange(local_heads, dtype=jnp.int32)[None, :]
+    query_blocks = jnp.where(head_mask[None], chosen_queries[:, :, None], jnp.zeros((), jnp.bfloat16))
+    key_rows = kv_cache[0]
+    value_rows = kv_cache[1]
     scores = (
-        jnp.einsum("phd,pthd->pht", chosen_queries, key_rows, preferred_element_type=jnp.float32)
+        jnp.einsum("ptc,pch->pth", key_rows, query_blocks, preferred_element_type=jnp.float32)
         * score_scale
     )
     position = page_index[:, None] * page_len + offsets[None, :]
     usable = (owners[:, None] >= 0) & (position < lengths[clamped][:, None])
-    page_max = jnp.max(jnp.where(usable[:, None, :], scores, NEGATIVE), axis=2)
-    raw = jnp.where(usable[:, None, :], jnp.exp(scores - page_max[:, :, None]), 0.0)
-    page_total = jnp.sum(raw, axis=2)
-    page_sum = jnp.einsum(
-        "pht,pthd->phd", raw.astype(jnp.bfloat16), value_rows, preferred_element_type=jnp.float32
+    page_max = jnp.max(jnp.where(usable[:, :, None], scores, NEGATIVE), axis=1)
+    raw = jnp.where(usable[:, :, None], jnp.exp(scores - page_max[:, None, :]), 0.0)
+    page_total = jnp.sum(raw, axis=1)
+    head_sums = jnp.einsum(
+        "pth,ptc->phc", raw.astype(jnp.bfloat16), value_rows, preferred_element_type=jnp.float32
     )
+    page_sum = jnp.sum(jnp.where(head_mask.T[None], head_sums, 0.0), axis=1)
 
     member = owners[:, None] == request_ids[None, :]
     seg_max = jnp.max(jnp.where(member[:, :, None], page_max[:, None, :], NEGATIVE), axis=0)
@@ -109,7 +120,7 @@
     local_max = jnp.maximum(seg_max, self_full)
     factors = jnp.where(owners[:, None] >= 0, jnp.exp(page_max - local_max[clamped]), 0.0)
     payload = jnp.concatenate(
-        [(page_sum * factors[:, :, None]).reshape(pool_pages, head_cols), page_total * factors],
+        [page_sum * jnp.repeat(factors, HEAD_DIM, axis=1), page_total * factors],
         axis=1,
     )
     onehot = member.astype(jnp.float32)

time: 116 us -> 93.9 us (0.81)
  local copies, waits for them, and re-layouts: 32.4 us -> 14.4 us
  waiting for transfers between devices: 26.4 us -> 23 us
  starting transfers between devices: 23.7 us -> 22.2 us
    unnamed x20 -> x14, local copies, waits for them, and re-layouts: 17.9 us -> 5.16 us
    ppermute x5 -> x0, starting transfers between devices: 9.35 us -> none  [butterfly_gather(): other = lax.ppermute(value, axis, pairs)]
    all_to_all x0 -> x1, starting transfers between devices: none -> 7.62 us  [exchange_gather(): gathered = lax.all_to_all(spread, axis, 0, 0, tiled=True)]
    slice x2 -> x1, local copies, waits for them, and re-layouts: 6.12 us -> 0.02 us  [body(): every_query = exchange_gather(projected[:, 0], 'dp')]
    ppermute x5 -> x0, waiting for transfers between devices: 4.31 us -> none  [butterfly_gather(): other = lax.ppermute(value, axis, pairs)]
    all_to_all x0 -> x1, waiting for transfers between devices: none -> 1.44 us  [exchange_gather(): gathered = lax.all_to_all(spread, axis, 0, 0, tiled=True)]
  transfers between devices with their start and end apart: 11 -> 7, of which waited for: 8 -> 6; matrix products, arithmetic and copies ran while one was open for 26% -> 13% of each run, Pallas kernels for 0% -> 0%
where the time goes in v3:
time: 93.9 us; the launch traced here: 93.5 us
  waiting for transfers between devices  23 us (24%)
  starting transfers between devices  22.2 us (24%)
  blocking collectives  15.8 us (17%)
  local copies, waits for them, and re-layouts  14.4 us (15%)
  matrix products  10.5 us (11%)
  other arithmetic  6.53 us (7%)
  between operations  0.96 us (1%)
    ppermute x6, waiting for transfers between devices, butterfly_sum(): value = value + lax.ppermute(value, axis, pairs)  21.6 us
    all_to_all x1, blocking collectives, body(): received = lax.all_to_all(packed, 'dp', 0, 0, tiled=True)  15.8 us
    ppermute x6, starting transfers between devices, butterfly_sum(): value = value + lax.ppermute(value, axis, pairs)  14.6 us
    all_to_all x1, starting transfers between devices, exchange_gather(): gathered = lax.all_to_all(spread, axis, 0, 0, tiled=True)  7.62 us
    unnamed x14, local copies, waits for them, and re-layouts  5.16 us
    dot_general x1, matrix products, body(): jnp.einsum('ptc,pch->pth', key_rows, query_blocks, preferred_element_type...  4.54 us
    dot_general x1, matrix products, body(): jnp.einsum('pth,ptc->phc', raw.astype(jnp.bfloat16), value_rows, preferre...  3.48 us
    dot_general x1, local copies, waits for them, and re-layouts, body(): jnp.dot(normed_mlp, w_gate_up.reshape(w_gate_up.shape[0], 2 * hidden_cols...  2.85 us
  transfers between devices with their start and end apart: 7, of which 6 were waited for; matrix products, arithmetic and copies ran while one was open for 13% of the time, Pallas kernels for 0%

profile of v3, /device:TPU:2, one launch (start us, length us, event | category | flops | bytes accessed | tf_op | source)
XLA Modules:
  0.0 93.5 jit_solution(2976770342859289256)
XLA Ops:
  0.6 1.5 %copy.61 = bf16[1024,3,128]{0,2,1:T(8,128)(2,1)S(1)} copy(bf16[1024,3,128]{2,0,1:T(8,128)(2,1)} %param.13) | data formatting | bytes 1572864 | tf_op args[2]
  2.1 0.9 fusion.20
  3.0 1.1 %convolution_convert_fusion = bf16[16,384]{1,0:T(8,128)(2,1)S(1)} fusion(bf16[1024,384]{0,1:T(8,128)(2,1)S(1)} %bitcast.60, bf16[16,1024]{1,0:T(8,128)(2,1)} %param.11, f32[1024]{0:T(1024)} %param.12, f32[16]{0:T(128)S(1)} %add_rsqrt_fusion.1), kind=kOutput, calls=%fused_computation.12 | convolution fusion | flops 12654592 | bytes 835648 | tf_op jit(solution)/shard_map/dot_general | solution.py:77
  4.2 0.7 broadcast_in_dim.131
  4.8 7.6 %all-to-all-start = ((bf16[32,16,128]{2,1,0:T(8,128)(2,1)}), bf16[32,16,128]{2,1,0:T(8,128)(2,1)S(1)}, u32[]{:S(2)}, u32[]{:S(2)}) async-start(bf16[32,16,128]{2,1,0:T(8,128)(2,1)} %broadcast_in_dim.131), calls=%async_computation | async-start | bytes 262144 | tf_op jit(solution)/shard_map/all_to_all | solution.py:34
  12.5 0.7 broadcast_maximum_fusion
  13.1 0.7 broadcast_compare_fusion
  13.8 0.8 iota_compare_fusion
  14.6 0.7 broadcast_multiply_fusion.1
  15.5 0.1 copy.73
  15.7 1.6 %gather_fusion = s32[128]{0:T(128)S(1)} fusion(s32[512]{0:T(512)} %param.19, s32[1024]{0:T(1024)S(1)} %pad_clamp_fusion), kind=kCustom, calls=%fused_computation | custom fusion | bytes 1536 | tf_op jit(solution)/shard_map/gather | solution.py:106
  17.3 0.1 fusion.28
  17.5 0.2 dynamic_update_slice.6
  17.6 1.4 %all-to-all-done = bf16[32,16,128]{2,1,0:T(8,128)(2,1)S(1)} async-done(((bf16[32,16,128]{2,1,0:T(8,128)(2,1)}), bf16[32,16,128]{2,1,0:T(8,128)(2,1)S(1)}, u32[]{:S(2)}, u32[]{:S(2)}) %all-to-all-start) | async-done | bytes 131104 | tf_op jit(solution)/shard_map/all_to_all | solution.py:34
  19.1 0.7 gather_fusion.1
  19.8 4.5 %select_reduce_fusion.1 = (f32[128,2]{1,0:T(8,128)S(1)}, f32[128,2,128]{2,1,0:T(2,128)S(1)}) fusion(pred[128,128]{1,0:T(8,128)(4,1)S(1)} %fusion.28, bf16[2,128,128,128]{3,2,1,0:T(8,128)(2,1)} %param.18, pred[128,2]{0,1:T(4,128)(4,1)S(1)} %iota_compare_fusion.2, bf16[128,128]{1,0:T(8,128)(2,1)S(1)} %gather_fusion.1), kind=kOutput, calls=%fused_computation.27 | convolution fusion | flops 8519424 | bytes 4375808 | tf_op jit(solution)/shard_map/ptc,pch->pth/dot_general | solution.py:102
  24.4 0.2 select_reduce_fusion
  24.6 0.1 copy.66
  24.8 0.4 bitcast_reduce_fusion
  25.2 0.6 gather_fusion.2
  25.8 3.5 %fusion.12 = f32[128,128]{1,0:T(8,128)S(1)} fusion(bf16[2,128,128,128]{3,2,1,0:T(8,128)(2,1)} %param.18, pred[2,128]{1,0:T(4,128)(4,1)S(1)} %iota_compare_fusion.3, f32[128,2,128]{2,1,0:T(2,128)S(1)} %get-tuple-element.12, pred[128,128]{1,0:T(8,128)(4,1)S(1)} %fusion.28, f32[128,2]{1,0:T(8,128)S(1)} %get-tuple-element.11), kind=kOutput, calls=%fused_computation.11 | convolution fusion | flops 8536064 | bytes 4408576 | tf_op jit(solution)/shard_map/pth,ptc->phc/dot_general | solution.py:110
  29.5 0.1 copy.68
  29.6 0.4 fusion.16
  30.1 0.7 add.83
  30.9 0.2 copy.69
  31.1 15.8 %all_to_all.10 = f32[32,16,132]{2,1,0:T(8,128)S(1)} all-to-all(f32[32,16,132]{2,1,0:T(8,128)S(1)} %bitcast.62), channel_id=1, replica_groups=mesh['dp'=32,'mp'=8] {'dp'}, dimensions={0} | all-to-all | bytes 540672 | tf_op jit(solution)/shard_map/all_to_all | solution.py:140
  46.9 0.1 slice_reduce_fusion
  47.0 0.1 subtract_exponential_fusion
  47.2 0.6 broadcast_in_dim.143
  47.8 0.3 reshape.194
  48.4 0.2 fusion.45
  48.5 1.9 %collective-permute-start = (f32[16,1024]{1,0:T(8,128)S(1)}, f32[16,1024]{1,0:T(8,128)S(1)}, u32[]{:S(2)}, u32[]{:S(2)}) collective-permute-start(f32[16,1024]{1,0:T(8,128)S(1)} %fusion.45), channel_id=1, source_target_pairs={{0,1},{1,0},{2,3},{3,2},{4,5},{5,4},{6,7},{7,6},{8,9},{9,8},{10,11... | collective-permute-start | bytes 196616 | tf_op jit(solution)/shard_map/ppermute | solution.py:26
  50.4 3.0 %collective-permute-done = f32[16,1024]{1,0:T(8,128)S(1)} collective-permute-done((f32[16,1024]{1,0:T(8,128)S(1)}, f32[16,1024]{1,0:T(8,128)S(1)}, u32[]{:S(2)}, u32[]{:S(2)}) %collective-permute-start) | collective-permute-done | bytes 65568 | tf_op jit(solution)/shard_map/ppermute | solution.py:26
  53.4 3.4 %collective-permute-start.1 = (f32[16,1024]{1,0:T(8,128)S(1)}, f32[16,1024]{1,0:T(8,128)S(1)}, u32[]{:S(2)}, u32[]{:S(2)}) collective-permute-start(f32[16,1024]{1,0:T(8,128)S(1)} %add.84), channel_id=1, source_target_pairs={{0,2},{1,3},{2,0},{3,1},{4,6},{5,7},{6,4},{7,5},{8,10},{9,11},{10,... | collective-permute-start | bytes 196616 | tf_op jit(solution)/shard_map/ppermute | solution.py:26
  56.8 3.7 %collective-permute-done.1 = f32[16,1024]{1,0:T(8,128)S(1)} collective-permute-done((f32[16,1024]{1,0:T(8,128)S(1)}, f32[16,1024]{1,0:T(8,128)S(1)}, u32[]{:S(2)}, u32[]{:S(2)}) %collective-permute-start.1) | collective-permute-done | bytes 65568 | tf_op jit(solution)/shard_map/ppermute | solution.py:26
  60.5 6.3 %collective-permute-start.2 = (f32[16,1024]{1,0:T(8,128)S(1)}, f32[16,1024]{1,0:T(8,128)S(1)}, u32[]{:S(2)}, u32[]{:S(2)}) collective-permute-start(f32[16,1024]{1,0:T(8,128)S(1)} %add.85), channel_id=1, source_target_pairs={{0,4},{1,5},{2,6},{3,7},{4,0},{5,1},{6,2},{7,3},{8,12},{9,13},{10,... | collective-permute-start | bytes 196616 | tf_op jit(solution)/shard_map/ppermute | solution.py:26
  66.8 3.5 %copy.75 = bf16[128,8,2,512]{3,1,2,0:T(8,128)(2,1)} copy(bf16[128,8,2,512]{3,2,1,0:T(2,128)(2,1)} %bitcast.61) | data formatting | bytes 4194304
  70.3 2.9 %copy.70 = bf16[1024,1024]{1,0:T(8,128)(2,1)S(1)} copy(bf16[1024,1024]{0,1:T(8,128)(2,1)} %bitcast.59) | data formatting | bytes 4194304 | tf_op jit(solution)/shard_map/dot_general | solution.py:157
  73.2 0.1 fusion.24
  73.4 0.6 fusion.30
  74.0 0.3 fusion.41
  74.3 4.3 %collective-permute-done.3 = f32[16,1024]{1,0:T(8,128)S(1)} collective-permute-done((f32[16,1024]{1,0:T(8,128)S(1)}, f32[16,1024]{1,0:T(8,128)S(1)}, u32[]{:S(2)}, u32[]{:S(2)}) %collective-permute-start.3) | collective-permute-done | bytes 65568 | tf_op jit(solution)/shard_map/ppermute | solution.py:26
  78.6 0.6 collective-permute-start.4
  79.1 4.9 %collective-permute-done.4 = f32[16,1024]{1,0:T(8,128)S(1)} collective-permute-done((f32[16,1024]{1,0:T(8,128)S(1)}, f32[16,1024]{1,0:T(8,128)S(1)}, u32[]{:S(2)}, u32[]{:S(2)}) %collective-permute-start.4) | collective-permute-done | bytes 65568 | tf_op jit(solution)/shard_map/ppermute | solution.py:26
  84.1 2.5 %collective-permute-start.5 = (f32[16,1024]{1,0:T(8,128)S(1)}, f32[16,1024]{1,0:T(8,128)S(1)}, u32[]{:S(2)}, u32[]{:S(2)}) collective-permute-start(f32[16,1024]{1,0:T(8,128)S(1)} %add.91), channel_id=1, source_target_pairs={{0,4},{1,5},{2,6},{3,7},{4,0},{5,1},{6,2},{7,3},{8,12},{9,13},{10,... | collective-permute-start | bytes 196616 | tf_op jit(solution)/shard_map/ppermute | solution.py:26
  86.5 0.6 pad_maximum_fusion.1
  87.1 5.7 %collective-permute-done.5 = f32[16,1024]{1,0:T(8,128)S(1)} collective-permute-done((f32[16,1024]{1,0:T(8,128)S(1)}, f32[16,1024]{1,0:T(8,128)S(1)}, u32[]{:S(2)}, u32[]{:S(2)}) %collective-permute-start.5) | collective-permute-done | bytes 65568 | tf_op jit(solution)/shard_map/ppermute | solution.py:26
  92.8 0.6 fusion.27
  (47 shorter events, 1.2 us)
Async XLA Ops:
  0.6 73.4 %copy-start = (bf16[512,1024]{1,0:T(8,128)(2,1)S(1)}, bf16[512,1024]{1,0:T(8,128)(2,1)}, u32[]{:S(2)}) copy-start(bf16[512,1024]{1,0:T(8,128)(2,1)} %param.17) | copy-start | bytes 3145732
  4.8 14.2 %all-to-all-start = ((bf16[32,16,128]{2,1,0:T(8,128)(2,1)}), bf16[32,16,128]{2,1,0:T(8,128)(2,1)S(1)}, u32[]{:S(2)}, u32[]{:S(2)}) async-start(bf16[32,16,128]{2,1,0:T(8,128)(2,1)} %broadcast_in_dim.131), calls=%async_computation | async-start | bytes 262144 | tf_op jit(solution)/shard_map/all_to_all | solution.py:34
  24.3 5.3 %copy-start.4 = (s32[128]{0:T(128)S(1)}, s32[128]{0:T(128)}, u32[]{:S(2)}) copy-start(s32[128]{0:T(128)} %param.20) | copy-start | bytes 1540
  29.3 19.0 %copy-start.2 = (bf16[128,1024]{1,0:T(8,128)(2,1)S(1)}, bf16[128,1024]{1,0:T(8,128)(2,1)}, u32[]{:S(2)}) copy-start(bf16[128,1024]{1,0:T(8,128)(2,1)} %param.14) | copy-start | bytes 786436
  48.5 4.9 %collective-permute-start = (f32[16,1024]{1,0:T(8,128)S(1)}, f32[16,1024]{1,0:T(8,128)S(1)}, u32[]{:S(2)}, u32[]{:S(2)}) collective-permute-start(f32[16,1024]{1,0:T(8,128)S(1)} %fusion.45), channel_id=1, source_target_pairs={{0,1},{1,0},{2,3},{3,2},{4,5},{5,4},{6,7},{7,6},{8,9},{9,8},{10,11... | collective-permute-start | bytes 196616 | tf_op jit(solution)/shard_map/ppermute | solution.py:26
  53.4 7.1 %collective-permute-start.1 = (f32[16,1024]{1,0:T(8,128)S(1)}, f32[16,1024]{1,0:T(8,128)S(1)}, u32[]{:S(2)}, u32[]{:S(2)}) collective-permute-start(f32[16,1024]{1,0:T(8,128)S(1)} %add.84), channel_id=1, source_target_pairs={{0,2},{1,3},{2,0},{3,1},{4,6},{5,7},{6,4},{7,5},{8,10},{9,11},{10,... | collective-permute-start | bytes 196616 | tf_op jit(solution)/shard_map/ppermute | solution.py:26
  60.5 12.7 %collective-permute-start.2 = (f32[16,1024]{1,0:T(8,128)S(1)}, f32[16,1024]{1,0:T(8,128)S(1)}, u32[]{:S(2)}, u32[]{:S(2)}) collective-permute-start(f32[16,1024]{1,0:T(8,128)S(1)} %add.85), channel_id=1, source_target_pairs={{0,4},{1,5},{2,6},{3,7},{4,0},{5,1},{6,2},{7,3},{8,12},{9,13},{10,... | collective-permute-start | bytes 196616 | tf_op jit(solution)/shard_map/ppermute | solution.py:26
  66.8 6.4 %copy-start.1 = (bf16[16,1024]{1,0:T(8,128)(2,1)S(1)}, bf16[16,1024]{1,0:T(8,128)(2,1)}, u32[]{:S(2)}) copy-start(bf16[16,1024]{1,0:T(8,128)(2,1)} %param.11) | copy-start | bytes 98308
  66.8 6.6 %copy-start.3 = (f32[1024]{0:T(1024)S(1)}, f32[1024]{0:T(1024)}, u32[]{:S(2)}) copy-start(f32[1024]{0:T(1024)} %param.15) | copy-start | bytes 12292
  74.3 4.3 %collective-permute-start.3 = (f32[16,1024]{1,0:T(8,128)S(1)}, f32[16,1024]{1,0:T(8,128)S(1)}, u32[]{:S(2)}, u32[]{:S(2)}) collective-permute-start(f32[16,1024]{1,0:T(8,128)S(1)} %fusion.41), channel_id=1, source_target_pairs={{0,1},{1,0},{2,3},{3,2},{4,5},{5,4},{6,7},{7,6},{8,9},{9,8},{10,11... | collective-permute-start | bytes 196616 | tf_op jit(solution)/shard_map/ppermute | solution.py:26
  78.6 5.5 %collective-permute-start.4 = (f32[16,1024]{1,0:T(8,128)S(1)}, f32[16,1024]{1,0:T(8,128)S(1)}, u32[]{:S(2)}, u32[]{:S(2)}) collective-permute-start(f32[16,1024]{1,0:T(8,128)S(1)} %add.90), channel_id=1, source_target_pairs={{0,2},{1,3},{2,0},{3,1},{4,6},{5,7},{6,4},{7,5},{8,10},{9,11},{10,... | collective-permute-start | bytes 196616 | tf_op jit(solution)/shard_map/ppermute | solution.py:26
  84.1 8.7 %collective-permute-start.5 = (f32[16,1024]{1,0:T(8,128)S(1)}, f32[16,1024]{1,0:T(8,128)S(1)}, u32[]{:S(2)}, u32[]{:S(2)}) collective-permute-start(f32[16,1024]{1,0:T(8,128)S(1)} %add.91), channel_id=1, source_target_pairs={{0,4},{1,5},{2,6},{3,7},{4,0},{5,1},{6,2},{7,3},{8,12},{9,13},{10,... | collective-permute-start | bytes 196616 | tf_op jit(solution)/shard_map/ppermute | solution.py:26

commit v4 on v3

--- a/solution.py
+++ b/solution.py
@@ -82,6 +82,10 @@
     )
     appended = jnp.stack([projected[:, 1], projected[:, 2]])
     every_query = exchange_gather(projected[:, 0], "dp")
+    hidden_cols = w_gate_up.shape[2]
+    every_query, gate_up_weights = lax.optimization_barrier(
+        (every_query, w_gate_up.reshape(w_gate_up.shape[0], 2 * hidden_cols))
+    )
     own_queries = projected[:, 0].reshape(local_rows, local_heads, HEAD_DIM).astype(jnp.float32)
     own_keys = projected[:, 1].reshape(local_rows, local_heads, HEAD_DIM).astype(jnp.float32)
     own_values = projected[:, 2].reshape(local_rows, local_heads, HEAD_DIM).astype(jnp.float32)
@@ -153,10 +157,9 @@
         (hidden.astype(jnp.float32) + attended).astype(jnp.bfloat16)
     )
     normed_mlp = rms_norm(residual, mlp_gain)
-    hidden_cols = w_gate_up.shape[2]
     gate_up = jnp.dot(
         normed_mlp,
-        w_gate_up.reshape(w_gate_up.shape[0], 2 * hidden_cols),
+        gate_up_weights,
         preferred_element_type=jnp.float32,
     ).reshape(local_rows, 2, hidden_cols)
     activated = (jax.nn.silu(gate_up[:, 0]) * gate_up[:, 1]).astype(jnp.bfloat16)

time: 93.9 us -> 109 us (1.16)
  other arithmetic: 6.53 us -> 13.4 us
  starting transfers between devices: 22.2 us -> 29 us
  waiting for transfers between devices: 23 us -> 17.1 us
  matrix products: 10.5 us -> 13.2 us
  local copies, waits for them, and re-layouts: 14.4 us -> 16.6 us
  blocking collectives: 15.8 us -> 17.5 us
    ppermute x6, starting transfers between devices: 14.6 us -> 21.4 us  [butterfly_sum(): value = value + lax.ppermute(value, axis, pairs)]
    ppermute x6, waiting for transfers between devices: 21.6 us -> 17.1 us  [butterfly_sum(): value = value + lax.ppermute(value, axis, pairs)]
    dot_general x1 -> x0, local copies, waits for them, and re-layouts: 2.85 us -> none  [body(): jnp.dot(normed_mlp, w_gate_up.reshape(w_gate_up.shape[0], 2 * hidden_cols...]
    reshape x1, local copies, waits for them, and re-layouts: 0.3 us -> 2.06 us  [body(): jnp.repeat(shrink, HEAD_DIM, axis=2)]
    concatenate x1, local copies, waits for them, and re-layouts: 0.2 us -> 1.95 us  [body(): packed = jnp.concatenate([local_sums, local_max], axis=1)]
    all_to_all x1, blocking collectives: 15.8 us -> 17.5 us  [body(): received = lax.all_to_all(packed, 'dp', 0, 0, tiled=True)]
    reduce_sum x1, other arithmetic: 0.39 us -> 1.89 us  [body(): page_total = jnp.sum(raw, axis=1)]
    mul x1, other arithmetic: 0.09 us -> 1.58 us  [body(): page_total * factors]
  transfers between devices with their start and end apart: 7 -> 7, of which waited for: 6 -> 6; matrix products, arithmetic and copies ran while one was open for 13% -> 7% of each run, Pallas kernels for 0% -> 0%
where the time goes in v4:
time: 109 us; the launch traced here: 108 us
  starting transfers between devices  29 us (27%)
  blocking collectives  17.5 us (16%)
  waiting for transfers between devices  17.1 us (16%)
  local copies, waits for them, and re-layouts  16.6 us (15%)
  other arithmetic  13.4 us (12%)
  matrix products  13.2 us (12%)
    ppermute x6, starting transfers between devices, butterfly_sum(): value = value + lax.ppermute(value, axis, pairs)  21.4 us
    all_to_all x1, blocking collectives, body(): received = lax.all_to_all(packed, 'dp', 0, 0, tiled=True)  17.5 us
    ppermute x6, waiting for transfers between devices, butterfly_sum(): value = value + lax.ppermute(value, axis, pairs)  17.1 us
    all_to_all x1, starting transfers between devices, exchange_gather(): gathered = lax.all_to_all(spread, axis, 0, 0, tiled=True)  7.62 us
    dot_general x1, matrix products, body(): jnp.einsum('ptc,pch->pth', key_rows, query_blocks, preferred_element_type...  5.11 us
    unnamed x18, local copies, waits for them, and re-layouts  4.37 us
    dot_general x1, matrix products, body(): jnp.einsum('pth,ptc->phc', raw.astype(jnp.bfloat16), value_rows, preferre...  4.08 us
  transfers between devices with their start and end apart: 7, of which 6 were waited for; matrix products, arithmetic and copies ran while one was open for 7% of the time, Pallas kernels for 0%

profile of v4, /device:TPU:2, one launch (start us, length us, event | category | flops | bytes accessed | tf_op | source)
XLA Modules:
  0.0 107.7 jit_solution(2447295777524996914)
XLA Ops:
  0.7 1.0 fusion.20
  1.6 1.4 %copy.61 = bf16[1024,3,128]{0,2,1:T(8,128)(2,1)S(1)} copy(bf16[1024,3,128]{2,0,1:T(8,128)(2,1)} %param.13) | data formatting | bytes 1572864 | tf_op args[2]
  3.1 1.1 convolution_convert_fusion
  4.2 0.6 fusion.50
  4.8 0.7 broadcast_in_dim.131
  5.4 7.6 %all-to-all-start = ((bf16[32,16,128]{2,1,0:T(8,128)(2,1)}), bf16[32,16,128]{2,1,0:T(8,128)(2,1)S(1)}, u32[]{:S(2)}, u32[]{:S(2)}) async-start(bf16[32,16,128]{2,1,0:T(8,128)(2,1)} %broadcast_in_dim.131), calls=%async_computation | async-start | bytes 262144 | tf_op jit(solution)/shard_map/all_to_all | solution.py:34
  13.1 0.7 broadcast_compare_fusion
  13.7 0.7 and_select_fusion
  14.4 0.8 iota_compare_fusion
  15.2 0.7 broadcast_multiply_fusion.1
  16.3 2.2 %copy.77 = bf16[128,8,2,512]{3,1,2,0:T(8,128)(2,1)S(1)} copy(bf16[128,8,2,512]{3,2,1,0:T(2,128)(2,1)} %bitcast.52) | data formatting | bytes 4194304
  18.4 1.3 %gather_fusion = s32[128]{0:T(128)S(1)} fusion(s32[512]{0:T(512)S(1)} %copy-done.1, s32[1024]{0:T(1024)S(1)} %pad_clamp_fusion), kind=kCustom, calls=%fused_computation | custom fusion | bytes 1536 | tf_op jit(solution)/shard_map/gather | solution.py:110
  19.9 0.2 dynamic_update_slice.6
  20.0 0.6 iota_compare_fusion.3
  20.6 0.7 gather_fusion.1
  21.3 5.1 %select_reduce_fusion.1 = (f32[128,2]{1,0:T(8,128)S(1)}, f32[128,2,128]{2,1,0:T(2,128)}) fusion(pred[128,128]{1,0:T(8,128)(4,1)S(1)} %fusion.28, bf16[2,128,128,128]{3,2,1,0:T(8,128)(2,1)} %param.18, pred[128,2]{0,1:T(4,128)(4,1)S(1)} %iota_compare_fusion.2, bf16[128,128]{1,0:T(8,128)(2,1)S(1)} %gather_fusion.1), kind=kOutput, calls=%fused_computation.27 | convolution fusion | flops 8519424 | bytes 4375808 | tf_op jit(solution)/shard_map/ptc,pch->pth/dot_general | solution.py:106
  26.9 1.9 %bitcast_reduce_fusion = f32[128,2]{1,0:T(8,128)} fusion(f32[128,2,128]{2,1,0:T(2,128)} %get-tuple-element.18, f32[128,2]{1,0:T(8,128)S(1)} %get-tuple-element.17, pred[128,128]{1,0:T(8,128)(4,1)S(1)} %fusion.28), kind=kLoop, calls=%fused_computation.24 | loop fusion | flops 98048 | bytes 149504 | tf_op jit(solution)/shard_map/reduce_sum | solution.py:113
  28.8 4.1 %fusion.12 = f32[128,128]{1,0:T(8,128)} fusion(bf16[2,128,128,128]{3,2,1,0:T(8,128)(2,1)} %param.18, pred[2,128]{1,0:T(4,128)(4,1)} %iota_compare_fusion.3, f32[128,2,128]{2,1,0:T(2,128)} %get-tuple-element.18, pred[128,128]{1,0:T(8,128)(4,1)S(1)} %fusion.28, f32[128,2]{1,0:T(8,128)S(1)} %get-tuple-element.17), kind=kOutput, calls=%fused_computation.11 | convolution fusion | flops 8536064 | bytes 4408832 | tf_op jit(solution)/shard_map/pth,ptc->phc/dot_general | solution.py:114
  32.9 1.2 %gather_fusion.2 = f32[128,2]{1,0:T(8,128)} fusion(f32[512,2]{1,0:T(8,128)S(1)} %copy.66, s32[1024]{0:T(1024)S(1)} %pad_clamp_fusion), kind=kCustom, calls=%fused_computation.2 | custom fusion | bytes 2560 | tf_op jit(solution)/shard_map/gather | solution.py:125
  34.1 1.6 %fusion.48 = (f32[128,2]{1,0:T(8,128)}, f32[128,2]{1,0:T(8,128)S(1)}) fusion(f32[128,2]{1,0:T(8,128)} %bitcast_reduce_fusion, f32[128,2]{1,0:T(8,128)S(1)} %get-tuple-element.17, f32[128,2]{1,0:T(8,128)} %gather_fusion.2, pred[128]{0:T(512)(128)(4,1)} %copy-done.6), kind=kLoop, calls=%fused_computation.85 | loop fusion | flops 768 | bytes 5248 | tf_op jit(solution)/shard_map/mul | solution.py:127
  35.9 0.8 mul.112
  36.7 1.2 %fusion.16 = f32[512,130]{0,1:T(8,128)S(1)} fusion(f32[128,2]{1,0:T(8,128)} %get-tuple-element.10, f32[128,128]{1,0:T(8,128)S(1)} %mul.112, s32[128]{0:T(128)} %param.20), kind=kOutput, calls=%fused_computation.20 | convolution fusion | flops 102318336 | bytes 333312 | tf_op jit(solution)/shard_map/pr,pc->rc/dot_general | solution.py:131
  37.9 0.7 maximum_add_fusion
  38.7 1.3 %add.83 = f32[512,130]{0,1:T(8,128)S(1)} dynamic-update-slice(f32[512,130]{0,1:T(8,128)S(1)} %fusion.16, f32[16,130]{0,1:T(8,128)} %maximum_add_fusion, s32[]{:T(128)S(6)} %select_n.53, s32[]{:T(128)} %constant.17.clone.1) | dynamic-update-slice | bytes 16644 | tf_op jit(solution)/shard_map/add | solution.py:138
  40.0 0.7 pad_maximum_fusion
  40.7 1.9 %copy.69 = f32[512,132]{1,0:T(8,128)} copy(f32[512,132]{0,1:T(8,128)} %pad_maximum_fusion) | data formatting | bytes 540672 | tf_op jit(solution)/shard_map/concatenate | solution.py:142
  42.6 17.5 %all_to_all.10 = f32[32,16,132]{2,1,0:T(8,128)S(1)} all-to-all(f32[32,16,132]{2,1,0:T(8,128)} %bitcast.53), channel_id=1, replica_groups=mesh['dp'=32,'mp'=8] {'dp'}, dimensions={0} | all-to-all | bytes 540672 | tf_op jit(solution)/shard_map/all_to_all | solution.py:144
  60.3 0.6 copy-done.2
  61.1 1.4 %broadcast_in_dim.143 = f32[32,16,2,64]{3,2,1,0:T(2,128)} broadcast(f32[32,16,2]{2,1,0:T(8,128)S(1)} %subtract_exponential_fusion), dimensions={0,1,2} | broadcast | bytes 266240 | tf_op jit(solution)/shard_map/broadcast_in_dim | solution.py:148
  62.5 2.1 %reshape.196 = f32[32,16,128]{2,1,0:T(8,128)} reshape(f32[32,16,2,64]{3,2,1,0:T(2,128)} %broadcast_in_dim.143) | data formatting | bytes 524288 | tf_op jit(solution)/shard_map/reshape | solution.py:148
  64.5 1.2 %fusion.15 = f32[16,130]{1,0:T(8,128)S(1)} fusion(f32[32,16,132]{2,1,0:T(8,128)} %copy-done.2, f32[32,16,2]{2,1,0:T(8,128)S(1)} %subtract_exponential_fusion, f32[32,16,128]{2,1,0:T(8,128)} %reshape.196), kind=kLoop, calls=%fused_computation.14 | loop fusion | flops 197600 | bytes 540800 | tf_op jit(solution)/shard_map/reduce_sum | solution.py:149
  65.9 1.1 %fusion.43 = f32[16,1024]{1,0:T(8,128)S(1)} fusion(bf16[128,1024]{1,0:T(8,128)(2,1)} %param.14, f32[16,128]{1,0:T(8,128)S(1)} %div.35, f32[16,130]{1,0:T(8,128)S(1)} %fusion.15), kind=kOutput, calls=%fused_computation.64 | convolution fusion | flops 4198400 | bytes 344064 | tf_op jit(solution)/shard_map/dot_general | solution.py:155
  67.0 1.9 %collective-permute-start = (f32[16,1024]{1,0:T(8,128)S(1)}, f32[16,1024]{1,0:T(8,128)S(1)}, u32[]{:S(2)}, u32[]{:S(2)}) collective-permute-start(f32[16,1024]{1,0:T(8,128)S(1)} %fusion.43), channel_id=1, source_target_pairs={{0,1},{1,0},{2,3},{3,2},{4,5},{5,4},{6,7},{7,6},{8,9},{9,8},{10,11... | collective-permute-start | bytes 196616 | tf_op jit(solution)/shard_map/ppermute | solution.py:26
  68.9 3.0 %collective-permute-done = f32[16,1024]{1,0:T(8,128)S(1)} collective-permute-done((f32[16,1024]{1,0:T(8,128)S(1)}, f32[16,1024]{1,0:T(8,128)S(1)}, u32[]{:S(2)}, u32[]{:S(2)}) %collective-permute-start) | collective-permute-done | bytes 65568 | tf_op jit(solution)/shard_map/ppermute | solution.py:26
  71.9 3.4 %collective-permute-start.1 = (f32[16,1024]{1,0:T(8,128)S(1)}, f32[16,1024]{1,0:T(8,128)S(1)}, u32[]{:S(2)}, u32[]{:S(2)}) collective-permute-start(f32[16,1024]{1,0:T(8,128)S(1)} %add.84), channel_id=1, source_target_pairs={{0,2},{1,3},{2,0},{3,1},{4,6},{5,7},{6,4},{7,5},{8,10},{9,11},{10,... | collective-permute-start | bytes 196616 | tf_op jit(solution)/shard_map/ppermute | solution.py:26
  75.3 3.7 %collective-permute-done.1 = f32[16,1024]{1,0:T(8,128)S(1)} collective-permute-done((f32[16,1024]{1,0:T(8,128)S(1)}, f32[16,1024]{1,0:T(8,128)S(1)}, u32[]{:S(2)}, u32[]{:S(2)}) %collective-permute-start.1) | collective-permute-done | bytes 65568 | tf_op jit(solution)/shard_map/ppermute | solution.py:26
  79.0 6.3 %collective-permute-start.2 = (f32[16,1024]{1,0:T(8,128)S(1)}, f32[16,1024]{1,0:T(8,128)S(1)}, u32[]{:S(2)}, u32[]{:S(2)}) collective-permute-start(f32[16,1024]{1,0:T(8,128)S(1)} %add.85), channel_id=1, source_target_pairs={{0,4},{1,5},{2,6},{3,7},{4,0},{5,1},{6,2},{7,3},{8,12},{9,13},{10,... | collective-permute-start | bytes 196616 | tf_op jit(solution)/shard_map/ppermute | solution.py:26
  85.3 2.2 %collective-permute-done.2 = f32[16,1024]{1,0:T(8,128)S(1)} collective-permute-done((f32[16,1024]{1,0:T(8,128)S(1)}, f32[16,1024]{1,0:T(8,128)S(1)}, u32[]{:S(2)}, u32[]{:S(2)}) %collective-permute-start.2) | collective-permute-done | bytes 65568 | tf_op jit(solution)/shard_map/ppermute | solution.py:26
  87.7 0.4 fusion.29
  88.2 0.2 fusion.39
  88.5 0.5 collective-permute-start.3
  89.0 3.8 %collective-permute-done.3 = f32[16,1024]{1,0:T(8,128)S(1)} collective-permute-done((f32[16,1024]{1,0:T(8,128)S(1)}, f32[16,1024]{1,0:T(8,128)S(1)}, u32[]{:S(2)}, u32[]{:S(2)}) %collective-permute-start.3) | collective-permute-done | bytes 65568 | tf_op jit(solution)/shard_map/ppermute | solution.py:26
  92.8 2.6 %collective-permute-start.4 = (f32[16,1024]{1,0:T(8,128)S(1)}, f32[16,1024]{1,0:T(8,128)S(1)}, u32[]{:S(2)}, u32[]{:S(2)}) collective-permute-start(f32[16,1024]{1,0:T(8,128)S(1)} %add.90), channel_id=1, source_target_pairs={{0,2},{1,3},{2,0},{3,1},{4,6},{5,7},{6,4},{7,5},{8,10},{9,11},{10,... | collective-permute-start | bytes 196616 | tf_op jit(solution)/shard_map/ppermute | solution.py:26
  95.4 2.6 %collective-permute-done.4 = f32[16,1024]{1,0:T(8,128)S(1)} collective-permute-done((f32[16,1024]{1,0:T(8,128)S(1)}, f32[16,1024]{1,0:T(8,128)S(1)}, u32[]{:S(2)}, u32[]{:S(2)}) %collective-permute-start.4) | collective-permute-done | bytes 65568 | tf_op jit(solution)/shard_map/ppermute | solution.py:26
  98.0 6.7 %collective-permute-start.5 = (f32[16,1024]{1,0:T(8,128)S(1)}, f32[16,1024]{1,0:T(8,128)S(1)}, u32[]{:S(2)}, u32[]{:S(2)}) collective-permute-start(f32[16,1024]{1,0:T(8,128)S(1)} %add.91), channel_id=1, source_target_pairs={{0,4},{1,5},{2,6},{3,7},{4,0},{5,1},{6,2},{7,3},{8,12},{9,13},{10,... | collective-permute-start | bytes 196616 | tf_op jit(solution)/shard_map/ppermute | solution.py:26
  104.8 0.6 pad_maximum_fusion.1
  105.4 1.7 %collective-permute-done.5 = f32[16,1024]{1,0:T(8,128)S(1)} collective-permute-done((f32[16,1024]{1,0:T(8,128)S(1)}, f32[16,1024]{1,0:T(8,128)S(1)}, u32[]{:S(2)}, u32[]{:S(2)}) %collective-permute-start.5) | collective-permute-done | bytes 65568 | tf_op jit(solution)/shard_map/ppermute | solution.py:26
  107.1 0.6 fusion.27
  (51 shorter events, 2.0 us)
Async XLA Ops:
  0.6 87.6 %copy-start = (bf16[512,1024]{1,0:T(8,128)(2,1)S(1)}, bf16[512,1024]{1,0:T(8,128)(2,1)}, u32[]{:S(2)}) copy-start(bf16[512,1024]{1,0:T(8,128)(2,1)} %param.17) | copy-start | bytes 3145732
  0.6 17.8 %copy-start.1 = (s32[512]{0:T(512)S(1)}, s32[512]{0:T(512)}, u32[]{:S(2)}) copy-start(s32[512]{0:T(512)} %param.19) | copy-start | bytes 6148
  5.4 15.2 %all-to-all-start = ((bf16[32,16,128]{2,1,0:T(8,128)(2,1)}), bf16[32,16,128]{2,1,0:T(8,128)(2,1)S(1)}, u32[]{:S(2)}, u32[]{:S(2)}) async-start(bf16[32,16,128]{2,1,0:T(8,128)(2,1)} %broadcast_in_dim.131), calls=%async_computation | async-start | bytes 262144 | tf_op jit(solution)/shard_map/all_to_all | solution.py:34
  13.7 12.7 %copy-start.6 = (pred[128]{0:T(512)(128)(4,1)}, pred[128]{0:T(512)(128)(4,1)S(1)}, u32[]{:S(2)}) copy-start(pred[128]{0:T(512)(128)(4,1)S(1)} %broadcast_compare_fusion) | copy-start | bytes 388
  34.1 53.4 %copy-start.3 = (bf16[16,1024]{1,0:T(8,128)(2,1)S(1)}, bf16[16,1024]{1,0:T(8,128)(2,1)}, u32[]{:S(2)}) copy-start(bf16[16,1024]{1,0:T(8,128)(2,1)} %param.11) | copy-start | bytes 98308
  35.7 52.0 %copy-start.5 = (f32[1024]{0:T(1024)S(1)}, f32[1024]{0:T(1024)}, u32[]{:S(2)}) copy-start(f32[1024]{0:T(1024)} %param.15) | copy-start | bytes 12292
  60.1 0.8 copy-start.2
  60.1 35.3 %copy-start.4 = (bf16[16,1,128]{2,1,0:T(2,128)(2,1)S(1)}, bf16[16,1,128]{2,1,0:T(2,128)(2,1)}, u32[]{:S(2)}) copy-start(bf16[16,1,128]{2,1,0:T(2,128)(2,1)} %get-tuple-element.16) | copy-start | bytes 12292
  67.0 4.9 %collective-permute-start = (f32[16,1024]{1,0:T(8,128)S(1)}, f32[16,1024]{1,0:T(8,128)S(1)}, u32[]{:S(2)}, u32[]{:S(2)}) collective-permute-start(f32[16,1024]{1,0:T(8,128)S(1)} %fusion.43), channel_id=1, source_target_pairs={{0,1},{1,0},{2,3},{3,2},{4,5},{5,4},{6,7},{7,6},{8,9},{9,8},{10,11... | collective-permute-start | bytes 196616 | tf_op jit(solution)/shard_map/ppermute | solution.py:26
  71.9 7.1 %collective-permute-start.1 = (f32[16,1024]{1,0:T(8,128)S(1)}, f32[16,1024]{1,0:T(8,128)S(1)}, u32[]{:S(2)}, u32[]{:S(2)}) collective-permute-start(f32[16,1024]{1,0:T(8,128)S(1)} %add.84), channel_id=1, source_target_pairs={{0,2},{1,3},{2,0},{3,1},{4,6},{5,7},{6,4},{7,5},{8,10},{9,11},{10,... | collective-permute-start | bytes 196616 | tf_op jit(solution)/shard_map/ppermute | solution.py:26
  79.0 8.5 %collective-permute-start.2 = (f32[16,1024]{1,0:T(8,128)S(1)}, f32[16,1024]{1,0:T(8,128)S(1)}, u32[]{:S(2)}, u32[]{:S(2)}) collective-permute-start(f32[16,1024]{1,0:T(8,128)S(1)} %add.85), channel_id=1, source_target_pairs={{0,4},{1,5},{2,6},{3,7},{4,0},{5,1},{6,2},{7,3},{8,12},{9,13},{10,... | collective-permute-start | bytes 196616 | tf_op jit(solution)/shard_map/ppermute | solution.py:26
  88.5 4.3 %collective-permute-start.3 = (f32[16,1024]{1,0:T(8,128)S(1)}, f32[16,1024]{1,0:T(8,128)S(1)}, u32[]{:S(2)}, u32[]{:S(2)}) collective-permute-start(f32[16,1024]{1,0:T(8,128)S(1)} %fusion.39), channel_id=1, source_target_pairs={{0,1},{1,0},{2,3},{3,2},{4,5},{5,4},{6,7},{7,6},{8,9},{9,8},{10,11... | collective-permute-start | bytes 196616 | tf_op jit(solution)/shard_map/ppermute | solution.py:26
  92.8 5.3 %collective-permute-start.4 = (f32[16,1024]{1,0:T(8,128)S(1)}, f32[16,1024]{1,0:T(8,128)S(1)}, u32[]{:S(2)}, u32[]{:S(2)}) collective-permute-start(f32[16,1024]{1,0:T(8,128)S(1)} %add.90), channel_id=1, source_target_pairs={{0,2},{1,3},{2,0},{3,1},{4,6},{5,7},{6,4},{7,5},{8,10},{9,11},{10,... | collective-permute-start | bytes 196616 | tf_op jit(solution)/shard_map/ppermute | solution.py:26
  98.0 9.1 %collective-permute-start.5 = (f32[16,1024]{1,0:T(8,128)S(1)}, f32[16,1024]{1,0:T(8,128)S(1)}, u32[]{:S(2)}, u32[]{:S(2)}) collective-permute-start(f32[16,1024]{1,0:T(8,128)S(1)} %add.91), channel_id=1, source_target_pairs={{0,4},{1,5},{2,6},{3,7},{4,0},{5,1},{6,2},{7,3},{8,12},{9,13},{10,... | collective-permute-start | bytes 196616 | tf_op jit(solution)/shard_map/ppermute | solution.py:26

commit v5 on v3

--- a/solution.py
+++ b/solution.py
@@ -135,14 +135,36 @@
         jnp.zeros_like(local_sums), self_payload, (home_row, 0)
     )
 
-    packed = jnp.concatenate([local_sums, local_max], axis=1)
-    packed = packed.reshape(data_devices, local_rows, packed.shape[1])
+    lanes = 128
+    stats = jnp.concatenate([local_sums[:, head_cols:], local_max], axis=1)
+    stats = stats.reshape(data_devices, local_rows * 2 * local_heads)
+    stats_rows = -(-stats.shape[1] // lanes)
+    stats = jnp.pad(stats, ((0, 0), (0, stats_rows * lanes - stats.shape[1])))
+    weighted_rows = local_rows * head_cols // lanes
+    packed = jnp.concatenate(
+        [
+            local_sums[:, :head_cols].reshape(data_devices, weighted_rows, lanes),
+            stats.reshape(data_devices, stats_rows, lanes),
+        ],
+        axis=1,
+    )
     received = lax.all_to_all(packed, "dp", 0, 0, tiled=True)
-    source_max = received[:, :, head_cols + local_heads :]
+    source_weighted = received[:, :weighted_rows].reshape(data_devices, local_rows, head_cols)
+    source_stats = received[:, weighted_rows:].reshape(data_devices, stats_rows * lanes)
+    source_stats = source_stats[:, : local_rows * 2 * local_heads].reshape(
+        data_devices, local_rows, 2 * local_heads
+    )
+    source_totals = source_stats[:, :, :local_heads]
+    source_max = source_stats[:, :, local_heads:]
     global_max = jnp.max(source_max, axis=0)
     shrink = jnp.exp(source_max - global_max[None])
-    shrink_cols = jnp.concatenate([jnp.repeat(shrink, HEAD_DIM, axis=2), shrink], axis=2)
-    mine = jnp.sum(received[:, :, : head_cols + local_heads] * shrink_cols, axis=0)
+    mine = jnp.concatenate(
+        [
+            jnp.sum(source_weighted * jnp.repeat(shrink, HEAD_DIM, axis=2), axis=0),
+            jnp.sum(source_totals * shrink, axis=0),
+        ],
+        axis=1,
+    )
     own_weighted = mine[:, :head_cols].reshape(local_rows, local_heads, HEAD_DIM)
     own_totals = mine[:, head_cols:]
     context = (

time: 93.9 us -> 93.1 us (level)
  blocking collectives: 15.8 us -> 14.8 us
    all_to_all x1, blocking collectives: 15.8 us -> 14.8 us  [body(): received = lax.all_to_all(packed, 'dp', 0, 0, tiled=True)]
where the time goes in v5:
time: 93.1 us; the launch traced here: 92.2 us
  starting transfers between devices  22.3 us (24%)
  waiting for transfers between devices  22.2 us (24%)
  local copies, waits for them, and re-layouts  14.9 us (16%)
  blocking collectives  14.8 us (16%)
  matrix products  10.5 us (11%)
  other arithmetic  6.42 us (7%)
  between operations  1.01 us (1%)
    ppermute x6, waiting for transfers between devices, butterfly_sum(): value = value + lax.ppermute(value, axis, pairs)  20.7 us
    all_to_all x1, blocking collectives, body(): received = lax.all_to_all(packed, 'dp', 0, 0, tiled=True)  14.8 us
    ppermute x6, starting transfers between devices, butterfly_sum(): value = value + lax.ppermute(value, axis, pairs)  14.7 us
    all_to_all x1, starting transfers between devices, exchange_gather(): gathered = lax.all_to_all(spread, axis, 0, 0, tiled=True)  7.62 us
    unnamed x14, local copies, waits for them, and re-layouts  5.16 us
    dot_general x1, matrix products, body(): jnp.einsum('ptc,pch->pth', key_rows, query_blocks, preferred_element_type...  4.54 us
    dot_general x1, matrix products, body(): jnp.einsum('pth,ptc->phc', raw.astype(jnp.bfloat16), value_rows, preferre...  3.46 us
    dot_general x1, local copies, waits for them, and re-layouts, body(): jnp.dot(normed_mlp, w_gate_up.reshape(w_gate_up.shape[0], 2 * hidden_cols...  2.85 us
  transfers between devices with their start and end apart: 7, of which 6 were waited for; matrix products, arithmetic and copies ran while one was open for 13% of the time, Pallas kernels for 0%

profile of v5, /device:TPU:2, one launch (start us, length us, event | category | flops | bytes accessed | tf_op | source)
XLA Modules:
  0.0 92.2 jit_solution(11870529597435377581)
XLA Ops:
  0.6 1.5 %copy.93 = bf16[1024,3,128]{0,2,1:T(8,128)(2,1)S(1)} copy(bf16[1024,3,128]{2,0,1:T(8,128)(2,1)} %param.13) | data formatting | bytes 1572864 | tf_op args[2]
  2.1 0.9 fusion.20
  3.0 1.1 %convolution_convert_fusion = bf16[16,384]{1,0:T(8,128)(2,1)S(1)} fusion(bf16[1024,384]{0,1:T(8,128)(2,1)S(1)} %bitcast.66, bf16[16,1024]{1,0:T(8,128)(2,1)} %param.11, f32[1024]{0:T(1024)} %param.12, f32[16]{0:T(128)S(1)} %add_rsqrt_fusion.1), kind=kOutput, calls=%fused_computation.12 | convolution fusion | flops 12654592 | bytes 835648 | tf_op jit(solution)/shard_map/dot_general | solution.py:77
  4.2 0.7 broadcast_in_dim.131
  4.8 7.6 %all-to-all-start = ((bf16[32,16,128]{2,1,0:T(8,128)(2,1)}), bf16[32,16,128]{2,1,0:T(8,128)(2,1)S(1)}, u32[]{:S(2)}, u32[]{:S(2)}) async-start(bf16[32,16,128]{2,1,0:T(8,128)(2,1)} %broadcast_in_dim.131), calls=%async_computation | async-start | bytes 262144 | tf_op jit(solution)/shard_map/all_to_all | solution.py:34
  12.5 0.7 broadcast_maximum_fusion
  13.1 0.7 broadcast_compare_fusion
  13.8 0.8 iota_compare_fusion
  14.6 0.7 broadcast_multiply_fusion.1
  15.5 0.1 copy.109
  15.7 1.6 %gather_fusion = s32[128]{0:T(128)S(1)} fusion(s32[512]{0:T(512)} %param.19, s32[1024]{0:T(1024)S(1)} %pad_clamp_fusion), kind=kCustom, calls=%fused_computation | custom fusion | bytes 1536 | tf_op jit(solution)/shard_map/gather | solution.py:106
  17.3 0.1 fusion.28
  17.5 0.2 dynamic_update_slice.6
  17.6 1.4 %all-to-all-done = bf16[32,16,128]{2,1,0:T(8,128)(2,1)S(1)} async-done(((bf16[32,16,128]{2,1,0:T(8,128)(2,1)}), bf16[32,16,128]{2,1,0:T(8,128)(2,1)S(1)}, u32[]{:S(2)}, u32[]{:S(2)}) %all-to-all-start) | async-done | bytes 131104 | tf_op jit(solution)/shard_map/all_to_all | solution.py:34
  19.1 0.7 gather_fusion.1
  19.8 4.5 %select_reduce_fusion.1 = (f32[128,2]{1,0:T(8,128)S(1)}, f32[128,2,128]{2,1,0:T(2,128)S(1)}) fusion(pred[128,128]{1,0:T(8,128)(4,1)S(1)} %fusion.28, bf16[2,128,128,128]{3,2,1,0:T(8,128)(2,1)} %param.18, pred[128,2]{0,1:T(4,128)(4,1)S(1)} %iota_compare_fusion.2, bf16[128,128]{1,0:T(8,128)(2,1)S(1)} %gather_fusion.1), kind=kOutput, calls=%fused_computation.25 | convolution fusion | flops 8519424 | bytes 4375808 | tf_op jit(solution)/shard_map/ptc,pch->pth/dot_general | solution.py:102
  24.4 0.2 select_reduce_fusion
  24.6 0.1 copy.98
  24.8 0.4 bitcast_reduce_fusion
  25.2 0.6 gather_fusion.2
  25.8 3.5 %fusion.12 = f32[128,128]{1,0:T(8,128)S(1)} fusion(bf16[2,128,128,128]{3,2,1,0:T(8,128)(2,1)} %param.18, pred[2,128]{1,0:T(4,128)(4,1)S(1)} %iota_compare_fusion.3, f32[128,2,128]{2,1,0:T(2,128)S(1)} %get-tuple-element.16, pred[128,128]{1,0:T(8,128)(4,1)S(1)} %fusion.28, f32[128,2]{1,0:T(8,128)S(1)} %get-tuple-element.15), kind=kOutput, calls=%fused_computation.11 | convolution fusion | flops 8536064 | bytes 4408576 | tf_op jit(solution)/shard_map/pth,ptc->phc/dot_general | solution.py:110
  29.6 0.4 fusion.16
  30.1 0.7 add.85
  30.9 0.1 copy.102
  31.0 0.2 reshape.206
  31.4 14.8 %all_to_all.10 = f32[32,17,128]{2,1,0:T(8,128)S(1)} all-to-all(f32[32,17,128]{2,1,0:T(8,128)S(1)} %pad_maximum_fusion), channel_id=1, replica_groups=mesh['dp'=32,'mp'=8] {'dp'}, dimensions={0} | all-to-all | bytes 557056 | tf_op jit(solution)/shard_map/all_to_all | solution.py:151
  46.3 0.2 fusion.43
  46.5 0.2 copy.105
  46.7 0.6 broadcast_in_dim.143
  47.3 0.3 reshape.210
  47.8 0.2 fusion.46
  48.0 1.9 %collective-permute-start = (f32[16,1024]{1,0:T(8,128)S(1)}, f32[16,1024]{1,0:T(8,128)S(1)}, u32[]{:S(2)}, u32[]{:S(2)}) collective-permute-start(f32[16,1024]{1,0:T(8,128)S(1)} %fusion.46), channel_id=1, source_target_pairs={{0,1},{1,0},{2,3},{3,2},{4,5},{5,4},{6,7},{7,6},{8,9},{9,8},{10,11... | collective-permute-start | bytes 196616 | tf_op jit(solution)/shard_map/ppermute | solution.py:26
  49.9 2.7 %collective-permute-done = f32[16,1024]{1,0:T(8,128)S(1)} collective-permute-done((f32[16,1024]{1,0:T(8,128)S(1)}, f32[16,1024]{1,0:T(8,128)S(1)}, u32[]{:S(2)}, u32[]{:S(2)}) %collective-permute-start) | collective-permute-done | bytes 65568 | tf_op jit(solution)/shard_map/ppermute | solution.py:26
  52.6 3.4 %collective-permute-start.1 = (f32[16,1024]{1,0:T(8,128)S(1)}, f32[16,1024]{1,0:T(8,128)S(1)}, u32[]{:S(2)}, u32[]{:S(2)}) collective-permute-start(f32[16,1024]{1,0:T(8,128)S(1)} %add.86), channel_id=1, source_target_pairs={{0,2},{1,3},{2,0},{3,1},{4,6},{5,7},{6,4},{7,5},{8,10},{9,11},{10,... | collective-permute-start | bytes 196616 | tf_op jit(solution)/shard_map/ppermute | solution.py:26
  56.0 3.6 %collective-permute-done.1 = f32[16,1024]{1,0:T(8,128)S(1)} collective-permute-done((f32[16,1024]{1,0:T(8,128)S(1)}, f32[16,1024]{1,0:T(8,128)S(1)}, u32[]{:S(2)}, u32[]{:S(2)}) %collective-permute-start.1) | collective-permute-done | bytes 65568 | tf_op jit(solution)/shard_map/ppermute | solution.py:26
  59.6 6.1 %collective-permute-start.2 = (f32[16,1024]{1,0:T(8,128)S(1)}, f32[16,1024]{1,0:T(8,128)S(1)}, u32[]{:S(2)}, u32[]{:S(2)}) collective-permute-start(f32[16,1024]{1,0:T(8,128)S(1)} %add.87), channel_id=1, source_target_pairs={{0,4},{1,5},{2,6},{3,7},{4,0},{5,1},{6,2},{7,3},{8,12},{9,13},{10,... | collective-permute-start | bytes 196616 | tf_op jit(solution)/shard_map/ppermute | solution.py:26
  65.7 3.5 %copy.111 = bf16[128,8,2,512]{3,1,2,0:T(8,128)(2,1)} copy(bf16[128,8,2,512]{3,2,1,0:T(2,128)(2,1)} %bitcast.67) | data formatting | bytes 4194304
  69.2 2.9 %copy.106 = bf16[1024,1024]{1,0:T(8,128)(2,1)S(1)} copy(bf16[1024,1024]{0,1:T(8,128)(2,1)} %bitcast.65) | data formatting | bytes 4194304 | tf_op jit(solution)/shard_map/dot_general | solution.py:179
  72.3 0.6 fusion.30
  72.9 0.3 fusion.41
  73.2 0.4 collective-permute-start.3
  73.6 3.9 %collective-permute-done.3 = f32[16,1024]{1,0:T(8,128)S(1)} collective-permute-done((f32[16,1024]{1,0:T(8,128)S(1)}, f32[16,1024]{1,0:T(8,128)S(1)}, u32[]{:S(2)}, u32[]{:S(2)}) %collective-permute-start.3) | collective-permute-done | bytes 65568 | tf_op jit(solution)/shard_map/ppermute | solution.py:26
  77.5 0.9 collective-permute-start.4
  78.4 4.8 %collective-permute-done.4 = f32[16,1024]{1,0:T(8,128)S(1)} collective-permute-done((f32[16,1024]{1,0:T(8,128)S(1)}, f32[16,1024]{1,0:T(8,128)S(1)}, u32[]{:S(2)}, u32[]{:S(2)}) %collective-permute-start.4) | collective-permute-done | bytes 65568 | tf_op jit(solution)/shard_map/ppermute | solution.py:26
  83.3 2.0 %collective-permute-start.5 = (f32[16,1024]{1,0:T(8,128)S(1)}, f32[16,1024]{1,0:T(8,128)S(1)}, u32[]{:S(2)}, u32[]{:S(2)}) collective-permute-start(f32[16,1024]{1,0:T(8,128)S(1)} %add.93), channel_id=1, source_target_pairs={{0,4},{1,5},{2,6},{3,7},{4,0},{5,1},{6,2},{7,3},{8,12},{9,13},{10,... | collective-permute-start | bytes 196616 | tf_op jit(solution)/shard_map/ppermute | solution.py:26
  85.3 0.6 pad_maximum_fusion.1
  85.9 5.6 %collective-permute-done.5 = f32[16,1024]{1,0:T(8,128)S(1)} collective-permute-done((f32[16,1024]{1,0:T(8,128)S(1)}, f32[16,1024]{1,0:T(8,128)S(1)}, u32[]{:S(2)}, u32[]{:S(2)}) %collective-permute-start.5) | collective-permute-done | bytes 65568 | tf_op jit(solution)/shard_map/ppermute | solution.py:26
  91.5 0.6 fusion.27
  (54 shorter events, 1.6 us)
Async XLA Ops:
  0.6 72.3 %copy-start = (bf16[512,1024]{1,0:T(8,128)(2,1)S(1)}, bf16[512,1024]{1,0:T(8,128)(2,1)}, u32[]{:S(2)}) copy-start(bf16[512,1024]{1,0:T(8,128)(2,1)} %param.17) | copy-start | bytes 3145732
  4.8 14.2 %all-to-all-start = ((bf16[32,16,128]{2,1,0:T(8,128)(2,1)}), bf16[32,16,128]{2,1,0:T(8,128)(2,1)S(1)}, u32[]{:S(2)}, u32[]{:S(2)}) async-start(bf16[32,16,128]{2,1,0:T(8,128)(2,1)} %broadcast_in_dim.131), calls=%async_computation | async-start | bytes 262144 | tf_op jit(solution)/shard_map/all_to_all | solution.py:34
  24.3 5.3 %copy-start.4 = (s32[128]{0:T(128)S(1)}, s32[128]{0:T(128)}, u32[]{:S(2)}) copy-start(s32[128]{0:T(128)} %param.20) | copy-start | bytes 1540
  29.3 18.5 %copy-start.2 = (bf16[128,1024]{1,0:T(8,128)(2,1)S(1)}, bf16[128,1024]{1,0:T(8,128)(2,1)}, u32[]{:S(2)}) copy-start(bf16[128,1024]{1,0:T(8,128)(2,1)} %param.14) | copy-start | bytes 786436
  48.0 4.6 %collective-permute-start = (f32[16,1024]{1,0:T(8,128)S(1)}, f32[16,1024]{1,0:T(8,128)S(1)}, u32[]{:S(2)}, u32[]{:S(2)}) collective-permute-start(f32[16,1024]{1,0:T(8,128)S(1)} %fusion.46), channel_id=1, source_target_pairs={{0,1},{1,0},{2,3},{3,2},{4,5},{5,4},{6,7},{7,6},{8,9},{9,8},{10,11... | collective-permute-start | bytes 196616 | tf_op jit(solution)/shard_map/ppermute | solution.py:26
  52.6 7.0 %collective-permute-start.1 = (f32[16,1024]{1,0:T(8,128)S(1)}, f32[16,1024]{1,0:T(8,128)S(1)}, u32[]{:S(2)}, u32[]{:S(2)}) collective-permute-start(f32[16,1024]{1,0:T(8,128)S(1)} %add.86), channel_id=1, source_target_pairs={{0,2},{1,3},{2,0},{3,1},{4,6},{5,7},{6,4},{7,5},{8,10},{9,11},{10,... | collective-permute-start | bytes 196616 | tf_op jit(solution)/shard_map/ppermute | solution.py:26
  59.6 12.5 %collective-permute-start.2 = (f32[16,1024]{1,0:T(8,128)S(1)}, f32[16,1024]{1,0:T(8,128)S(1)}, u32[]{:S(2)}, u32[]{:S(2)}) collective-permute-start(f32[16,1024]{1,0:T(8,128)S(1)} %add.87), channel_id=1, source_target_pairs={{0,4},{1,5},{2,6},{3,7},{4,0},{5,1},{6,2},{7,3},{8,12},{9,13},{10,... | collective-permute-start | bytes 196616 | tf_op jit(solution)/shard_map/ppermute | solution.py:26
  65.7 6.4 %copy-start.1 = (bf16[16,1024]{1,0:T(8,128)(2,1)S(1)}, bf16[16,1024]{1,0:T(8,128)(2,1)}, u32[]{:S(2)}) copy-start(bf16[16,1024]{1,0:T(8,128)(2,1)} %param.11) | copy-start | bytes 98308
  65.7 6.6 %copy-start.3 = (f32[1024]{0:T(1024)S(1)}, f32[1024]{0:T(1024)}, u32[]{:S(2)}) copy-start(f32[1024]{0:T(1024)} %param.15) | copy-start | bytes 12292
  73.2 4.3 %collective-permute-start.3 = (f32[16,1024]{1,0:T(8,128)S(1)}, f32[16,1024]{1,0:T(8,128)S(1)}, u32[]{:S(2)}, u32[]{:S(2)}) collective-permute-start(f32[16,1024]{1,0:T(8,128)S(1)} %fusion.41), channel_id=1, source_target_pairs={{0,1},{1,0},{2,3},{3,2},{4,5},{5,4},{6,7},{7,6},{8,9},{9,8},{10,11... | collective-permute-start | bytes 196616 | tf_op jit(solution)/shard_map/ppermute | solution.py:26
  77.5 5.8 %collective-permute-start.4 = (f32[16,1024]{1,0:T(8,128)S(1)}, f32[16,1024]{1,0:T(8,128)S(1)}, u32[]{:S(2)}, u32[]{:S(2)}) collective-permute-start(f32[16,1024]{1,0:T(8,128)S(1)} %add.92), channel_id=1, source_target_pairs={{0,2},{1,3},{2,0},{3,1},{4,6},{5,7},{6,4},{7,5},{8,10},{9,11},{10,... | collective-permute-start | bytes 196616 | tf_op jit(solution)/shard_map/ppermute | solution.py:26
  83.3 8.3 %collective-permute-start.5 = (f32[16,1024]{1,0:T(8,128)S(1)}, f32[16,1024]{1,0:T(8,128)S(1)}, u32[]{:S(2)}, u32[]{:S(2)}) collective-permute-start(f32[16,1024]{1,0:T(8,128)S(1)} %add.93), channel_id=1, source_target_pairs={{0,4},{1,5},{2,6},{3,7},{4,0},{5,1},{6,2},{7,3},{8,12},{9,13},{10,... | collective-permute-start | bytes 196616 | tf_op jit(solution)/shard_map/ppermute | solution.py:26

commit v6 on v5

--- a/solution.py
+++ b/solution.py
@@ -81,6 +81,7 @@
         local_rows, 3, head_cols
     )
     appended = jnp.stack([projected[:, 1], projected[:, 2]])
+    full_w_out = butterfly_gather(w_out, "mp")
     every_query = exchange_gather(projected[:, 0], "dp")
     own_queries = projected[:, 0].reshape(local_rows, local_heads, HEAD_DIM).astype(jnp.float32)
     own_keys = projected[:, 1].reshape(local_rows, local_heads, HEAD_DIM).astype(jnp.float32)
@@ -170,7 +171,11 @@
     context = (
         (own_weighted / own_totals[:, :, None]).reshape(local_rows, head_cols).astype(jnp.bfloat16)
     )
-    attended = butterfly_sum(jnp.dot(context, w_out, preferred_element_type=jnp.float32), "mp")
+    model_devices = lax.axis_size("mp")
+    every_context = exchange_gather(context, "mp")
+    every_context = every_context.reshape(model_devices, local_rows, head_cols)
+    every_context = every_context.transpose(1, 0, 2).reshape(local_rows, model_devices * head_cols)
+    attended = jnp.dot(every_context, full_w_out, preferred_element_type=jnp.float32)
     residual = lax.optimization_barrier(
         (hidden.astype(jnp.float32) + attended).astype(jnp.bfloat16)
     )

time: 93.1 us -> 135 us (1.45)
  waiting for transfers between devices: 22.2 us -> 60.7 us
  starting transfers between devices: 22.3 us -> 25.9 us
  matrix products: 10.5 us -> 13.2 us
  blocking collectives: 14.8 us -> 13.3 us
    all_to_all x1 -> x2, waiting for transfers between devices: 1.44 us -> 25 us  [exchange_gather(): gathered = lax.all_to_all(spread, axis, 0, 0, tiled=True)]
    ppermute x0 -> x3, waiting for transfers between devices: none -> 21.7 us  [butterfly_gather(): other = lax.ppermute(value, axis, pairs)]
    ppermute x0 -> x3, starting transfers between devices: none -> 11.5 us  [butterfly_gather(): other = lax.ppermute(value, axis, pairs)]
    ppermute x6 -> x3, starting transfers between devices: 14.7 us -> 3.29 us  [butterfly_sum(): value = value + lax.ppermute(value, axis, pairs)]
    ppermute x6 -> x3, waiting for transfers between devices: 20.7 us -> 14 us  [butterfly_sum(): value = value + lax.ppermute(value, axis, pairs)]
    all_to_all x1 -> x2, starting transfers between devices: 7.62 us -> 11.1 us  [exchange_gather(): gathered = lax.all_to_all(spread, axis, 0, 0, tiled=True)]
    dot_general x1, matrix products: 0.15 us -> 2.77 us  [body(): jnp.dot(every_context, full_w_out, preferred_element_type=jnp.float32)]
    select_n x0 -> x2, other arithmetic: none -> 1.62 us  [butterfly_gather(): jnp.where(low, jnp.concatenate([value, other], 0), jnp.concatenate([other...]
  transfers between devices with their start and end apart: 7 -> 8, of which waited for: 6 -> 6; matrix products, arithmetic and copies ran while one was open for 13% -> 20% of each run, Pallas kernels for 0% -> 0%
where the time goes in v6:
time: 135 us
  waiting for transfers between devices  60.7 us (45%)
  starting transfers between devices  25.9 us (19%)
  local copies, waits for them, and re-layouts  15.1 us (11%)
  blocking collectives  13.3 us (10%)
  matrix products  13.2 us (10%)
  other arithmetic  5.38 us (4%)
    all_to_all x2, waiting for transfers between devices, exchange_gather(): gathered = lax.all_to_all(spread, axis, 0, 0, tiled=True)  25 us
    ppermute x3, waiting for transfers between devices, butterfly_gather(): other = lax.ppermute(value, axis, pairs)  21.7 us
    ppermute x3, waiting for transfers between devices, butterfly_sum(): value = value + lax.ppermute(value, axis, pairs)  14 us
    all_to_all x1, blocking collectives, body(): received = lax.all_to_all(packed, 'dp', 0, 0, tiled=True)  13.3 us
    ppermute x3, starting transfers between devices, butterfly_gather(): other = lax.ppermute(value, axis, pairs)  11.5 us
    all_to_all x2, starting transfers between devices, exchange_gather(): gathered = lax.all_to_all(spread, axis, 0, 0, tiled=True)  11.1 us
    unnamed x18, local copies, waits for them, and re-layouts  5.08 us
    dot_general x1, matrix products, body(): jnp.einsum('ptc,pch->pth', key_rows, query_blocks, preferred_element_type...  4.54 us
  transfers between devices with their start and end apart: 8, of which 6 were waited for; matrix products, arithmetic and copies ran while one was open for 20% of the time, Pallas kernels for 0%

profile of v6, /device:TPU:2, one launch (start us, length us, event | category | flops | bytes accessed | tf_op | source)
XLA Modules:
  0.0 134.7 jit_solution(2313673326884390564)
XLA Ops:
  0.7 2.0 %collective-permute-start = (bf16[128,1024]{1,0:T(8,128)(2,1)}, bf16[128,1024]{1,0:T(8,128)(2,1)S(1)}, u32[]{:S(2)}, u32[]{:S(2)}) collective-permute-start(bf16[128,1024]{1,0:T(8,128)(2,1)} %param.14), channel_id=1, source_target_pairs={{0,1},{1,0},{2,3},{3,2},{4,5},{5,4},{6,7},{7,6},{8,9},{9,8},{10,11... | collective-permute-start | bytes 786440 | tf_op jit(solution)/shard_map/ppermute | solution.py:46
  2.7 1.4 %copy.96 = bf16[1024,3,128]{0,2,1:T(8,128)(2,1)S(1)} copy(bf16[1024,3,128]{2,0,1:T(8,128)(2,1)} %param.13) | data formatting | bytes 1572864 | tf_op args[2]
  4.1 0.9 fusion.29
  5.0 1.1 convolution_convert_fusion
  6.1 0.7 broadcast_in_dim.137
  6.8 7.6 %all-to-all-start = ((bf16[32,16,128]{2,1,0:T(8,128)(2,1)}), bf16[32,16,128]{2,1,0:T(8,128)(2,1)S(1)}, u32[]{:S(2)}, u32[]{:S(2)}) async-start(bf16[32,16,128]{2,1,0:T(8,128)(2,1)} %broadcast_in_dim.137), calls=%async_computation | async-start | bytes 262144 | tf_op jit(solution)/shard_map/all_to_all | solution.py:34
  14.9 0.1 copy.113
  15.1 1.3 gather_fusion
  16.5 0.2 dynamic_update_slice.6
  16.7 4.4 %all-to-all-done = bf16[32,16,128]{2,1,0:T(8,128)(2,1)S(1)} async-done(((bf16[32,16,128]{2,1,0:T(8,128)(2,1)}), bf16[32,16,128]{2,1,0:T(8,128)(2,1)S(1)}, u32[]{:S(2)}, u32[]{:S(2)}) %all-to-all-start) | async-done | bytes 131104 | tf_op jit(solution)/shard_map/all_to_all | solution.py:34
  21.0 0.7 gather_fusion.1
  21.7 4.5 %select_reduce_fusion.1 = (f32[128,2]{1,0:T(8,128)S(1)}, f32[128,2,128]{2,1,0:T(2,128)S(1)}) fusion(pred[128,128]{1,0:T(8,128)(4,1)S(1)} %fusion.36, bf16[2,128,128,128]{3,2,1,0:T(8,128)(2,1)} %param.18, pred[128,2]{0,1:T(4,128)(4,1)S(1)} %iota_compare_fusion.2, bf16[128,128]{1,0:T(8,128)(2,1)S(1)} %gather_fusion.1), kind=kOutput, calls=%fused_computation.37 | convolution fusion | flops 8519424 | bytes 4375808 | tf_op jit(solution)/shard_map/ptc,pch->pth/dot_general | solution.py:103
  26.3 0.4 bitcast_reduce_fusion
  26.8 0.1 select_reduce_fusion
  26.9 0.1 copy.101
  27.1 0.7 gather_fusion.2
  28.0 3.5 %fusion.21 = f32[128,128]{1,0:T(8,128)S(1)} fusion(bf16[2,128,128,128]{3,2,1,0:T(8,128)(2,1)} %param.18, pred[2,128]{1,0:T(4,128)(4,1)S(1)} %iota_compare_fusion.3, f32[128,2,128]{2,1,0:T(2,128)S(1)} %get-tuple-element.16, pred[128,128]{1,0:T(8,128)(4,1)S(1)} %fusion.36, f32[128,2]{1,0:T(8,128)S(1)} %get-tuple-element.15), kind=kOutput, calls=%fused_computation.21 | convolution fusion | flops 8536064 | bytes 4408576 | tf_op jit(solution)/shard_map/pth,ptc->phc/dot_general | solution.py:111
  31.6 0.1 maximum_select_fusion.7
  31.7 3.4 %collective-permute-start.1 = (bf16[256,1024]{1,0:T(8,128)(2,1)S(1)}, bf16[256,1024]{1,0:T(8,128)(2,1)S(1)}, u32[]{:S(2)}, u32[]{:S(2)}) collective-permute-start(bf16[256,1024]{1,0:T(8,128)(2,1)S(1)} %maximum_select_fusion.7), channel_id=1, source_target_pairs={{0,2},{1,3},{2,0},{3,1},{4,6},{5,7},{6,4},{7,5},{8,10},{9,11},{10,... | collective-permute-start | bytes 1572872 | tf_op jit(solution)/shard_map/ppermute | solution.py:46
  35.1 0.4 fusion.25
  35.6 0.7 add.76
  36.3 21.7 %collective-permute-done.1 = bf16[256,1024]{1,0:T(8,128)(2,1)S(1)} collective-permute-done((bf16[256,1024]{1,0:T(8,128)(2,1)S(1)}, bf16[256,1024]{1,0:T(8,128)(2,1)S(1)}, u32[]{:S(2)}, u32[]{:S(2)}) %collective-permute-start.1) | collective-permute-done | bytes 524320 | tf_op jit(solution)/shard_map/ppermute | solution.py:46
  58.0 1.5 %maximum_select_fusion.6 = bf16[512,1024]{1,0:T(8,128)(2,1)} fusion(bf16[256,1024]{1,0:T(8,128)(2,1)S(1)} %collective-permute-done.1, bf16[256,1024]{1,0:T(8,128)(2,1)S(1)} %maximum_select_fusion.7, pred[]{:T(512)S(6)} %eq.64), kind=kLoop, calls=%fused_computation.23 | loop fusion | flops 4718592 | bytes 2097153 | tf_op jit(solution)/shard_map/jit(_where)/select_n | solution.py:48
  59.5 6.1 %collective-permute-start.2 = (bf16[512,1024]{1,0:T(8,128)(2,1)}, bf16[512,1024]{1,0:T(8,128)(2,1)}, u32[]{:S(2)}, u32[]{:S(2)}) collective-permute-start(bf16[512,1024]{1,0:T(8,128)(2,1)} %maximum_select_fusion.6), channel_id=1, source_target_pairs={{0,4},{1,5},{2,6},{3,7},{4,0},{5,1},{6,2},{7,3},{8,12},{9,13},{10,... | collective-permute-start | bytes 3145736 | tf_op jit(solution)/shard_map/ppermute | solution.py:46
  65.7 0.1 copy.105
  65.8 0.2 reshape.217
  66.0 0.1 copy.104
  66.2 13.3 %all_to_all.15 = f32[32,17,128]{2,1,0:T(8,128)S(1)} all-to-all(f32[32,17,128]{2,1,0:T(8,128)S(1)} %pad_maximum_fusion), channel_id=1, replica_groups=mesh['dp'=32,'mp'=8] {'dp'}, dimensions={0} | all-to-all | bytes 557056 | tf_op jit(solution)/shard_map/all_to_all | solution.py:152
  79.5 0.2 fusion.53
  79.7 0.2 copy.108
  79.9 0.6 broadcast_in_dim.149
  80.5 0.3 reshape.221
  81.1 0.6 broadcast_in_dim.150
  81.7 3.5 %all-to-all-start.2 = ((bf16[8,16,128]{2,1,0:T(8,128)(2,1)}), bf16[8,16,128]{2,1,0:T(8,128)(2,1)S(1)}, u32[]{:S(2)}, u32[]{:S(2)}) async-start(bf16[8,16,128]{2,1,0:T(8,128)(2,1)} %broadcast_in_dim.150), calls=%async_computation.2 | async-start | bytes 65536 | tf_op jit(solution)/shard_map/all_to_all | solution.py:34
  85.2 3.5 %copy.116 = bf16[128,8,2,512]{3,1,2,0:T(8,128)(2,1)} copy(bf16[128,8,2,512]{3,2,1,0:T(2,128)(2,1)} %bitcast.74) | data formatting | bytes 4194304
  88.8 2.9 %copy.110 = bf16[1024,1024]{1,0:T(8,128)(2,1)S(1)} copy(bf16[1024,1024]{0,1:T(8,128)(2,1)} %bitcast.72) | data formatting | bytes 4194304 | tf_op jit(solution)/shard_map/dot_general | solution.py:184
  91.6 20.6 %all-to-all-done.2 = bf16[8,16,128]{2,1,0:T(8,128)(2,1)S(1)} async-done(((bf16[8,16,128]{2,1,0:T(8,128)(2,1)}), bf16[8,16,128]{2,1,0:T(8,128)(2,1)S(1)}, u32[]{:S(2)}, u32[]{:S(2)}) %all-to-all-start.2) | async-done | bytes 32800 | tf_op jit(solution)/shard_map/all_to_all | solution.py:34
  112.3 2.8 %fusion.20 = bf16[16,1024]{1,0:T(8,128)(2,1)S(1)} fusion(bf16[512,1024]{1,0:T(8,128)(2,1)} %collective-permute-done.2, bf16[512,1024]{1,0:T(8,128)(2,1)} %maximum_select_fusion.6, pred[]{:T(512)S(6)} %eq.63, bf16[16,1024]{1,0:T(8,128)(2,1)S(1)} %copy-done.3, bf16[8,16,128]{2,1,0:T(8,128)(2,1)S(1)} %all-to-all-done.2), kind=kOutput, calls=%fused_computation.20 | convolution fusion | flops 43040768 | bytes 2195457 | tf_op jit(solution)/shard_map/dot_general | solution.py:178
  115.0 0.1 fusion.32
  115.2 0.6 fusion.38
  115.8 0.3 fusion.51
  116.1 4.3 %collective-permute-done.3 = f32[16,1024]{1,0:T(8,128)S(1)} collective-permute-done((f32[16,1024]{1,0:T(8,128)S(1)}, f32[16,1024]{1,0:T(8,128)S(1)}, u32[]{:S(2)}, u32[]{:S(2)}) %collective-permute-start.3) | collective-permute-done | bytes 65568 | tf_op jit(solution)/shard_map/ppermute | solution.py:26
  120.4 0.6 collective-permute-start.4
  121.0 4.8 %collective-permute-done.4 = f32[16,1024]{1,0:T(8,128)S(1)} collective-permute-done((f32[16,1024]{1,0:T(8,128)S(1)}, f32[16,1024]{1,0:T(8,128)S(1)}, u32[]{:S(2)}, u32[]{:S(2)}) %collective-permute-start.4) | collective-permute-done | bytes 65568 | tf_op jit(solution)/shard_map/ppermute | solution.py:26
  125.8 2.7 %collective-permute-start.5 = (f32[16,1024]{1,0:T(8,128)S(1)}, f32[16,1024]{1,0:T(8,128)S(1)}, u32[]{:S(2)}, u32[]{:S(2)}) collective-permute-start(f32[16,1024]{1,0:T(8,128)S(1)} %add.81), channel_id=1, source_target_pairs={{0,4},{1,5},{2,6},{3,7},{4,0},{5,1},{6,2},{7,3},{8,12},{9,13},{10,... | collective-permute-start | bytes 196616 | tf_op jit(solution)/shard_map/ppermute | solution.py:26
  128.5 0.6 pad_maximum_fusion.1
  129.1 4.9 %collective-permute-done.5 = f32[16,1024]{1,0:T(8,128)S(1)} collective-permute-done((f32[16,1024]{1,0:T(8,128)S(1)}, f32[16,1024]{1,0:T(8,128)S(1)}, u32[]{:S(2)}, u32[]{:S(2)}) %collective-permute-start.5) | collective-permute-done | bytes 65568 | tf_op jit(solution)/shard_map/ppermute | solution.py:26
  134.1 0.6 fusion.35
  (61 shorter events, 1.6 us)
Async XLA Ops:
  0.6 115.2 %copy-start = (bf16[512,1024]{1,0:T(8,128)(2,1)S(1)}, bf16[512,1024]{1,0:T(8,128)(2,1)}, u32[]{:S(2)}) copy-start(bf16[512,1024]{1,0:T(8,128)(2,1)} %param.17) | copy-start | bytes 3145732
  0.6 13.8 %copy-start.5 = (s32[128]{0:T(128)S(1)}, s32[128]{0:T(128)}, u32[]{:S(2)}) copy-start(s32[128]{0:T(128)} %param.20) | copy-start | bytes 1540
  0.7 14.0 %copy-start.6 = (s32[128]{0:T(128)S(1)}, s32[128]{0:T(128)}, u32[]{:S(2)}) copy-start(s32[128]{0:T(128)} %param.21) | copy-start | bytes 1540
  0.7 14.4 %copy-start.1 = (s32[512]{0:T(512)S(1)}, s32[512]{0:T(512)}, u32[]{:S(2)}) copy-start(s32[512]{0:T(512)} %param.19) | copy-start | bytes 6148
  0.7 30.9 %collective-permute-start = (bf16[128,1024]{1,0:T(8,128)(2,1)}, bf16[128,1024]{1,0:T(8,128)(2,1)S(1)}, u32[]{:S(2)}, u32[]{:S(2)}) collective-permute-start(bf16[128,1024]{1,0:T(8,128)(2,1)} %param.14), channel_id=1, source_target_pairs={{0,1},{1,0},{2,3},{3,2},{4,5},{5,4},{6,7},{7,6},{8,9},{9,8},{10,11... | collective-permute-start | bytes 786440 | tf_op jit(solution)/shard_map/ppermute | solution.py:46
  6.8 14.2 %all-to-all-start = ((bf16[32,16,128]{2,1,0:T(8,128)(2,1)}), bf16[32,16,128]{2,1,0:T(8,128)(2,1)S(1)}, u32[]{:S(2)}, u32[]{:S(2)}) async-start(bf16[32,16,128]{2,1,0:T(8,128)(2,1)} %broadcast_in_dim.137), calls=%async_computation | async-start | bytes 262144 | tf_op jit(solution)/shard_map/all_to_all | solution.py:34
  28.0 3.6 %copy-start.2 = (bf16[128,1024]{1,0:T(8,128)(2,1)S(1)}, bf16[128,1024]{1,0:T(8,128)(2,1)}, u32[]{:S(2)}) copy-start(bf16[128,1024]{1,0:T(8,128)(2,1)} %param.14) | copy-start | bytes 786436
  31.7 26.3 %collective-permute-start.1 = (bf16[256,1024]{1,0:T(8,128)(2,1)S(1)}, bf16[256,1024]{1,0:T(8,128)(2,1)S(1)}, u32[]{:S(2)}, u32[]{:S(2)}) collective-permute-start(bf16[256,1024]{1,0:T(8,128)(2,1)S(1)} %maximum_select_fusion.7), channel_id=1, source_target_pairs={{0,2},{1,3},{2,0},{3,1},{4,6},{5,7},{6,4},{7,5},{8,10},{9,11},{10,... | collective-permute-start | bytes 1572872 | tf_op jit(solution)/shard_map/ppermute | solution.py:46
  59.5 52.7 %collective-permute-start.2 = (bf16[512,1024]{1,0:T(8,128)(2,1)}, bf16[512,1024]{1,0:T(8,128)(2,1)}, u32[]{:S(2)}, u32[]{:S(2)}) collective-permute-start(bf16[512,1024]{1,0:T(8,128)(2,1)} %maximum_select_fusion.6), channel_id=1, source_target_pairs={{0,4},{1,5},{2,6},{3,7},{4,0},{5,1},{6,2},{7,3},{8,12},{9,13},{10,... | collective-permute-start | bytes 3145736 | tf_op jit(solution)/shard_map/ppermute | solution.py:46
  81.7 30.6 %all-to-all-start.2 = ((bf16[8,16,128]{2,1,0:T(8,128)(2,1)}), bf16[8,16,128]{2,1,0:T(8,128)(2,1)S(1)}, u32[]{:S(2)}, u32[]{:S(2)}) async-start(bf16[8,16,128]{2,1,0:T(8,128)(2,1)} %broadcast_in_dim.150), calls=%async_computation.2 | async-start | bytes 65536 | tf_op jit(solution)/shard_map/all_to_all | solution.py:34
  88.7 23.5 %copy-start.3 = (bf16[16,1024]{1,0:T(8,128)(2,1)S(1)}, bf16[16,1024]{1,0:T(8,128)(2,1)}, u32[]{:S(2)}) copy-start(bf16[16,1024]{1,0:T(8,128)(2,1)} %param.11) | copy-start | bytes 98308
  91.6 23.6 %copy-start.4 = (f32[1024]{0:T(1024)S(1)}, f32[1024]{0:T(1024)}, u32[]{:S(2)}) copy-start(f32[1024]{0:T(1024)} %param.15) | copy-start | bytes 12292
  116.1 4.3 %collective-permute-start.3 = (f32[16,1024]{1,0:T(8,128)S(1)}, f32[16,1024]{1,0:T(8,128)S(1)}, u32[]{:S(2)}, u32[]{:S(2)}) collective-permute-start(f32[16,1024]{1,0:T(8,128)S(1)} %fusion.51), channel_id=1, source_target_pairs={{0,1},{1,0},{2,3},{3,2},{4,5},{5,4},{6,7},{7,6},{8,9},{9,8},{10,11... | collective-permute-start | bytes 196616 | tf_op jit(solution)/shard_map/ppermute | solution.py:26
  120.4 5.4 %collective-permute-start.4 = (f32[16,1024]{1,0:T(8,128)S(1)}, f32[16,1024]{1,0:T(8,128)S(1)}, u32[]{:S(2)}, u32[]{:S(2)}) collective-permute-start(f32[16,1024]{1,0:T(8,128)S(1)} %add.80), channel_id=1, source_target_pairs={{0,2},{1,3},{2,0},{3,1},{4,6},{5,7},{6,4},{7,5},{8,10},{9,11},{10,... | collective-permute-start | bytes 196616 | tf_op jit(solution)/shard_map/ppermute | solution.py:26
  125.8 8.3 %collective-permute-start.5 = (f32[16,1024]{1,0:T(8,128)S(1)}, f32[16,1024]{1,0:T(8,128)S(1)}, u32[]{:S(2)}, u32[]{:S(2)}) collective-permute-start(f32[16,1024]{1,0:T(8,128)S(1)} %add.81), channel_id=1, source_target_pairs={{0,4},{1,5},{2,6},{3,7},{4,0},{5,1},{6,2},{7,3},{8,12},{9,13},{10,... | collective-permute-start | bytes 196616 | tf_op jit(solution)/shard_map/ppermute | solution.py:26

commit v7 on v5

--- a/solution.py
+++ b/solution.py
@@ -74,12 +74,8 @@
     requests = local_rows * data_devices
     score_scale = HEAD_DIM ** (-0.5)
     normed = rms_norm(hidden, attn_gain)
-    projected = jnp.dot(
-        normed, w_qkv.reshape(w_qkv.shape[0], 3 * head_cols), preferred_element_type=jnp.float32
-    )
-    projected = lax.optimization_barrier(projected.astype(jnp.bfloat16)).reshape(
-        local_rows, 3, head_cols
-    )
+    projected = jnp.einsum("rd,dkc->rkc", normed, w_qkv, preferred_element_type=jnp.float32)
+    projected = lax.optimization_barrier(projected.astype(jnp.bfloat16))
     appended = jnp.stack([projected[:, 1], projected[:, 2]])
     every_query = exchange_gather(projected[:, 0], "dp")
     own_queries = projected[:, 0].reshape(local_rows, local_heads, HEAD_DIM).astype(jnp.float32)
@@ -176,11 +172,7 @@
     )
     normed_mlp = rms_norm(residual, mlp_gain)
     hidden_cols = w_gate_up.shape[2]
-    gate_up = jnp.dot(
-        normed_mlp,
-        w_gate_up.reshape(w_gate_up.shape[0], 2 * hidden_cols),
-        preferred_element_type=jnp.float32,
-    ).reshape(local_rows, 2, hidden_cols)
+    gate_up = jnp.einsum("rd,dkc->rkc", normed_mlp, w_gate_up, preferred_element_type=jnp.float32)
     activated = (jax.nn.silu(gate_up[:, 0]) * gate_up[:, 1]).astype(jnp.bfloat16)
     lowered = butterfly_sum(jnp.dot(activated, w_down, preferred_element_type=jnp.float32), "mp")
     hidden_out = (residual.astype(jnp.float32) + lowered).astype(jnp.bfloat16)

time: 93.1 us -> 89 us (0.956)
  local copies, waits for them, and re-layouts: 14.9 us -> 5.91 us
  starting transfers between devices: 22.3 us -> 29.9 us
  waiting for transfers between devices: 22.2 us -> 18.2 us
  matrix products: 10.5 us -> 12.9 us
    ppermute x6, starting transfers between devices: 14.7 us -> 22.2 us  [butterfly_sum(): value = value + lax.ppermute(value, axis, pairs)]
    unnamed x14 -> x9, local copies, waits for them, and re-layouts: 5.16 us -> 0.13 us
    ppermute x6, waiting for transfers between devices: 20.7 us -> 16.3 us  [butterfly_sum(): value = value + lax.ppermute(value, axis, pairs)]
    dot_general x1 -> x0, local copies, waits for them, and re-layouts: 2.85 us -> none  [body(): jnp.dot(normed_mlp, w_gate_up.reshape(w_gate_up.shape[0], 2 * hidden_cols...]
    dot_general x1, matrix products: 0.26 us -> 1.48 us  [body(): jnp.dot(activated, w_down, preferred_element_type=jnp.float32)]
    dot_general x1, matrix products: 0.15 us -> 1.1 us  [body(): jnp.dot(context, w_out, preferred_element_type=jnp.float32)]
  transfers between devices with their start and end apart: 7 -> 7, of which waited for: 6 -> 7; matrix products, arithmetic and copies ran while one was open for 13% -> 6% of each run, Pallas kernels for 0% -> 0%
where the time goes in v7:
time: 89 us; the launch traced here: 88.5 us
  starting transfers between devices  29.9 us (34%)
  waiting for transfers between devices  18.2 us (20%)
  blocking collectives  14.2 us (16%)
  matrix products  12.9 us (14%)
  other arithmetic  6.53 us (7%)
  local copies, waits for them, and re-layouts  5.91 us (7%)
  between operations  0.96 us (1%)
    ppermute x6, starting transfers between devices, butterfly_sum(): value = value + lax.ppermute(value, axis, pairs)  22.2 us
    ppermute x6, waiting for transfers between devices, butterfly_sum(): value = value + lax.ppermute(value, axis, pairs)  16.3 us
    all_to_all x1, blocking collectives, body(): received = lax.all_to_all(packed, 'dp', 0, 0, tiled=True)  14.2 us
    all_to_all x1, starting transfers between devices, exchange_gather(): gathered = lax.all_to_all(spread, axis, 0, 0, tiled=True)  7.62 us
    dot_general x1, matrix products, body(): jnp.einsum('ptc,pch->pth', key_rows, query_blocks, preferred_element_type...  4.54 us
    dot_general x1, matrix products, body(): jnp.einsum('pth,ptc->phc', raw.astype(jnp.bfloat16), value_rows, preferre...  3.49 us
    all_to_all x1, waiting for transfers between devices, exchange_gather(): gathered = lax.all_to_all(spread, axis, 0, 0, tiled=True)  1.82 us
  transfers between devices with their start and end apart: 7, of which 7 were waited for; matrix products, arithmetic and copies ran while one was open for 6% of the time, Pallas kernels for 0%

profile of v7, /device:TPU:2, one launch (start us, length us, event | category | flops | bytes accessed | tf_op | source)
XLA Modules:
  0.0 88.5 jit_solution(4730864489981432893)
XLA Ops:
  0.6 1.0 %fusion.22 = f32[16]{0:T(128)S(1)} fusion(bf16[16,1024]{1,0:T(8,128)(2,1)} %param.11), kind=kLoop, calls=%fused_computation.36 | loop fusion | flops 49136 | bytes 32832 | tf_op jit(solution)/shard_map/reduce_sum | solution.py:15
  1.7 1.4 %convolution_convert_fusion = bf16[16,3,128]{2,0,1:T(8,128)(2,1)S(1)} fusion(bf16[1024,3,128]{2,0,1:T(8,128)(2,1)} %param.13, bf16[16,1024]{1,0:T(8,128)(2,1)} %param.11, f32[1024]{0:T(1024)} %param.12, f32[16]{0:T(128)S(1)} %add_rsqrt_fusion.1), kind=kOutput, calls=%fused_computation.14 | convolution fusion | flops 12654592 | bytes 835648 | tf_op jit(solution)/shard_map/rd,dkc->rkc/dot_general | solution.py:77
  3.1 0.7 broadcast_in_dim.131
  3.8 7.6 %all-to-all-start = ((bf16[32,16,128]{2,1,0:T(8,128)(2,1)}), bf16[32,16,128]{2,1,0:T(8,128)(2,1)S(1)}, u32[]{:S(2)}, u32[]{:S(2)}) async-start(bf16[32,16,128]{2,1,0:T(8,128)(2,1)} %broadcast_in_dim.131), calls=%async_computation | async-start | bytes 262144 | tf_op jit(solution)/shard_map/all_to_all | solution.py:34
  11.4 0.7 broadcast_compare_fusion
  12.1 0.7 broadcast_maximum_fusion
  12.7 0.8 iota_compare_fusion
  13.5 0.7 broadcast_multiply_fusion
  14.3 1.7 %gather_fusion = s32[128]{0:T(128)S(1)} fusion(s32[512]{0:T(512)} %param.19, s32[1024]{0:T(1024)S(1)} %pad_clamp_fusion), kind=kCustom, calls=%fused_computation | custom fusion | bytes 1536 | tf_op jit(solution)/shard_map/gather | solution.py:102
  15.9 0.1 reduce_sum.65
  16.0 0.1 fusion.30
  16.2 1.8 %all-to-all-done = bf16[32,16,128]{2,1,0:T(8,128)(2,1)S(1)} async-done(((bf16[32,16,128]{2,1,0:T(8,128)(2,1)}), bf16[32,16,128]{2,1,0:T(8,128)(2,1)S(1)}, u32[]{:S(2)}, u32[]{:S(2)}) %all-to-all-start) | async-done | bytes 131104 | tf_op jit(solution)/shard_map/all_to_all | solution.py:34
  18.0 0.7 gather_fusion.1
  18.7 4.5 %select_reduce_fusion.1 = (f32[128,2]{1,0:T(8,128)S(1)}, f32[128,2,128]{2,1,0:T(2,128)S(1)}) fusion(pred[128,128]{1,0:T(8,128)(4,1)S(1)} %fusion.30, bf16[2,128,128,128]{3,2,1,0:T(8,128)(2,1)} %param.18, pred[128,2]{0,1:T(4,128)(4,1)S(1)} %iota_compare_fusion.2, bf16[128,128]{1,0:T(8,128)(2,1)S(1)} %gather_fusion.1), kind=kOutput, calls=%fused_computation.28 | convolution fusion | flops 8519424 | bytes 4375808 | tf_op jit(solution)/shard_map/ptc,pch->pth/dot_general | solution.py:98
  23.3 0.2 select_reduce_fusion
  23.5 0.1 copy.50
  23.7 0.6 gather_fusion.2
  24.4 0.4 bitcast_reduce_fusion
  24.8 3.5 %fusion.14 = f32[128,128]{1,0:T(8,128)S(1)} fusion(bf16[2,128,128,128]{3,2,1,0:T(8,128)(2,1)} %param.18, pred[2,128]{1,0:T(4,128)(4,1)S(1)} %iota_compare_fusion.3, f32[128,2,128]{2,1,0:T(2,128)S(1)} %get-tuple-element.10, pred[128,128]{1,0:T(8,128)(4,1)S(1)} %fusion.30, f32[128,2]{1,0:T(8,128)S(1)} %get-tuple-element.9), kind=kOutput, calls=%fused_computation.13 | convolution fusion | flops 8536064 | bytes 4408576 | tf_op jit(solution)/shard_map/pth,ptc->phc/dot_general | solution.py:106
  28.4 0.1 fusion.57
  28.6 0.1 copy.52
  28.7 0.5 fusion.18
  29.3 0.1 pad_maximum_fusion.1
  29.5 0.1 reshape.193
  29.7 14.2 %all_to_all.10 = f32[32,17,128]{2,1,0:T(8,128)S(1)} all-to-all(f32[32,17,128]{2,1,0:T(8,128)S(1)} %pad_maximum_fusion), channel_id=1, replica_groups=mesh['dp'=32,'mp'=8] {'dp'}, dimensions={0} | all-to-all | bytes 557056 | tf_op jit(solution)/shard_map/all_to_all | solution.py:147
  43.8 0.1 copy.59
  43.9 0.2 fusion.45
  44.3 0.2 copy.56
  44.5 0.6 broadcast_in_dim.143
  45.1 0.3 reshape.197
  45.5 1.1 %fusion.49 = f32[16,1024]{1,0:T(8,128)S(1)} fusion(bf16[128,1024]{1,0:T(8,128)(2,1)} %param.14, f32[16,128]{1,0:T(8,128)S(1)} %fusion.17, f32[16,128]{1,0:T(8,128)S(1)} %div.35), kind=kOutput, calls=%fused_computation.73 | convolution fusion | flops 4198400 | bytes 344064 | tf_op jit(solution)/shard_map/dot_general | solution.py:169
  46.6 1.9 %collective-permute-start = (f32[16,1024]{1,0:T(8,128)S(1)}, f32[16,1024]{1,0:T(8,128)S(1)}, u32[]{:S(2)}, u32[]{:S(2)}) collective-permute-start(f32[16,1024]{1,0:T(8,128)S(1)} %fusion.49), channel_id=1, source_target_pairs={{0,1},{1,0},{2,3},{3,2},{4,5},{5,4},{6,7},{7,6},{8,9},{9,8},{10,11... | collective-permute-start | bytes 196616 | tf_op jit(solution)/shard_map/ppermute | solution.py:26
  48.5 2.7 %collective-permute-done = f32[16,1024]{1,0:T(8,128)S(1)} collective-permute-done((f32[16,1024]{1,0:T(8,128)S(1)}, f32[16,1024]{1,0:T(8,128)S(1)}, u32[]{:S(2)}, u32[]{:S(2)}) %collective-permute-start) | collective-permute-done | bytes 65568 | tf_op jit(solution)/shard_map/ppermute | solution.py:26
  51.2 3.4 %collective-permute-start.1 = (f32[16,1024]{1,0:T(8,128)S(1)}, f32[16,1024]{1,0:T(8,128)S(1)}, u32[]{:S(2)}, u32[]{:S(2)}) collective-permute-start(f32[16,1024]{1,0:T(8,128)S(1)} %add.86), channel_id=1, source_target_pairs={{0,2},{1,3},{2,0},{3,1},{4,6},{5,7},{6,4},{7,5},{8,10},{9,11},{10,... | collective-permute-start | bytes 196616 | tf_op jit(solution)/shard_map/ppermute | solution.py:26
  54.6 3.6 %collective-permute-done.1 = f32[16,1024]{1,0:T(8,128)S(1)} collective-permute-done((f32[16,1024]{1,0:T(8,128)S(1)}, f32[16,1024]{1,0:T(8,128)S(1)}, u32[]{:S(2)}, u32[]{:S(2)}) %collective-permute-start.1) | collective-permute-done | bytes 65568 | tf_op jit(solution)/shard_map/ppermute | solution.py:26
  58.2 6.1 %collective-permute-start.2 = (f32[16,1024]{1,0:T(8,128)S(1)}, f32[16,1024]{1,0:T(8,128)S(1)}, u32[]{:S(2)}, u32[]{:S(2)}) collective-permute-start(f32[16,1024]{1,0:T(8,128)S(1)} %add.87), channel_id=1, source_target_pairs={{0,4},{1,5},{2,6},{3,7},{4,0},{5,1},{6,2},{7,3},{8,12},{9,13},{10,... | collective-permute-start | bytes 196616 | tf_op jit(solution)/shard_map/ppermute | solution.py:26
  64.3 2.2 %collective-permute-done.2 = f32[16,1024]{1,0:T(8,128)S(1)} collective-permute-done((f32[16,1024]{1,0:T(8,128)S(1)}, f32[16,1024]{1,0:T(8,128)S(1)}, u32[]{:S(2)}, u32[]{:S(2)}) %collective-permute-start.2) | collective-permute-done | bytes 65568 | tf_op jit(solution)/shard_map/ppermute | solution.py:26
  66.6 0.1 fusion.26
  66.8 0.4 fusion.6
  67.2 1.5 %fusion.43 = f32[16,1024]{1,0:T(8,128)S(1)} fusion(bf16[512,1024]{1,0:T(8,128)(2,1)} %param.17, f32[16,2,512]{2,0,1:T(8,128)S(1)} %fusion.6), kind=kOutput, calls=%fused_computation.59 | convolution fusion | flops 16826368 | bytes 1179648 | tf_op jit(solution)/shard_map/dot_general | solution.py:177
  68.7 0.5 collective-permute-start.3
  69.2 3.7 %collective-permute-done.3 = f32[16,1024]{1,0:T(8,128)S(1)} collective-permute-done((f32[16,1024]{1,0:T(8,128)S(1)}, f32[16,1024]{1,0:T(8,128)S(1)}, u32[]{:S(2)}, u32[]{:S(2)}) %collective-permute-start.3) | collective-permute-done | bytes 65568 | tf_op jit(solution)/shard_map/ppermute | solution.py:26
  72.9 2.9 %collective-permute-start.4 = (f32[16,1024]{1,0:T(8,128)S(1)}, f32[16,1024]{1,0:T(8,128)S(1)}, u32[]{:S(2)}, u32[]{:S(2)}) collective-permute-start(f32[16,1024]{1,0:T(8,128)S(1)} %add.92), channel_id=1, source_target_pairs={{0,2},{1,3},{2,0},{3,1},{4,6},{5,7},{6,4},{7,5},{8,10},{9,11},{10,... | collective-permute-start | bytes 196616 | tf_op jit(solution)/shard_map/ppermute | solution.py:26
  75.9 2.3 %collective-permute-done.4 = f32[16,1024]{1,0:T(8,128)S(1)} collective-permute-done((f32[16,1024]{1,0:T(8,128)S(1)}, f32[16,1024]{1,0:T(8,128)S(1)}, u32[]{:S(2)}, u32[]{:S(2)}) %collective-permute-start.4) | collective-permute-done | bytes 65568 | tf_op jit(solution)/shard_map/ppermute | solution.py:26
  78.2 7.4 %collective-permute-start.5 = (f32[16,1024]{1,0:T(8,128)S(1)}, f32[16,1024]{1,0:T(8,128)S(1)}, u32[]{:S(2)}, u32[]{:S(2)}) collective-permute-start(f32[16,1024]{1,0:T(8,128)S(1)} %add.93), channel_id=1, source_target_pairs={{0,4},{1,5},{2,6},{3,7},{4,0},{5,1},{6,2},{7,3},{8,12},{9,13},{10,... | collective-permute-start | bytes 196616 | tf_op jit(solution)/shard_map/ppermute | solution.py:26
  85.6 0.6 pad_maximum_fusion.2
  86.2 1.6 %collective-permute-done.5 = f32[16,1024]{1,0:T(8,128)S(1)} collective-permute-done((f32[16,1024]{1,0:T(8,128)S(1)}, f32[16,1024]{1,0:T(8,128)S(1)}, u32[]{:S(2)}, u32[]{:S(2)}) %collective-permute-start.5) | collective-permute-done | bytes 65568 | tf_op jit(solution)/shard_map/ppermute | solution.py:26
  87.9 0.6 fusion.29
  (43 shorter events, 0.9 us)
Async XLA Ops:
  0.6 66.1 %copy-start = (bf16[1024,2,512]{2,1,0:T(2,128)(2,1)S(1)}, bf16[1024,2,512]{2,1,0:T(2,128)(2,1)}, u32[]{:S(2)}) copy-start(bf16[1024,2,512]{2,1,0:T(2,128)(2,1)} %param.16) | copy-start | bytes 6291460
  3.8 14.2 %all-to-all-start = ((bf16[32,16,128]{2,1,0:T(8,128)(2,1)}), bf16[32,16,128]{2,1,0:T(8,128)(2,1)S(1)}, u32[]{:S(2)}, u32[]{:S(2)}) async-start(bf16[32,16,128]{2,1,0:T(8,128)(2,1)} %broadcast_in_dim.131), calls=%async_computation | async-start | bytes 262144 | tf_op jit(solution)/shard_map/all_to_all | solution.py:34
  23.3 5.5 %copy-start.3 = (s32[128]{0:T(128)S(1)}, s32[128]{0:T(128)}, u32[]{:S(2)}) copy-start(s32[128]{0:T(128)} %param.20) | copy-start | bytes 1540
  28.5 38.1 %copy-start.1 = (bf16[16,1024]{1,0:T(8,128)(2,1)S(1)}, bf16[16,1024]{1,0:T(8,128)(2,1)}, u32[]{:S(2)}) copy-start(bf16[16,1024]{1,0:T(8,128)(2,1)} %param.11) | copy-start | bytes 98308
  28.6 38.2 %copy-start.2 = (f32[1024]{0:T(1024)S(1)}, f32[1024]{0:T(1024)}, u32[]{:S(2)}) copy-start(f32[1024]{0:T(1024)} %param.15) | copy-start | bytes 12292
  46.6 4.6 %collective-permute-start = (f32[16,1024]{1,0:T(8,128)S(1)}, f32[16,1024]{1,0:T(8,128)S(1)}, u32[]{:S(2)}, u32[]{:S(2)}) collective-permute-start(f32[16,1024]{1,0:T(8,128)S(1)} %fusion.49), channel_id=1, source_target_pairs={{0,1},{1,0},{2,3},{3,2},{4,5},{5,4},{6,7},{7,6},{8,9},{9,8},{10,11... | collective-permute-start | bytes 196616 | tf_op jit(solution)/shard_map/ppermute | solution.py:26
  51.2 7.0 %collective-permute-start.1 = (f32[16,1024]{1,0:T(8,128)S(1)}, f32[16,1024]{1,0:T(8,128)S(1)}, u32[]{:S(2)}, u32[]{:S(2)}) collective-permute-start(f32[16,1024]{1,0:T(8,128)S(1)} %add.86), channel_id=1, source_target_pairs={{0,2},{1,3},{2,0},{3,1},{4,6},{5,7},{6,4},{7,5},{8,10},{9,11},{10,... | collective-permute-start | bytes 196616 | tf_op jit(solution)/shard_map/ppermute | solution.py:26
  58.2 8.3 %collective-permute-start.2 = (f32[16,1024]{1,0:T(8,128)S(1)}, f32[16,1024]{1,0:T(8,128)S(1)}, u32[]{:S(2)}, u32[]{:S(2)}) collective-permute-start(f32[16,1024]{1,0:T(8,128)S(1)} %add.87), channel_id=1, source_target_pairs={{0,4},{1,5},{2,6},{3,7},{4,0},{5,1},{6,2},{7,3},{8,12},{9,13},{10,... | collective-permute-start | bytes 196616 | tf_op jit(solution)/shard_map/ppermute | solution.py:26
  68.7 4.3 %collective-permute-start.3 = (f32[16,1024]{1,0:T(8,128)S(1)}, f32[16,1024]{1,0:T(8,128)S(1)}, u32[]{:S(2)}, u32[]{:S(2)}) collective-permute-start(f32[16,1024]{1,0:T(8,128)S(1)} %fusion.43), channel_id=1, source_target_pairs={{0,1},{1,0},{2,3},{3,2},{4,5},{5,4},{6,7},{7,6},{8,9},{9,8},{10,11... | collective-permute-start | bytes 196616 | tf_op jit(solution)/shard_map/ppermute | solution.py:26
  72.9 5.3 %collective-permute-start.4 = (f32[16,1024]{1,0:T(8,128)S(1)}, f32[16,1024]{1,0:T(8,128)S(1)}, u32[]{:S(2)}, u32[]{:S(2)}) collective-permute-start(f32[16,1024]{1,0:T(8,128)S(1)} %add.92), channel_id=1, source_target_pairs={{0,2},{1,3},{2,0},{3,1},{4,6},{5,7},{6,4},{7,5},{8,10},{9,11},{10,... | collective-permute-start | bytes 196616 | tf_op jit(solution)/shard_map/ppermute | solution.py:26
  78.2 9.7 %collective-permute-start.5 = (f32[16,1024]{1,0:T(8,128)S(1)}, f32[16,1024]{1,0:T(8,128)S(1)}, u32[]{:S(2)}, u32[]{:S(2)}) collective-permute-start(f32[16,1024]{1,0:T(8,128)S(1)} %add.93), channel_id=1, source_target_pairs={{0,4},{1,5},{2,6},{3,7},{4,0},{5,1},{6,2},{7,3},{8,12},{9,13},{10,... | collective-permute-start | bytes 196616 | tf_op jit(solution)/shard_map/ppermute | solution.py:26

commit v8 on v7

--- a/solution.py
+++ b/solution.py
@@ -91,20 +91,20 @@
     chosen_queries = every_query[clamped]
     head_of_col = jnp.arange(head_cols, dtype=jnp.int32) // HEAD_DIM
     head_mask = head_of_col[:, None] == jnp.arange(local_heads, dtype=jnp.int32)[None, :]
-    query_blocks = jnp.where(head_mask[None], chosen_queries[:, :, None], jnp.zeros((), jnp.bfloat16))
+    query_blocks = jnp.where(head_mask.T[None], chosen_queries[:, None, :], jnp.zeros((), jnp.bfloat16))
     key_rows = kv_cache[0]
     value_rows = kv_cache[1]
     scores = (
-        jnp.einsum("ptc,pch->pth", key_rows, query_blocks, preferred_element_type=jnp.float32)
+        jnp.einsum("phc,ptc->pht", query_blocks, key_rows, preferred_element_type=jnp.float32)
         * score_scale
     )
     position = page_index[:, None] * page_len + offsets[None, :]
     usable = (owners[:, None] >= 0) & (position < lengths[clamped][:, None])
-    page_max = jnp.max(jnp.where(usable[:, :, None], scores, NEGATIVE), axis=1)
-    raw = jnp.where(usable[:, :, None], jnp.exp(scores - page_max[:, None, :]), 0.0)
-    page_total = jnp.sum(raw, axis=1)
+    page_max = jnp.max(jnp.where(usable[:, None, :], scores, NEGATIVE), axis=2)
+    raw = jnp.where(usable[:, None, :], jnp.exp(scores - page_max[:, :, None]), 0.0)
+    page_total = jnp.sum(raw, axis=2)
     head_sums = jnp.einsum(
-        "pth,ptc->phc", raw.astype(jnp.bfloat16), value_rows, preferred_element_type=jnp.float32
+        "pht,ptc->phc", raw.astype(jnp.bfloat16), value_rows, preferred_element_type=jnp.float32
     )
     page_sum = jnp.sum(jnp.where(head_mask.T[None], head_sums, 0.0), axis=1)
 

time: 89 us -> 88.9 us (level)
  no operation moved by 1% of the time
where the time goes in v8:
time: 88.9 us; the launch traced here: 88.5 us
  starting transfers between devices  29.9 us (34%)
  waiting for transfers between devices  18.2 us (20%)
  blocking collectives  14.1 us (16%)
  matrix products  13 us (15%)
  other arithmetic  6.5 us (7%)
  local copies, waits for them, and re-layouts  5.91 us (7%)
  between operations  0.94 us (1%)
    ppermute x6, starting transfers between devices, butterfly_sum(): value = value + lax.ppermute(value, axis, pairs)  22.2 us
    ppermute x6, waiting for transfers between devices, butterfly_sum(): value = value + lax.ppermute(value, axis, pairs)  16.3 us
    all_to_all x1, blocking collectives, body(): received = lax.all_to_all(packed, 'dp', 0, 0, tiled=True)  14.1 us
    all_to_all x1, starting transfers between devices, exchange_gather(): gathered = lax.all_to_all(spread, axis, 0, 0, tiled=True)  7.62 us
    dot_general x1, matrix products, body(): jnp.einsum('phc,ptc->pht', query_blocks, key_rows, preferred_element_type...  4.54 us
    dot_general x1, matrix products, body(): jnp.einsum('pht,ptc->phc', raw.astype(jnp.bfloat16), value_rows, preferre...  3.5 us
    all_to_all x1, waiting for transfers between devices, exchange_gather(): gathered = lax.all_to_all(spread, axis, 0, 0, tiled=True)  1.84 us
  transfers between devices with their start and end apart: 7, of which 7 were waited for; matrix products, arithmetic and copies ran while one was open for 6% of the time, Pallas kernels for 0%

profile of v8, /device:TPU:2, one launch (start us, length us, event | category | flops | bytes accessed | tf_op | source)
XLA Modules:
  0.0 88.5 jit_solution(12646211734926493174)
XLA Ops:
  0.6 1.0 %fusion.22 = f32[16]{0:T(128)S(1)} fusion(bf16[16,1024]{1,0:T(8,128)(2,1)} %param.11), kind=kLoop, calls=%fused_computation.34 | loop fusion | flops 49136 | bytes 32832 | tf_op jit(solution)/shard_map/reduce_sum | solution.py:15
  1.7 1.4 %convolution_convert_fusion = bf16[16,3,128]{2,0,1:T(8,128)(2,1)S(1)} fusion(bf16[1024,3,128]{2,0,1:T(8,128)(2,1)} %param.13, bf16[16,1024]{1,0:T(8,128)(2,1)} %param.11, f32[1024]{0:T(1024)} %param.12, f32[16]{0:T(128)S(1)} %add_rsqrt_fusion.1), kind=kOutput, calls=%fused_computation.14 | convolution fusion | flops 12654592 | bytes 835648 | tf_op jit(solution)/shard_map/rd,dkc->rkc/dot_general | solution.py:77
  3.1 0.7 broadcast_in_dim.130
  3.8 7.6 %all-to-all-start = ((bf16[32,16,128]{2,1,0:T(8,128)(2,1)}), bf16[32,16,128]{2,1,0:T(8,128)(2,1)S(1)}, u32[]{:S(2)}, u32[]{:S(2)}) async-start(bf16[32,16,128]{2,1,0:T(8,128)(2,1)} %broadcast_in_dim.130), calls=%async_computation | async-start | bytes 262144 | tf_op jit(solution)/shard_map/all_to_all | solution.py:34
  11.4 0.7 broadcast_compare_fusion
  12.1 0.7 and_select_fusion
  12.7 0.8 iota_compare_fusion
  13.5 0.7 broadcast_multiply_fusion
  14.3 1.7 %gather_fusion = s32[128]{0:T(128)S(1)} fusion(s32[512]{0:T(512)} %param.19, s32[1024]{0:T(1024)S(1)} %pad_clamp_fusion), kind=kCustom, calls=%fused_computation | custom fusion | bytes 1536 | tf_op jit(solution)/shard_map/gather | solution.py:102
  15.9 0.1 reduce_sum.65
  16.0 0.1 fusion.31
  16.2 1.8 %all-to-all-done = bf16[32,16,128]{2,1,0:T(8,128)(2,1)S(1)} async-done(((bf16[32,16,128]{2,1,0:T(8,128)(2,1)}), bf16[32,16,128]{2,1,0:T(8,128)(2,1)S(1)}, u32[]{:S(2)}, u32[]{:S(2)}) %all-to-all-start) | async-done | bytes 131104 | tf_op jit(solution)/shard_map/all_to_all | solution.py:34
  18.0 0.7 gather_fusion.1
  18.7 4.5 %select_reduce_fusion.1 = (f32[128,2]{1,0:T(8,128)S(1)}, f32[128,2,128]{2,1,0:T(2,128)S(1)}) fusion(pred[128,128]{1,0:T(8,128)(4,1)S(1)} %fusion.31, bf16[2,128,128,128]{3,2,1,0:T(8,128)(2,1)} %param.18, pred[2,128]{1,0:T(4,128)(4,1)S(1)} %iota_compare_fusion.2, bf16[128,128]{1,0:T(8,128)(2,1)S(1)} %gather_fusion.1), kind=kOutput, calls=%fused_computation.26 | convolution fusion | flops 8519424 | bytes 4375808 | tf_op jit(solution)/shard_map/phc,ptc->pht/dot_general | solution.py:98
  23.3 3.5 %fusion.14 = f32[128,128]{1,0:T(8,128)S(1)} fusion(bf16[2,128,128,128]{3,2,1,0:T(8,128)(2,1)} %param.18, pred[2,128]{1,0:T(4,128)(4,1)S(1)} %iota_compare_fusion.2, f32[128,2,128]{2,1,0:T(2,128)S(1)} %get-tuple-element.10, pred[128,128]{1,0:T(8,128)(4,1)S(1)} %fusion.31, f32[128,2]{1,0:T(8,128)S(1)} %get-tuple-element.9), kind=kOutput, calls=%fused_computation.13 | convolution fusion | flops 8536064 | bytes 4408576 | tf_op jit(solution)/shard_map/pht,ptc->phc/dot_general | solution.py:106
  26.8 0.4 fusion.58
  27.2 0.1 select_reduce_fusion
  27.4 0.1 copy.50
  27.6 0.6 gather_fusion.2
  28.4 0.1 fusion.59
  28.6 0.1 copy.52
  28.7 0.5 fusion.18
  29.3 0.1 pad_maximum_fusion.1
  29.4 0.1 reshape.163
  29.6 14.1 %all_to_all.10 = f32[32,17,128]{2,1,0:T(8,128)S(1)} all-to-all(f32[32,17,128]{2,1,0:T(8,128)S(1)} %pad_maximum_fusion), channel_id=1, replica_groups=mesh['dp'=32,'mp'=8] {'dp'}, dimensions={0} | all-to-all | bytes 557056 | tf_op jit(solution)/shard_map/all_to_all | solution.py:147
  43.8 0.1 copy.59
  43.9 0.2 fusion.46
  44.3 0.2 copy.56
  44.5 0.6 broadcast_in_dim.142
  45.1 0.3 reshape.167
  45.4 1.1 %fusion.50 = f32[16,1024]{1,0:T(8,128)S(1)} fusion(bf16[128,1024]{1,0:T(8,128)(2,1)} %param.14, f32[16,128]{1,0:T(8,128)S(1)} %fusion.17, f32[16,128]{1,0:T(8,128)S(1)} %div.35), kind=kOutput, calls=%fused_computation.72 | convolution fusion | flops 4198400 | bytes 344064 | tf_op jit(solution)/shard_map/dot_general | solution.py:169
  46.5 1.9 %collective-permute-start = (f32[16,1024]{1,0:T(8,128)S(1)}, f32[16,1024]{1,0:T(8,128)S(1)}, u32[]{:S(2)}, u32[]{:S(2)}) collective-permute-start(f32[16,1024]{1,0:T(8,128)S(1)} %fusion.50), channel_id=1, source_target_pairs={{0,1},{1,0},{2,3},{3,2},{4,5},{5,4},{6,7},{7,6},{8,9},{9,8},{10,11... | collective-permute-start | bytes 196616 | tf_op jit(solution)/shard_map/ppermute | solution.py:26
  48.5 2.7 %collective-permute-done = f32[16,1024]{1,0:T(8,128)S(1)} collective-permute-done((f32[16,1024]{1,0:T(8,128)S(1)}, f32[16,1024]{1,0:T(8,128)S(1)}, u32[]{:S(2)}, u32[]{:S(2)}) %collective-permute-start) | collective-permute-done | bytes 65568 | tf_op jit(solution)/shard_map/ppermute | solution.py:26
  51.2 3.4 %collective-permute-start.1 = (f32[16,1024]{1,0:T(8,128)S(1)}, f32[16,1024]{1,0:T(8,128)S(1)}, u32[]{:S(2)}, u32[]{:S(2)}) collective-permute-start(f32[16,1024]{1,0:T(8,128)S(1)} %add.86), channel_id=1, source_target_pairs={{0,2},{1,3},{2,0},{3,1},{4,6},{5,7},{6,4},{7,5},{8,10},{9,11},{10,... | collective-permute-start | bytes 196616 | tf_op jit(solution)/shard_map/ppermute | solution.py:26
  54.5 3.6 %collective-permute-done.1 = f32[16,1024]{1,0:T(8,128)S(1)} collective-permute-done((f32[16,1024]{1,0:T(8,128)S(1)}, f32[16,1024]{1,0:T(8,128)S(1)}, u32[]{:S(2)}, u32[]{:S(2)}) %collective-permute-start.1) | collective-permute-done | bytes 65568 | tf_op jit(solution)/shard_map/ppermute | solution.py:26
  58.2 6.1 %collective-permute-start.2 = (f32[16,1024]{1,0:T(8,128)S(1)}, f32[16,1024]{1,0:T(8,128)S(1)}, u32[]{:S(2)}, u32[]{:S(2)}) collective-permute-start(f32[16,1024]{1,0:T(8,128)S(1)} %add.87), channel_id=1, source_target_pairs={{0,4},{1,5},{2,6},{3,7},{4,0},{5,1},{6,2},{7,3},{8,12},{9,13},{10,... | collective-permute-start | bytes 196616 | tf_op jit(solution)/shard_map/ppermute | solution.py:26
  64.3 2.2 %collective-permute-done.2 = f32[16,1024]{1,0:T(8,128)S(1)} collective-permute-done((f32[16,1024]{1,0:T(8,128)S(1)}, f32[16,1024]{1,0:T(8,128)S(1)}, u32[]{:S(2)}, u32[]{:S(2)}) %collective-permute-start.2) | collective-permute-done | bytes 65568 | tf_op jit(solution)/shard_map/ppermute | solution.py:26
  66.6 0.1 fusion.26
  66.7 0.4 fusion.6
  67.2 1.5 %fusion.44 = f32[16,1024]{1,0:T(8,128)S(1)} fusion(bf16[512,1024]{1,0:T(8,128)(2,1)} %param.17, f32[16,2,512]{2,0,1:T(8,128)S(1)} %fusion.6), kind=kOutput, calls=%fused_computation.58 | convolution fusion | flops 16826368 | bytes 1179648 | tf_op jit(solution)/shard_map/dot_general | solution.py:177
  68.6 0.5 collective-permute-start.3
  69.2 3.7 %collective-permute-done.3 = f32[16,1024]{1,0:T(8,128)S(1)} collective-permute-done((f32[16,1024]{1,0:T(8,128)S(1)}, f32[16,1024]{1,0:T(8,128)S(1)}, u32[]{:S(2)}, u32[]{:S(2)}) %collective-permute-start.3) | collective-permute-done | bytes 65568 | tf_op jit(solution)/shard_map/ppermute | solution.py:26
  72.9 2.9 %collective-permute-start.4 = (f32[16,1024]{1,0:T(8,128)S(1)}, f32[16,1024]{1,0:T(8,128)S(1)}, u32[]{:S(2)}, u32[]{:S(2)}) collective-permute-start(f32[16,1024]{1,0:T(8,128)S(1)} %add.92), channel_id=1, source_target_pairs={{0,2},{1,3},{2,0},{3,1},{4,6},{5,7},{6,4},{7,5},{8,10},{9,11},{10,... | collective-permute-start | bytes 196616 | tf_op jit(solution)/shard_map/ppermute | solution.py:26
  75.8 2.3 %collective-permute-done.4 = f32[16,1024]{1,0:T(8,128)S(1)} collective-permute-done((f32[16,1024]{1,0:T(8,128)S(1)}, f32[16,1024]{1,0:T(8,128)S(1)}, u32[]{:S(2)}, u32[]{:S(2)}) %collective-permute-start.4) | collective-permute-done | bytes 65568 | tf_op jit(solution)/shard_map/ppermute | solution.py:26
  78.2 7.4 %collective-permute-start.5 = (f32[16,1024]{1,0:T(8,128)S(1)}, f32[16,1024]{1,0:T(8,128)S(1)}, u32[]{:S(2)}, u32[]{:S(2)}) collective-permute-start(f32[16,1024]{1,0:T(8,128)S(1)} %add.93), channel_id=1, source_target_pairs={{0,4},{1,5},{2,6},{3,7},{4,0},{5,1},{6,2},{7,3},{8,12},{9,13},{10,... | collective-permute-start | bytes 196616 | tf_op jit(solution)/shard_map/ppermute | solution.py:26
  85.6 0.6 pad_maximum_fusion.2
  86.2 1.6 %collective-permute-done.5 = f32[16,1024]{1,0:T(8,128)S(1)} collective-permute-done((f32[16,1024]{1,0:T(8,128)S(1)}, f32[16,1024]{1,0:T(8,128)S(1)}, u32[]{:S(2)}, u32[]{:S(2)}) %collective-permute-start.5) | collective-permute-done | bytes 65568 | tf_op jit(solution)/shard_map/ppermute | solution.py:26
  87.8 0.6 fusion.29
  (41 shorter events, 0.9 us)
Async XLA Ops:
  0.6 66.1 %copy-start = (bf16[1024,2,512]{2,1,0:T(2,128)(2,1)S(1)}, bf16[1024,2,512]{2,1,0:T(2,128)(2,1)}, u32[]{:S(2)}) copy-start(bf16[1024,2,512]{2,1,0:T(2,128)(2,1)} %param.16) | copy-start | bytes 6291460
  3.8 14.2 %all-to-all-start = ((bf16[32,16,128]{2,1,0:T(8,128)(2,1)}), bf16[32,16,128]{2,1,0:T(8,128)(2,1)S(1)}, u32[]{:S(2)}, u32[]{:S(2)}) async-start(bf16[32,16,128]{2,1,0:T(8,128)(2,1)} %broadcast_in_dim.130), calls=%async_computation | async-start | bytes 262144 | tf_op jit(solution)/shard_map/all_to_all | solution.py:34
  23.3 5.4 %copy-start.3 = (s32[128]{0:T(128)S(1)}, s32[128]{0:T(128)}, u32[]{:S(2)}) copy-start(s32[128]{0:T(128)} %param.20) | copy-start | bytes 1540
  28.5 38.1 %copy-start.1 = (bf16[16,1024]{1,0:T(8,128)(2,1)S(1)}, bf16[16,1024]{1,0:T(8,128)(2,1)}, u32[]{:S(2)}) copy-start(bf16[16,1024]{1,0:T(8,128)(2,1)} %param.11) | copy-start | bytes 98308
  28.6 38.1 %copy-start.2 = (f32[1024]{0:T(1024)S(1)}, f32[1024]{0:T(1024)}, u32[]{:S(2)}) copy-start(f32[1024]{0:T(1024)} %param.15) | copy-start | bytes 12292
  46.5 4.6 %collective-permute-start = (f32[16,1024]{1,0:T(8,128)S(1)}, f32[16,1024]{1,0:T(8,128)S(1)}, u32[]{:S(2)}, u32[]{:S(2)}) collective-permute-start(f32[16,1024]{1,0:T(8,128)S(1)} %fusion.50), channel_id=1, source_target_pairs={{0,1},{1,0},{2,3},{3,2},{4,5},{5,4},{6,7},{7,6},{8,9},{9,8},{10,11... | collective-permute-start | bytes 196616 | tf_op jit(solution)/shard_map/ppermute | solution.py:26
  51.2 7.0 %collective-permute-start.1 = (f32[16,1024]{1,0:T(8,128)S(1)}, f32[16,1024]{1,0:T(8,128)S(1)}, u32[]{:S(2)}, u32[]{:S(2)}) collective-permute-start(f32[16,1024]{1,0:T(8,128)S(1)} %add.86), channel_id=1, source_target_pairs={{0,2},{1,3},{2,0},{3,1},{4,6},{5,7},{6,4},{7,5},{8,10},{9,11},{10,... | collective-permute-start | bytes 196616 | tf_op jit(solution)/shard_map/ppermute | solution.py:26
  58.2 8.3 %collective-permute-start.2 = (f32[16,1024]{1,0:T(8,128)S(1)}, f32[16,1024]{1,0:T(8,128)S(1)}, u32[]{:S(2)}, u32[]{:S(2)}) collective-permute-start(f32[16,1024]{1,0:T(8,128)S(1)} %add.87), channel_id=1, source_target_pairs={{0,4},{1,5},{2,6},{3,7},{4,0},{5,1},{6,2},{7,3},{8,12},{9,13},{10,... | collective-permute-start | bytes 196616 | tf_op jit(solution)/shard_map/ppermute | solution.py:26
  68.6 4.3 %collective-permute-start.3 = (f32[16,1024]{1,0:T(8,128)S(1)}, f32[16,1024]{1,0:T(8,128)S(1)}, u32[]{:S(2)}, u32[]{:S(2)}) collective-permute-start(f32[16,1024]{1,0:T(8,128)S(1)} %fusion.44), channel_id=1, source_target_pairs={{0,1},{1,0},{2,3},{3,2},{4,5},{5,4},{6,7},{7,6},{8,9},{9,8},{10,11... | collective-permute-start | bytes 196616 | tf_op jit(solution)/shard_map/ppermute | solution.py:26
  72.9 5.3 %collective-permute-start.4 = (f32[16,1024]{1,0:T(8,128)S(1)}, f32[16,1024]{1,0:T(8,128)S(1)}, u32[]{:S(2)}, u32[]{:S(2)}) collective-permute-start(f32[16,1024]{1,0:T(8,128)S(1)} %add.92), channel_id=1, source_target_pairs={{0,2},{1,3},{2,0},{3,1},{4,6},{5,7},{6,4},{7,5},{8,10},{9,11},{10,... | collective-permute-start | bytes 196616 | tf_op jit(solution)/shard_map/ppermute | solution.py:26
  78.2 9.7 %collective-permute-start.5 = (f32[16,1024]{1,0:T(8,128)S(1)}, f32[16,1024]{1,0:T(8,128)S(1)}, u32[]{:S(2)}, u32[]{:S(2)}) collective-permute-start(f32[16,1024]{1,0:T(8,128)S(1)} %add.93), channel_id=1, source_target_pairs={{0,4},{1,5},{2,6},{3,7},{4,0},{5,1},{6,2},{7,3},{8,12},{9,13},{10,... | collective-permute-start | bytes 196616 | tf_op jit(solution)/shard_map/ppermute | solution.py:26

commit v9 on v7

--- a/solution.py
+++ b/solution.py
@@ -23,6 +23,8 @@
     distance = 1
     while distance < size:
         pairs = [(j, j ^ distance) for j in range(size)]
+        if size == 8 and distance == 4:
+            pairs = [(0, 6), (6, 0), (1, 7), (7, 1), (2, 4), (4, 2), (3, 5), (5, 3)]
         value = value + lax.ppermute(value, axis, pairs)
         distance *= 2
     return value

time: 89 us -> 85.9 us (0.965)
  starting transfers between devices: 29.9 us -> 27.3 us
  waiting for transfers between devices: 18.2 us -> 16.8 us
    ppermute x6, starting transfers between devices: 22.2 us -> 19.7 us  [butterfly_sum(): value = value + lax.ppermute(value, axis, pairs)]
    ppermute x6, waiting for transfers between devices: 16.3 us -> 15 us  [butterfly_sum(): value = value + lax.ppermute(value, axis, pairs)]
where the time goes in v9:
time: 85.9 us; the launch traced here: 84.6 us
  starting transfers between devices  27.3 us (32%)
  waiting for transfers between devices  16.8 us (20%)
  blocking collectives  14.2 us (17%)
  matrix products  12.9 us (15%)
  other arithmetic  6.53 us (8%)
  local copies, waits for them, and re-layouts  5.91 us (7%)
  between operations  0.96 us (1%)
    ppermute x6, starting transfers between devices, butterfly_sum(): value = value + lax.ppermute(value, axis, pairs)  19.7 us
    ppermute x6, waiting for transfers between devices, butterfly_sum(): value = value + lax.ppermute(value, axis, pairs)  15 us
    all_to_all x1, blocking collectives, body(): received = lax.all_to_all(packed, 'dp', 0, 0, tiled=True)  14.2 us
    all_to_all x1, starting transfers between devices, exchange_gather(): gathered = lax.all_to_all(spread, axis, 0, 0, tiled=True)  7.62 us
    dot_general x1, matrix products, body(): jnp.einsum('ptc,pch->pth', key_rows, query_blocks, preferred_element_type...  4.54 us
    dot_general x1, matrix products, body(): jnp.einsum('pth,ptc->phc', raw.astype(jnp.bfloat16), value_rows, preferre...  3.49 us
    all_to_all x1, waiting for transfers between devices, exchange_gather(): gathered = lax.all_to_all(spread, axis, 0, 0, tiled=True)  1.82 us
  transfers between devices with their start and end apart: 7, of which 7 were waited for; matrix products, arithmetic and copies ran while one was open for 6% of the time, Pallas kernels for 0%

profile of v9, /device:TPU:2, one launch (start us, length us, event | category | flops | bytes accessed | tf_op | source)
XLA Modules:
  0.0 84.6 jit_solution(8253745740931593441)
XLA Ops:
  0.6 1.0 %fusion.22 = f32[16]{0:T(128)S(1)} fusion(bf16[16,1024]{1,0:T(8,128)(2,1)} %param.11), kind=kLoop, calls=%fused_computation.36 | loop fusion | flops 49136 | bytes 32832 | tf_op jit(solution)/shard_map/reduce_sum | solution.py:15
  1.7 1.4 %convolution_convert_fusion = bf16[16,3,128]{2,0,1:T(8,128)(2,1)S(1)} fusion(bf16[1024,3,128]{2,0,1:T(8,128)(2,1)} %param.13, bf16[16,1024]{1,0:T(8,128)(2,1)} %param.11, f32[1024]{0:T(1024)} %param.12, f32[16]{0:T(128)S(1)} %add_rsqrt_fusion.1), kind=kOutput, calls=%fused_computation.14 | convolution fusion | flops 12654592 | bytes 835648 | tf_op jit(solution)/shard_map/rd,dkc->rkc/dot_general | solution.py:79
  3.1 0.7 broadcast_in_dim.131
  3.8 7.6 %all-to-all-start = ((bf16[32,16,128]{2,1,0:T(8,128)(2,1)}), bf16[32,16,128]{2,1,0:T(8,128)(2,1)S(1)}, u32[]{:S(2)}, u32[]{:S(2)}) async-start(bf16[32,16,128]{2,1,0:T(8,128)(2,1)} %broadcast_in_dim.131), calls=%async_computation | async-start | bytes 262144 | tf_op jit(solution)/shard_map/all_to_all | solution.py:36
  11.4 0.7 broadcast_compare_fusion
  12.1 0.7 broadcast_maximum_fusion
  12.7 0.8 iota_compare_fusion
  13.5 0.7 broadcast_multiply_fusion
  14.3 1.7 %gather_fusion = s32[128]{0:T(128)S(1)} fusion(s32[512]{0:T(512)} %param.19, s32[1024]{0:T(1024)S(1)} %pad_clamp_fusion), kind=kCustom, calls=%fused_computation | custom fusion | bytes 1536 | tf_op jit(solution)/shard_map/gather | solution.py:104
  15.9 0.1 reduce_sum.65
  16.0 0.1 fusion.30
  16.2 1.8 %all-to-all-done = bf16[32,16,128]{2,1,0:T(8,128)(2,1)S(1)} async-done(((bf16[32,16,128]{2,1,0:T(8,128)(2,1)}), bf16[32,16,128]{2,1,0:T(8,128)(2,1)S(1)}, u32[]{:S(2)}, u32[]{:S(2)}) %all-to-all-start) | async-done | bytes 131104 | tf_op jit(solution)/shard_map/all_to_all | solution.py:36
  18.0 0.7 gather_fusion.1
  18.7 4.5 %select_reduce_fusion.1 = (f32[128,2]{1,0:T(8,128)S(1)}, f32[128,2,128]{2,1,0:T(2,128)S(1)}) fusion(pred[128,128]{1,0:T(8,128)(4,1)S(1)} %fusion.30, bf16[2,128,128,128]{3,2,1,0:T(8,128)(2,1)} %param.18, pred[128,2]{0,1:T(4,128)(4,1)S(1)} %iota_compare_fusion.2, bf16[128,128]{1,0:T(8,128)(2,1)S(1)} %gather_fusion.1), kind=kOutput, calls=%fused_computation.28 | convolution fusion | flops 8519424 | bytes 4375808 | tf_op jit(solution)/shard_map/ptc,pch->pth/dot_general | solution.py:100
  23.3 0.2 select_reduce_fusion
  23.5 0.1 copy.50
  23.7 0.6 gather_fusion.2
  24.4 0.4 bitcast_reduce_fusion
  24.8 3.5 %fusion.14 = f32[128,128]{1,0:T(8,128)S(1)} fusion(bf16[2,128,128,128]{3,2,1,0:T(8,128)(2,1)} %param.18, pred[2,128]{1,0:T(4,128)(4,1)S(1)} %iota_compare_fusion.3, f32[128,2,128]{2,1,0:T(2,128)S(1)} %get-tuple-element.10, pred[128,128]{1,0:T(8,128)(4,1)S(1)} %fusion.30, f32[128,2]{1,0:T(8,128)S(1)} %get-tuple-element.9), kind=kOutput, calls=%fused_computation.13 | convolution fusion | flops 8536064 | bytes 4408576 | tf_op jit(solution)/shard_map/pth,ptc->phc/dot_general | solution.py:108
  28.4 0.1 fusion.57
  28.6 0.1 copy.52
  28.7 0.5 fusion.18
  29.3 0.1 pad_maximum_fusion.1
  29.5 0.1 reshape.193
  29.7 14.2 %all_to_all.10 = f32[32,17,128]{2,1,0:T(8,128)S(1)} all-to-all(f32[32,17,128]{2,1,0:T(8,128)S(1)} %pad_maximum_fusion), channel_id=1, replica_groups=mesh['dp'=32,'mp'=8] {'dp'}, dimensions={0} | all-to-all | bytes 557056 | tf_op jit(solution)/shard_map/all_to_all | solution.py:149
  43.8 0.1 copy.59
  43.9 0.2 fusion.45
  44.3 0.2 copy.56
  44.5 0.6 broadcast_in_dim.143
  45.1 0.3 reshape.197
  45.5 1.1 %fusion.49 = f32[16,1024]{1,0:T(8,128)S(1)} fusion(bf16[128,1024]{1,0:T(8,128)(2,1)} %param.14, f32[16,128]{1,0:T(8,128)S(1)} %fusion.17, f32[16,128]{1,0:T(8,128)S(1)} %div.35), kind=kOutput, calls=%fused_computation.73 | convolution fusion | flops 4198400 | bytes 344064 | tf_op jit(solution)/shard_map/dot_general | solution.py:171
  46.6 1.9 %collective-permute-start = (f32[16,1024]{1,0:T(8,128)S(1)}, f32[16,1024]{1,0:T(8,128)S(1)}, u32[]{:S(2)}, u32[]{:S(2)}) collective-permute-start(f32[16,1024]{1,0:T(8,128)S(1)} %fusion.49), channel_id=1, source_target_pairs={{0,1},{1,0},{2,3},{3,2},{4,5},{5,4},{6,7},{7,6},{8,9},{9,8},{10,11... | collective-permute-start | bytes 196616 | tf_op jit(solution)/shard_map/ppermute | solution.py:28
  48.5 2.7 %collective-permute-done = f32[16,1024]{1,0:T(8,128)S(1)} collective-permute-done((f32[16,1024]{1,0:T(8,128)S(1)}, f32[16,1024]{1,0:T(8,128)S(1)}, u32[]{:S(2)}, u32[]{:S(2)}) %collective-permute-start) | collective-permute-done | bytes 65568 | tf_op jit(solution)/shard_map/ppermute | solution.py:28
  51.2 3.4 %collective-permute-start.1 = (f32[16,1024]{1,0:T(8,128)S(1)}, f32[16,1024]{1,0:T(8,128)S(1)}, u32[]{:S(2)}, u32[]{:S(2)}) collective-permute-start(f32[16,1024]{1,0:T(8,128)S(1)} %add.86), channel_id=1, source_target_pairs={{0,2},{1,3},{2,0},{3,1},{4,6},{5,7},{6,4},{7,5},{8,10},{9,11},{10,... | collective-permute-start | bytes 196616 | tf_op jit(solution)/shard_map/ppermute | solution.py:28
  54.6 3.6 %collective-permute-done.1 = f32[16,1024]{1,0:T(8,128)S(1)} collective-permute-done((f32[16,1024]{1,0:T(8,128)S(1)}, f32[16,1024]{1,0:T(8,128)S(1)}, u32[]{:S(2)}, u32[]{:S(2)}) %collective-permute-start.1) | collective-permute-done | bytes 65568 | tf_op jit(solution)/shard_map/ppermute | solution.py:28
  58.2 4.6 %collective-permute-start.2 = (f32[16,1024]{1,0:T(8,128)S(1)}, f32[16,1024]{1,0:T(8,128)S(1)}, u32[]{:S(2)}, u32[]{:S(2)}) collective-permute-start(f32[16,1024]{1,0:T(8,128)S(1)} %add.87), channel_id=1, source_target_pairs={{0,6},{6,0},{1,7},{7,1},{2,4},{4,2},{3,5},{5,3},{8,14},{14,8},{9,1... | collective-permute-start | bytes 196616 | tf_op jit(solution)/shard_map/ppermute | solution.py:28
  62.8 2.3 %collective-permute-done.2 = f32[16,1024]{1,0:T(8,128)S(1)} collective-permute-done((f32[16,1024]{1,0:T(8,128)S(1)}, f32[16,1024]{1,0:T(8,128)S(1)}, u32[]{:S(2)}, u32[]{:S(2)}) %collective-permute-start.2) | collective-permute-done | bytes 65568 | tf_op jit(solution)/shard_map/ppermute | solution.py:28
  65.1 0.1 fusion.26
  65.3 0.4 fusion.6
  65.7 1.5 %fusion.43 = f32[16,1024]{1,0:T(8,128)S(1)} fusion(bf16[512,1024]{1,0:T(8,128)(2,1)} %param.17, f32[16,2,512]{2,0,1:T(8,128)S(1)} %fusion.6), kind=kOutput, calls=%fused_computation.59 | convolution fusion | flops 16826368 | bytes 1179648 | tf_op jit(solution)/shard_map/dot_general | solution.py:179
  67.2 2.1 %collective-permute-start.3 = (f32[16,1024]{1,0:T(8,128)S(1)}, f32[16,1024]{1,0:T(8,128)S(1)}, u32[]{:S(2)}, u32[]{:S(2)}) collective-permute-start(f32[16,1024]{1,0:T(8,128)S(1)} %fusion.43), channel_id=1, source_target_pairs={{0,1},{1,0},{2,3},{3,2},{4,5},{5,4},{6,7},{7,6},{8,9},{9,8},{10,11... | collective-permute-start | bytes 196616 | tf_op jit(solution)/shard_map/ppermute | solution.py:28
  69.3 2.2 %collective-permute-done.3 = f32[16,1024]{1,0:T(8,128)S(1)} collective-permute-done((f32[16,1024]{1,0:T(8,128)S(1)}, f32[16,1024]{1,0:T(8,128)S(1)}, u32[]{:S(2)}, u32[]{:S(2)}) %collective-permute-start.3) | collective-permute-done | bytes 65568 | tf_op jit(solution)/shard_map/ppermute | solution.py:28
  71.5 3.6 %collective-permute-start.4 = (f32[16,1024]{1,0:T(8,128)S(1)}, f32[16,1024]{1,0:T(8,128)S(1)}, u32[]{:S(2)}, u32[]{:S(2)}) collective-permute-start(f32[16,1024]{1,0:T(8,128)S(1)} %add.92), channel_id=1, source_target_pairs={{0,2},{1,3},{2,0},{3,1},{4,6},{5,7},{6,4},{7,5},{8,10},{9,11},{10,... | collective-permute-start | bytes 196616 | tf_op jit(solution)/shard_map/ppermute | solution.py:28
  75.2 2.2 %collective-permute-done.4 = f32[16,1024]{1,0:T(8,128)S(1)} collective-permute-done((f32[16,1024]{1,0:T(8,128)S(1)}, f32[16,1024]{1,0:T(8,128)S(1)}, u32[]{:S(2)}, u32[]{:S(2)}) %collective-permute-start.4) | collective-permute-done | bytes 65568 | tf_op jit(solution)/shard_map/ppermute | solution.py:28
  77.4 4.0 %collective-permute-start.5 = (f32[16,1024]{1,0:T(8,128)S(1)}, f32[16,1024]{1,0:T(8,128)S(1)}, u32[]{:S(2)}, u32[]{:S(2)}) collective-permute-start(f32[16,1024]{1,0:T(8,128)S(1)} %add.93), channel_id=1, source_target_pairs={{0,6},{6,0},{1,7},{7,1},{2,4},{4,2},{3,5},{5,3},{8,14},{14,8},{9,1... | collective-permute-start | bytes 196616 | tf_op jit(solution)/shard_map/ppermute | solution.py:28
  81.5 0.6 pad_maximum_fusion.2
  82.1 1.9 %collective-permute-done.5 = f32[16,1024]{1,0:T(8,128)S(1)} collective-permute-done((f32[16,1024]{1,0:T(8,128)S(1)}, f32[16,1024]{1,0:T(8,128)S(1)}, u32[]{:S(2)}, u32[]{:S(2)}) %collective-permute-start.5) | collective-permute-done | bytes 65568 | tf_op jit(solution)/shard_map/ppermute | solution.py:28
  84.0 0.6 fusion.29
  (43 shorter events, 0.9 us)
Async XLA Ops:
  0.6 64.6 %copy-start = (bf16[1024,2,512]{2,1,0:T(2,128)(2,1)S(1)}, bf16[1024,2,512]{2,1,0:T(2,128)(2,1)}, u32[]{:S(2)}) copy-start(bf16[1024,2,512]{2,1,0:T(2,128)(2,1)} %param.16) | copy-start | bytes 6291460
  3.8 14.2 %all-to-all-start = ((bf16[32,16,128]{2,1,0:T(8,128)(2,1)}), bf16[32,16,128]{2,1,0:T(8,128)(2,1)S(1)}, u32[]{:S(2)}, u32[]{:S(2)}) async-start(bf16[32,16,128]{2,1,0:T(8,128)(2,1)} %broadcast_in_dim.131), calls=%async_computation | async-start | bytes 262144 | tf_op jit(solution)/shard_map/all_to_all | solution.py:36
  23.3 5.5 %copy-start.3 = (s32[128]{0:T(128)S(1)}, s32[128]{0:T(128)}, u32[]{:S(2)}) copy-start(s32[128]{0:T(128)} %param.20) | copy-start | bytes 1540
  28.5 36.6 %copy-start.1 = (bf16[16,1024]{1,0:T(8,128)(2,1)S(1)}, bf16[16,1024]{1,0:T(8,128)(2,1)}, u32[]{:S(2)}) copy-start(bf16[16,1024]{1,0:T(8,128)(2,1)} %param.11) | copy-start | bytes 98308
  28.6 36.7 %copy-start.2 = (f32[1024]{0:T(1024)S(1)}, f32[1024]{0:T(1024)}, u32[]{:S(2)}) copy-start(f32[1024]{0:T(1024)} %param.15) | copy-start | bytes 12292
  46.6 4.6 %collective-permute-start = (f32[16,1024]{1,0:T(8,128)S(1)}, f32[16,1024]{1,0:T(8,128)S(1)}, u32[]{:S(2)}, u32[]{:S(2)}) collective-permute-start(f32[16,1024]{1,0:T(8,128)S(1)} %fusion.49), channel_id=1, source_target_pairs={{0,1},{1,0},{2,3},{3,2},{4,5},{5,4},{6,7},{7,6},{8,9},{9,8},{10,11... | collective-permute-start | bytes 196616 | tf_op jit(solution)/shard_map/ppermute | solution.py:28
  51.2 7.0 %collective-permute-start.1 = (f32[16,1024]{1,0:T(8,128)S(1)}, f32[16,1024]{1,0:T(8,128)S(1)}, u32[]{:S(2)}, u32[]{:S(2)}) collective-permute-start(f32[16,1024]{1,0:T(8,128)S(1)} %add.86), channel_id=1, source_target_pairs={{0,2},{1,3},{2,0},{3,1},{4,6},{5,7},{6,4},{7,5},{8,10},{9,11},{10,... | collective-permute-start | bytes 196616 | tf_op jit(solution)/shard_map/ppermute | solution.py:28
  58.2 6.8 %collective-permute-start.2 = (f32[16,1024]{1,0:T(8,128)S(1)}, f32[16,1024]{1,0:T(8,128)S(1)}, u32[]{:S(2)}, u32[]{:S(2)}) collective-permute-start(f32[16,1024]{1,0:T(8,128)S(1)} %add.87), channel_id=1, source_target_pairs={{0,6},{6,0},{1,7},{7,1},{2,4},{4,2},{3,5},{5,3},{8,14},{14,8},{9,1... | collective-permute-start | bytes 196616 | tf_op jit(solution)/shard_map/ppermute | solution.py:28
  67.2 4.4 %collective-permute-start.3 = (f32[16,1024]{1,0:T(8,128)S(1)}, f32[16,1024]{1,0:T(8,128)S(1)}, u32[]{:S(2)}, u32[]{:S(2)}) collective-permute-start(f32[16,1024]{1,0:T(8,128)S(1)} %fusion.43), channel_id=1, source_target_pairs={{0,1},{1,0},{2,3},{3,2},{4,5},{5,4},{6,7},{7,6},{8,9},{9,8},{10,11... | collective-permute-start | bytes 196616 | tf_op jit(solution)/shard_map/ppermute | solution.py:28
  71.5 5.9 %collective-permute-start.4 = (f32[16,1024]{1,0:T(8,128)S(1)}, f32[16,1024]{1,0:T(8,128)S(1)}, u32[]{:S(2)}, u32[]{:S(2)}) collective-permute-start(f32[16,1024]{1,0:T(8,128)S(1)} %add.92), channel_id=1, source_target_pairs={{0,2},{1,3},{2,0},{3,1},{4,6},{5,7},{6,4},{7,5},{8,10},{9,11},{10,... | collective-permute-start | bytes 196616 | tf_op jit(solution)/shard_map/ppermute | solution.py:28
  77.4 6.5 %collective-permute-start.5 = (f32[16,1024]{1,0:T(8,128)S(1)}, f32[16,1024]{1,0:T(8,128)S(1)}, u32[]{:S(2)}, u32[]{:S(2)}) collective-permute-start(f32[16,1024]{1,0:T(8,128)S(1)} %add.93), channel_id=1, source_target_pairs={{0,6},{6,0},{1,7},{7,1},{2,4},{4,2},{3,5},{5,3},{8,14},{14,8},{9,1... | collective-permute-start | bytes 196616 | tf_op jit(solution)/shard_map/ppermute | solution.py:28

commit v10 on v9

--- a/solution.py
+++ b/solution.py
@@ -76,10 +76,17 @@
     requests = local_rows * data_devices
     score_scale = HEAD_DIM ** (-0.5)
     normed = rms_norm(hidden, attn_gain)
-    projected = jnp.einsum("rd,dkc->rkc", normed, w_qkv, preferred_element_type=jnp.float32)
-    projected = lax.optimization_barrier(projected.astype(jnp.bfloat16))
+    query_part = jnp.einsum(
+        "rd,dc->rc", normed, w_qkv[:, 0, :], preferred_element_type=jnp.float32
+    ).astype(jnp.bfloat16)
+    every_query = exchange_gather(query_part, "dp")
+    key_value_part = jnp.einsum(
+        "rd,dkc->rkc", normed, w_qkv[:, 1:, :], preferred_element_type=jnp.float32
+    ).astype(jnp.bfloat16)
+    projected = lax.optimization_barrier(
+        jnp.concatenate([query_part[:, None, :], key_value_part], axis=1)
+    )
     appended = jnp.stack([projected[:, 1], projected[:, 2]])
-    every_query = exchange_gather(projected[:, 0], "dp")
     own_queries = projected[:, 0].reshape(local_rows, local_heads, HEAD_DIM).astype(jnp.float32)
     own_keys = projected[:, 1].reshape(local_rows, local_heads, HEAD_DIM).astype(jnp.float32)
     own_values = projected[:, 2].reshape(local_rows, local_heads, HEAD_DIM).astype(jnp.float32)

time: 85.9 us -> 88.1 us (1.026)
  blocking collectives: 14.2 us -> 15.5 us
  waiting for transfers between devices: 16.8 us -> 15.5 us
    all_to_all x1, blocking collectives: 14.2 us -> 15.5 us  [body(): received = lax.all_to_all(packed, 'dp', 0, 0, tiled=True)]
    all_to_all x1, waiting for transfers between devices: 1.82 us -> 0.5 us  [exchange_gather(): gathered = lax.all_to_all(spread, axis, 0, 0, tiled=True)]
    dot_general x1 -> x2, matrix products: 1.42 us -> 2.48 us  [the longest x1 1.29 us: body(): jnp.einsum('rd,dkc->rkc', normed, w_qkv[:, 1:, :], preferred_element_type...]
  transfers between devices with their start and end apart: 7 -> 7, of which waited for: 7 -> 7; matrix products, arithmetic and copies ran while one was open for 6% -> 8% of each run, Pallas kernels for 0% -> 0%
where the time goes in v10:
time: 88.1 us; the launch traced here: 86.7 us
  starting transfers between devices  27.3 us (31%)
  waiting for transfers between devices  15.5 us (18%)
  blocking collectives  15.5 us (18%)
  matrix products  13.7 us (16%)
  other arithmetic  7.3 us (8%)
  local copies, waits for them, and re-layouts  6.5 us (7%)
  between operations  0.96 us (1%)
    ppermute x6, starting transfers between devices, butterfly_sum(): value = value + lax.ppermute(value, axis, pairs)  19.7 us
    all_to_all x1, blocking collectives, body(): received = lax.all_to_all(packed, 'dp', 0, 0, tiled=True)  15.5 us
    ppermute x6, waiting for transfers between devices, butterfly_sum(): value = value + lax.ppermute(value, axis, pairs)  15 us
    all_to_all x1, starting transfers between devices, exchange_gather(): gathered = lax.all_to_all(spread, axis, 0, 0, tiled=True)  7.62 us
    dot_general x1, matrix products, body(): jnp.einsum('ptc,pch->pth', key_rows, query_blocks, preferred_element_type...  4.54 us
    dot_general x1, matrix products, body(): jnp.einsum('pth,ptc->phc', raw.astype(jnp.bfloat16), value_rows, preferre...  3.48 us
  transfers between devices with their start and end apart: 7, of which 7 were waited for; matrix products, arithmetic and copies ran while one was open for 8% of the time, Pallas kernels for 0%

profile of v10, /device:TPU:2, one launch (start us, length us, event | category | flops | bytes accessed | tf_op | source)
XLA Modules:
  0.0 86.7 jit_solution(4060793810596684830)
XLA Ops:
  0.6 1.0 %fusion.25 = f32[16]{0:T(128)S(1)} fusion(bf16[16,1024]{1,0:T(8,128)(2,1)} %param.11), kind=kLoop, calls=%fused_computation.40 | loop fusion | flops 49136 | bytes 32832 | tf_op jit(solution)/shard_map/reduce_sum | solution.py:15
  1.7 1.2 %convolution_convert_fusion.1 = bf16[16,128]{1,0:T(8,128)(2,1)S(1)} fusion(bf16[1024,3,128]{2,0,1:T(8,128)(2,1)} %param.13, bf16[16,1024]{1,0:T(8,128)(2,1)} %param.11, f32[1024]{0:T(1024)} %param.12, f32[16]{0:T(128)S(1)} %add_rsqrt_fusion.1), kind=kOutput, calls=%fused_computation.15 | convolution fusion | flops 4261888 | bytes 303168 | tf_op jit(solution)/shard_map/rd,dc->rc/dot_general | solution.py:79
  2.9 0.7 broadcast_in_dim.133
  3.5 7.6 %all-to-all-start = ((bf16[32,16,128]{2,1,0:T(8,128)(2,1)}), bf16[32,16,128]{2,1,0:T(8,128)(2,1)S(1)}, u32[]{:S(2)}, u32[]{:S(2)}) async-start(bf16[32,16,128]{2,1,0:T(8,128)(2,1)} %broadcast_in_dim.133), calls=%async_computation | async-start | bytes 262144 | tf_op jit(solution)/shard_map/all_to_all | solution.py:36
  11.2 0.7 broadcast_compare_fusion
  11.8 0.7 broadcast_maximum_fusion
  12.5 1.3 %convolution_convert_fusion = bf16[16,2,128]{2,0,1:T(8,128)(2,1)S(1)} fusion(bf16[1024,3,128]{2,0,1:T(8,128)(2,1)} %param.13, bf16[16,1024]{1,0:T(8,128)(2,1)} %param.11, f32[1024]{0:T(1024)} %param.12, f32[16]{0:T(128)S(1)} %add_rsqrt_fusion.1), kind=kOutput, calls=%fused_computation.14 | convolution fusion | flops 8458240 | bytes 569408 | tf_op jit(solution)/shard_map/rd,dkc->rkc/dot_general | solution.py:83
  13.8 0.8 iota_compare_fusion
  14.6 0.7 broadcast_multiply_fusion
  15.4 1.6 %gather_fusion = s32[128]{0:T(128)S(1)} fusion(s32[512]{0:T(512)} %param.19, s32[1024]{0:T(1024)S(1)} %pad_clamp_fusion), kind=kCustom, calls=%fused_computation | custom fusion | bytes 1536 | tf_op jit(solution)/shard_map/gather | solution.py:111
  17.1 0.1 fusion.33
  17.3 0.5 all-to-all-done
  17.8 0.7 gather_fusion.1
  18.5 4.5 %select_reduce_fusion.1 = (f32[128,2]{1,0:T(8,128)S(1)}, f32[128,2,128]{2,1,0:T(2,128)S(1)}) fusion(pred[128,128]{1,0:T(8,128)(4,1)S(1)} %fusion.33, bf16[2,128,128,128]{3,2,1,0:T(8,128)(2,1)} %param.18, pred[128,2]{0,1:T(4,128)(4,1)S(1)} %iota_compare_fusion.2, bf16[128,128]{1,0:T(8,128)(2,1)S(1)} %gather_fusion.1), kind=kOutput, calls=%fused_computation.32 | convolution fusion | flops 8519424 | bytes 4375808 | tf_op jit(solution)/shard_map/ptc,pch->pth/dot_general | solution.py:107
  23.1 0.2 select_reduce_fusion
  23.3 0.1 copy.50
  23.5 0.6 gather_fusion.2
  24.1 0.4 bitcast_reduce_fusion
  24.5 3.5 %fusion.14 = f32[128,128]{1,0:T(8,128)S(1)} fusion(bf16[2,128,128,128]{3,2,1,0:T(8,128)(2,1)} %param.18, pred[2,128]{1,0:T(4,128)(4,1)S(1)} %iota_compare_fusion.3, f32[128,2,128]{2,1,0:T(2,128)S(1)} %get-tuple-element.9, pred[128,128]{1,0:T(8,128)(4,1)S(1)} %fusion.33, f32[128,2]{1,0:T(8,128)S(1)} %get-tuple-element.8), kind=kOutput, calls=%fused_computation.13 | convolution fusion | flops 8536064 | bytes 4408576 | tf_op jit(solution)/shard_map/pth,ptc->phc/dot_general | solution.py:115
  28.5 0.5 fusion.21
  29.1 0.1 pad_maximum_fusion.1
  29.2 0.1 reshape.193
  29.4 15.5 %all_to_all.10 = f32[32,17,128]{2,1,0:T(8,128)S(1)} all-to-all(f32[32,17,128]{2,1,0:T(8,128)S(1)} %pad_maximum_fusion), channel_id=1, replica_groups=mesh['dp'=32,'mp'=8] {'dp'}, dimensions={0} | all-to-all | bytes 557056 | tf_op jit(solution)/shard_map/all_to_all | solution.py:156
  44.9 0.1 copy.59
  45.0 0.2 fusion.45
  45.3 0.7 div.35
  45.9 0.2 copy.56
  46.2 0.6 broadcast_in_dim.145
  46.8 0.3 reshape.197
  47.1 0.8 fusion.51
  48.0 1.9 %collective-permute-start = (f32[16,1024]{1,0:T(8,128)S(1)}, f32[16,1024]{1,0:T(8,128)S(1)}, u32[]{:S(2)}, u32[]{:S(2)}) collective-permute-start(f32[16,1024]{1,0:T(8,128)S(1)} %fusion.51), channel_id=1, source_target_pairs={{0,1},{1,0},{2,3},{3,2},{4,5},{5,4},{6,7},{7,6},{8,9},{9,8},{10,11... | collective-permute-start | bytes 196616 | tf_op jit(solution)/shard_map/ppermute | solution.py:28
  49.9 2.7 %collective-permute-done = f32[16,1024]{1,0:T(8,128)S(1)} collective-permute-done((f32[16,1024]{1,0:T(8,128)S(1)}, f32[16,1024]{1,0:T(8,128)S(1)}, u32[]{:S(2)}, u32[]{:S(2)}) %collective-permute-start) | collective-permute-done | bytes 65568 | tf_op jit(solution)/shard_map/ppermute | solution.py:28
  52.6 3.4 %collective-permute-start.1 = (f32[16,1024]{1,0:T(8,128)S(1)}, f32[16,1024]{1,0:T(8,128)S(1)}, u32[]{:S(2)}, u32[]{:S(2)}) collective-permute-start(f32[16,1024]{1,0:T(8,128)S(1)} %add.86), channel_id=1, source_target_pairs={{0,2},{1,3},{2,0},{3,1},{4,6},{5,7},{6,4},{7,5},{8,10},{9,11},{10,... | collective-permute-start | bytes 196616 | tf_op jit(solution)/shard_map/ppermute | solution.py:28
  56.0 3.6 %collective-permute-done.1 = f32[16,1024]{1,0:T(8,128)S(1)} collective-permute-done((f32[16,1024]{1,0:T(8,128)S(1)}, f32[16,1024]{1,0:T(8,128)S(1)}, u32[]{:S(2)}, u32[]{:S(2)}) %collective-permute-start.1) | collective-permute-done | bytes 65568 | tf_op jit(solution)/shard_map/ppermute | solution.py:28
  59.6 4.6 %collective-permute-start.2 = (f32[16,1024]{1,0:T(8,128)S(1)}, f32[16,1024]{1,0:T(8,128)S(1)}, u32[]{:S(2)}, u32[]{:S(2)}) collective-permute-start(f32[16,1024]{1,0:T(8,128)S(1)} %add.87), channel_id=1, source_target_pairs={{0,6},{6,0},{1,7},{7,1},{2,4},{4,2},{3,5},{5,3},{8,14},{14,8},{9,1... | collective-permute-start | bytes 196616 | tf_op jit(solution)/shard_map/ppermute | solution.py:28
  64.2 2.3 %collective-permute-done.2 = f32[16,1024]{1,0:T(8,128)S(1)} collective-permute-done((f32[16,1024]{1,0:T(8,128)S(1)}, f32[16,1024]{1,0:T(8,128)S(1)}, u32[]{:S(2)}, u32[]{:S(2)}) %collective-permute-start.2) | collective-permute-done | bytes 65568 | tf_op jit(solution)/shard_map/ppermute | solution.py:28
  66.5 0.8 fusion.28
  67.3 0.1 fusion.29
  67.4 0.4 fusion.6
  67.8 1.5 %fusion.43 = f32[16,1024]{1,0:T(8,128)S(1)} fusion(bf16[512,1024]{1,0:T(8,128)(2,1)} %param.17, f32[16,2,512]{2,0,1:T(8,128)S(1)} %fusion.6), kind=kOutput, calls=%fused_computation.61 | convolution fusion | flops 16826368 | bytes 1179648 | tf_op jit(solution)/shard_map/dot_general | solution.py:186
  69.3 2.1 %collective-permute-start.3 = (f32[16,1024]{1,0:T(8,128)S(1)}, f32[16,1024]{1,0:T(8,128)S(1)}, u32[]{:S(2)}, u32[]{:S(2)}) collective-permute-start(f32[16,1024]{1,0:T(8,128)S(1)} %fusion.43), channel_id=1, source_target_pairs={{0,1},{1,0},{2,3},{3,2},{4,5},{5,4},{6,7},{7,6},{8,9},{9,8},{10,11... | collective-permute-start | bytes 196616 | tf_op jit(solution)/shard_map/ppermute | solution.py:28
  71.4 2.2 %collective-permute-done.3 = f32[16,1024]{1,0:T(8,128)S(1)} collective-permute-done((f32[16,1024]{1,0:T(8,128)S(1)}, f32[16,1024]{1,0:T(8,128)S(1)}, u32[]{:S(2)}, u32[]{:S(2)}) %collective-permute-start.3) | collective-permute-done | bytes 65568 | tf_op jit(solution)/shard_map/ppermute | solution.py:28
  73.7 3.6 %collective-permute-start.4 = (f32[16,1024]{1,0:T(8,128)S(1)}, f32[16,1024]{1,0:T(8,128)S(1)}, u32[]{:S(2)}, u32[]{:S(2)}) collective-permute-start(f32[16,1024]{1,0:T(8,128)S(1)} %add.92), channel_id=1, source_target_pairs={{0,2},{1,3},{2,0},{3,1},{4,6},{5,7},{6,4},{7,5},{8,10},{9,11},{10,... | collective-permute-start | bytes 196616 | tf_op jit(solution)/shard_map/ppermute | solution.py:28
  77.3 2.2 %collective-permute-done.4 = f32[16,1024]{1,0:T(8,128)S(1)} collective-permute-done((f32[16,1024]{1,0:T(8,128)S(1)}, f32[16,1024]{1,0:T(8,128)S(1)}, u32[]{:S(2)}, u32[]{:S(2)}) %collective-permute-start.4) | collective-permute-done | bytes 65568 | tf_op jit(solution)/shard_map/ppermute | solution.py:28
  79.6 4.0 %collective-permute-start.5 = (f32[16,1024]{1,0:T(8,128)S(1)}, f32[16,1024]{1,0:T(8,128)S(1)}, u32[]{:S(2)}, u32[]{:S(2)}) collective-permute-start(f32[16,1024]{1,0:T(8,128)S(1)} %add.93), channel_id=1, source_target_pairs={{0,6},{6,0},{1,7},{7,1},{2,4},{4,2},{3,5},{5,3},{8,14},{14,8},{9,1... | collective-permute-start | bytes 196616 | tf_op jit(solution)/shard_map/ppermute | solution.py:28
  83.7 0.6 pad_maximum_fusion.3
  84.3 1.9 %collective-permute-done.5 = f32[16,1024]{1,0:T(8,128)S(1)} collective-permute-done((f32[16,1024]{1,0:T(8,128)S(1)}, f32[16,1024]{1,0:T(8,128)S(1)}, u32[]{:S(2)}, u32[]{:S(2)}) %collective-permute-start.5) | collective-permute-done | bytes 65568 | tf_op jit(solution)/shard_map/ppermute | solution.py:28
  86.1 0.6 fusion.32
  (45 shorter events, 1.1 us)
Async XLA Ops:
  0.6 66.8 %copy-start = (bf16[1024,2,512]{2,1,0:T(2,128)(2,1)S(1)}, bf16[1024,2,512]{2,1,0:T(2,128)(2,1)}, u32[]{:S(2)}) copy-start(bf16[1024,2,512]{2,1,0:T(2,128)(2,1)} %param.16) | copy-start | bytes 6291460
  3.5 14.2 %all-to-all-start = ((bf16[32,16,128]{2,1,0:T(8,128)(2,1)}), bf16[32,16,128]{2,1,0:T(8,128)(2,1)S(1)}, u32[]{:S(2)}, u32[]{:S(2)}) async-start(bf16[32,16,128]{2,1,0:T(8,128)(2,1)} %broadcast_in_dim.133), calls=%async_computation | async-start | bytes 262144 | tf_op jit(solution)/shard_map/all_to_all | solution.py:36
  23.0 5.4 %copy-start.3 = (s32[128]{0:T(128)S(1)}, s32[128]{0:T(128)}, u32[]{:S(2)}) copy-start(s32[128]{0:T(128)} %param.20) | copy-start | bytes 1540
  28.0 19.1 %copy-start.1 = (bf16[128,1024]{1,0:T(8,128)(2,1)S(1)}, bf16[128,1024]{1,0:T(8,128)(2,1)}, u32[]{:S(2)}) copy-start(bf16[128,1024]{1,0:T(8,128)(2,1)} %param.14) | copy-start | bytes 786436
  28.3 39.1 %copy-start.2 = (f32[1024]{0:T(1024)S(1)}, f32[1024]{0:T(1024)}, u32[]{:S(2)}) copy-start(f32[1024]{0:T(1024)} %param.15) | copy-start | bytes 12292
  48.0 4.6 %collective-permute-start = (f32[16,1024]{1,0:T(8,128)S(1)}, f32[16,1024]{1,0:T(8,128)S(1)}, u32[]{:S(2)}, u32[]{:S(2)}) collective-permute-start(f32[16,1024]{1,0:T(8,128)S(1)} %fusion.51), channel_id=1, source_target_pairs={{0,1},{1,0},{2,3},{3,2},{4,5},{5,4},{6,7},{7,6},{8,9},{9,8},{10,11... | collective-permute-start | bytes 196616 | tf_op jit(solution)/shard_map/ppermute | solution.py:28
  52.6 7.0 %collective-permute-start.1 = (f32[16,1024]{1,0:T(8,128)S(1)}, f32[16,1024]{1,0:T(8,128)S(1)}, u32[]{:S(2)}, u32[]{:S(2)}) collective-permute-start(f32[16,1024]{1,0:T(8,128)S(1)} %add.86), channel_id=1, source_target_pairs={{0,2},{1,3},{2,0},{3,1},{4,6},{5,7},{6,4},{7,5},{8,10},{9,11},{10,... | collective-permute-start | bytes 196616 | tf_op jit(solution)/shard_map/ppermute | solution.py:28
  59.6 6.8 %collective-permute-start.2 = (f32[16,1024]{1,0:T(8,128)S(1)}, f32[16,1024]{1,0:T(8,128)S(1)}, u32[]{:S(2)}, u32[]{:S(2)}) collective-permute-start(f32[16,1024]{1,0:T(8,128)S(1)} %add.87), channel_id=1, source_target_pairs={{0,6},{6,0},{1,7},{7,1},{2,4},{4,2},{3,5},{5,3},{8,14},{14,8},{9,1... | collective-permute-start | bytes 196616 | tf_op jit(solution)/shard_map/ppermute | solution.py:28
  69.3 4.4 %collective-permute-start.3 = (f32[16,1024]{1,0:T(8,128)S(1)}, f32[16,1024]{1,0:T(8,128)S(1)}, u32[]{:S(2)}, u32[]{:S(2)}) collective-permute-start(f32[16,1024]{1,0:T(8,128)S(1)} %fusion.43), channel_id=1, source_target_pairs={{0,1},{1,0},{2,3},{3,2},{4,5},{5,4},{6,7},{7,6},{8,9},{9,8},{10,11... | collective-permute-start | bytes 196616 | tf_op jit(solution)/shard_map/ppermute | solution.py:28
  73.7 5.9 %collective-permute-start.4 = (f32[16,1024]{1,0:T(8,128)S(1)}, f32[16,1024]{1,0:T(8,128)S(1)}, u32[]{:S(2)}, u32[]{:S(2)}) collective-permute-start(f32[16,1024]{1,0:T(8,128)S(1)} %add.92), channel_id=1, source_target_pairs={{0,2},{1,3},{2,0},{3,1},{4,6},{5,7},{6,4},{7,5},{8,10},{9,11},{10,... | collective-permute-start | bytes 196616 | tf_op jit(solution)/shard_map/ppermute | solution.py:28
  79.6 6.5 %collective-permute-start.5 = (f32[16,1024]{1,0:T(8,128)S(1)}, f32[16,1024]{1,0:T(8,128)S(1)}, u32[]{:S(2)}, u32[]{:S(2)}) collective-permute-start(f32[16,1024]{1,0:T(8,128)S(1)} %add.93), channel_id=1, source_target_pairs={{0,6},{6,0},{1,7},{7,1},{2,4},{4,2},{3,5},{5,3},{8,14},{14,8},{9,1... | collective-permute-start | bytes 196616 | tf_op jit(solution)/shard_map/ppermute | solution.py:28

commit v11 on v9

--- a/solution.py
+++ b/solution.py
@@ -122,7 +122,12 @@
         axis=1,
     )
     onehot = member.astype(jnp.float32)
-    local_sums = jnp.einsum("pr,pc->rc", onehot, payload, precision=lax.Precision.HIGHEST)
+    payload_high = payload.astype(jnp.bfloat16)
+    payload_low = (payload - payload_high.astype(jnp.float32)).astype(jnp.bfloat16)
+    onehot_bf16 = onehot.astype(jnp.bfloat16)
+    local_sums = jnp.einsum(
+        "pr,pc->rc", onehot_bf16, payload_high, preferred_element_type=jnp.float32
+    ) + jnp.einsum("pr,pc->rc", onehot_bf16, payload_low, preferred_element_type=jnp.float32)
     home_max = lax.dynamic_slice_in_dim(local_max, home_row, local_rows, 0)
     self_weight = jnp.exp(self_scores - home_max)
     self_payload = jnp.concatenate(

time: 85.9 us -> 87.3 us (1.016)
  local copies, waits for them, and re-layouts: 5.91 us -> 6.99 us
where the time goes in v11:
time: 87.3 us; the launch traced here: 86 us
  starting transfers between devices  27.3 us (31%)
  waiting for transfers between devices  16.7 us (19%)
  blocking collectives  14.4 us (16%)
  matrix products  13.2 us (15%)
  local copies, waits for them, and re-layouts  6.99 us (8%)
  other arithmetic  6.48 us (7%)
  between operations  0.99 us (1%)
    ppermute x6, starting transfers between devices, butterfly_sum(): value = value + lax.ppermute(value, axis, pairs)  19.7 us
    ppermute x6, waiting for transfers between devices, butterfly_sum(): value = value + lax.ppermute(value, axis, pairs)  14.9 us
    all_to_all x1, blocking collectives, body(): received = lax.all_to_all(packed, 'dp', 0, 0, tiled=True)  14.4 us
    all_to_all x1, starting transfers between devices, exchange_gather(): gathered = lax.all_to_all(spread, axis, 0, 0, tiled=True)  7.62 us
    dot_general x1, matrix products, body(): jnp.einsum('ptc,pch->pth', key_rows, query_blocks, preferred_element_type...  4.54 us
    dot_general x1, matrix products, body(): jnp.einsum('pth,ptc->phc', raw.astype(jnp.bfloat16), value_rows, preferre...  3.48 us
    all_to_all x1, waiting for transfers between devices, exchange_gather(): gathered = lax.all_to_all(spread, axis, 0, 0, tiled=True)  1.81 us
  transfers between devices with their start and end apart: 7, of which 7 were waited for; matrix products, arithmetic and copies ran while one was open for 6% of the time, Pallas kernels for 0%

profile of v11, /device:TPU:2, one launch (start us, length us, event | category | flops | bytes accessed | tf_op | source)
XLA Modules:
  0.0 86.0 jit_solution(8050197255535466367)
XLA Ops:
  0.6 1.0 %fusion.23 = f32[16]{0:T(128)S(1)} fusion(bf16[16,1024]{1,0:T(8,128)(2,1)} %param.11), kind=kLoop, calls=%fused_computation.40 | loop fusion | flops 49136 | bytes 32832 | tf_op jit(solution)/shard_map/reduce_sum | solution.py:15
  1.7 1.6 %convolution_convert_fusion = bf16[16,3,128]{0,2,1:T(8,128)(2,1)S(1)} fusion(bf16[1024,3,128]{2,0,1:T(8,128)(2,1)} %param.13, bf16[16,1024]{1,0:T(8,128)(2,1)} %param.11, f32[1024]{0:T(1024)} %param.12, f32[16]{0:T(128)S(1)} %add_rsqrt_fusion.1), kind=kOutput, calls=%fused_computation.12 | convolution fusion | flops 12654592 | bytes 835648 | tf_op jit(solution)/shard_map/rd,dkc->rkc/dot_general | solution.py:79
  3.4 0.7 broadcast_in_dim.131
  4.1 7.6 %all-to-all-start = ((bf16[32,16,128]{2,1,0:T(8,128)(2,1)}), bf16[32,16,128]{2,1,0:T(8,128)(2,1)S(1)}, u32[]{:S(2)}, u32[]{:S(2)}) async-start(bf16[32,16,128]{2,1,0:T(8,128)(2,1)} %broadcast_in_dim.131), calls=%async_computation | async-start | bytes 262144 | tf_op jit(solution)/shard_map/all_to_all | solution.py:36
  11.7 0.7 broadcast_compare_fusion
  12.4 0.7 broadcast_maximum_fusion
  13.0 0.8 iota_compare_fusion
  13.8 0.7 broadcast_multiply_fusion.1
  14.5 1.6 %gather_fusion = s32[128]{0:T(128)S(1)} fusion(s32[512]{0:T(512)} %param.19, s32[1024]{0:T(1024)S(1)} %pad_clamp_fusion), kind=kCustom, calls=%fused_computation | custom fusion | bytes 1536 | tf_op jit(solution)/shard_map/gather | solution.py:104
  16.2 0.1 fusion.31
  16.3 0.2 dynamic_update_slice.6
  16.5 1.8 %all-to-all-done = bf16[32,16,128]{2,1,0:T(8,128)(2,1)S(1)} async-done(((bf16[32,16,128]{2,1,0:T(8,128)(2,1)}), bf16[32,16,128]{2,1,0:T(8,128)(2,1)S(1)}, u32[]{:S(2)}, u32[]{:S(2)}) %all-to-all-start) | async-done | bytes 131104 | tf_op jit(solution)/shard_map/all_to_all | solution.py:36
  18.3 0.7 gather_fusion.1
  19.0 4.5 %select_reduce_fusion.1 = (f32[128,2]{1,0:T(8,128)S(1)}, f32[128,2,128]{2,1,0:T(2,128)S(1)}) fusion(pred[128,128]{1,0:T(8,128)(4,1)S(1)} %fusion.31, bf16[2,128,128,128]{3,2,1,0:T(8,128)(2,1)} %param.18, pred[128,2]{0,1:T(4,128)(4,1)S(1)} %iota_compare_fusion.3, bf16[128,128]{1,0:T(8,128)(2,1)S(1)} %gather_fusion.1), kind=kOutput, calls=%fused_computation.28 | convolution fusion | flops 8519424 | bytes 4375808 | tf_op jit(solution)/shard_map/ptc,pch->pth/dot_general | solution.py:100
  23.6 0.2 select_reduce_fusion
  23.9 0.1 copy.105
  24.1 0.4 bitcast_reduce_fusion
  24.4 3.5 %fusion.14 = f32[128,128]{1,0:T(8,128)S(1)} fusion(bf16[2,128,128,128]{3,2,1,0:T(8,128)(2,1)} %param.18, pred[2,128]{1,0:T(4,128)(4,1)S(1)} %iota_compare_fusion.4, f32[128,2,128]{2,1,0:T(2,128)S(1)} %get-tuple-element.14, pred[128,128]{1,0:T(8,128)(4,1)S(1)} %fusion.31, f32[128,2]{1,0:T(8,128)S(1)} %get-tuple-element.13), kind=kOutput, calls=%fused_computation.15 | convolution fusion | flops 8536064 | bytes 4408576 | tf_op jit(solution)/shard_map/pth,ptc->phc/dot_general | solution.py:108
  27.9 0.7 gather_fusion.2
  28.9 0.3 fusion.18
  29.2 0.3 convolution_add_fusion
  29.5 0.7 add.92
  30.3 0.1 copy.108
  30.4 0.1 copy.109
  30.6 0.2 reshape.193
  30.8 14.4 %all_to_all.10 = f32[32,17,128]{2,1,0:T(8,128)S(1)} all-to-all(f32[32,17,128]{2,1,0:T(8,128)S(1)} %pad_maximum_fusion), channel_id=1, replica_groups=mesh['dp'=32,'mp'=8] {'dp'}, dimensions={0} | all-to-all | bytes 557056 | tf_op jit(solution)/shard_map/all_to_all | solution.py:154
  45.4 0.2 fusion.46
  45.7 0.2 copy.111
  45.9 0.6 broadcast_in_dim.143
  46.5 0.3 reshape.197
  46.9 1.1 %fusion.49 = f32[16,1024]{1,0:T(8,128)S(1)} fusion(bf16[128,1024]{1,0:T(8,128)(2,1)} %param.14, f32[16,128]{1,0:T(8,128)S(1)} %fusion.17, f32[16,128]{1,0:T(8,128)S(1)} %div.35), kind=kOutput, calls=%fused_computation.77 | convolution fusion | flops 4198400 | bytes 344064 | tf_op jit(solution)/shard_map/dot_general | solution.py:176
  48.0 1.9 %collective-permute-start = (f32[16,1024]{1,0:T(8,128)S(1)}, f32[16,1024]{1,0:T(8,128)S(1)}, u32[]{:S(2)}, u32[]{:S(2)}) collective-permute-start(f32[16,1024]{1,0:T(8,128)S(1)} %fusion.49), channel_id=1, source_target_pairs={{0,1},{1,0},{2,3},{3,2},{4,5},{5,4},{6,7},{7,6},{8,9},{9,8},{10,11... | collective-permute-start | bytes 196616 | tf_op jit(solution)/shard_map/ppermute | solution.py:28
  49.9 2.7 %collective-permute-done = f32[16,1024]{1,0:T(8,128)S(1)} collective-permute-done((f32[16,1024]{1,0:T(8,128)S(1)}, f32[16,1024]{1,0:T(8,128)S(1)}, u32[]{:S(2)}, u32[]{:S(2)}) %collective-permute-start) | collective-permute-done | bytes 65568 | tf_op jit(solution)/shard_map/ppermute | solution.py:28
  52.6 3.4 %collective-permute-start.1 = (f32[16,1024]{1,0:T(8,128)S(1)}, f32[16,1024]{1,0:T(8,128)S(1)}, u32[]{:S(2)}, u32[]{:S(2)}) collective-permute-start(f32[16,1024]{1,0:T(8,128)S(1)} %add.93), channel_id=1, source_target_pairs={{0,2},{1,3},{2,0},{3,1},{4,6},{5,7},{6,4},{7,5},{8,10},{9,11},{10,... | collective-permute-start | bytes 196616 | tf_op jit(solution)/shard_map/ppermute | solution.py:28
  56.0 3.6 %collective-permute-done.1 = f32[16,1024]{1,0:T(8,128)S(1)} collective-permute-done((f32[16,1024]{1,0:T(8,128)S(1)}, f32[16,1024]{1,0:T(8,128)S(1)}, u32[]{:S(2)}, u32[]{:S(2)}) %collective-permute-start.1) | collective-permute-done | bytes 65568 | tf_op jit(solution)/shard_map/ppermute | solution.py:28
  59.7 4.6 %collective-permute-start.2 = (f32[16,1024]{1,0:T(8,128)S(1)}, f32[16,1024]{1,0:T(8,128)S(1)}, u32[]{:S(2)}, u32[]{:S(2)}) collective-permute-start(f32[16,1024]{1,0:T(8,128)S(1)} %add.94), channel_id=1, source_target_pairs={{0,6},{6,0},{1,7},{7,1},{2,4},{4,2},{3,5},{5,3},{8,14},{14,8},{9,1... | collective-permute-start | bytes 196616 | tf_op jit(solution)/shard_map/ppermute | solution.py:28
  64.2 2.3 %collective-permute-done.2 = f32[16,1024]{1,0:T(8,128)S(1)} collective-permute-done((f32[16,1024]{1,0:T(8,128)S(1)}, f32[16,1024]{1,0:T(8,128)S(1)}, u32[]{:S(2)}, u32[]{:S(2)}) %collective-permute-start.2) | collective-permute-done | bytes 65568 | tf_op jit(solution)/shard_map/ppermute | solution.py:28
  66.5 0.1 fusion.27
  66.7 0.4 fusion.6
  67.1 1.5 %fusion.44 = f32[16,1024]{1,0:T(8,128)S(1)} fusion(bf16[512,1024]{1,0:T(8,128)(2,1)} %param.17, f32[16,2,512]{2,0,1:T(8,128)S(1)} %fusion.6), kind=kOutput, calls=%fused_computation.68 | convolution fusion | flops 16826368 | bytes 1179648 | tf_op jit(solution)/shard_map/dot_general | solution.py:184
  68.6 2.1 %collective-permute-start.3 = (f32[16,1024]{1,0:T(8,128)S(1)}, f32[16,1024]{1,0:T(8,128)S(1)}, u32[]{:S(2)}, u32[]{:S(2)}) collective-permute-start(f32[16,1024]{1,0:T(8,128)S(1)} %fusion.44), channel_id=1, source_target_pairs={{0,1},{1,0},{2,3},{3,2},{4,5},{5,4},{6,7},{7,6},{8,9},{9,8},{10,11... | collective-permute-start | bytes 196616 | tf_op jit(solution)/shard_map/ppermute | solution.py:28
  70.7 2.2 %collective-permute-done.3 = f32[16,1024]{1,0:T(8,128)S(1)} collective-permute-done((f32[16,1024]{1,0:T(8,128)S(1)}, f32[16,1024]{1,0:T(8,128)S(1)}, u32[]{:S(2)}, u32[]{:S(2)}) %collective-permute-start.3) | collective-permute-done | bytes 65568 | tf_op jit(solution)/shard_map/ppermute | solution.py:28
  73.0 3.6 %collective-permute-start.4 = (f32[16,1024]{1,0:T(8,128)S(1)}, f32[16,1024]{1,0:T(8,128)S(1)}, u32[]{:S(2)}, u32[]{:S(2)}) collective-permute-start(f32[16,1024]{1,0:T(8,128)S(1)} %add.99), channel_id=1, source_target_pairs={{0,2},{1,3},{2,0},{3,1},{4,6},{5,7},{6,4},{7,5},{8,10},{9,11},{10,... | collective-permute-start | bytes 196616 | tf_op jit(solution)/shard_map/ppermute | solution.py:28
  76.7 2.1 %collective-permute-done.4 = f32[16,1024]{1,0:T(8,128)S(1)} collective-permute-done((f32[16,1024]{1,0:T(8,128)S(1)}, f32[16,1024]{1,0:T(8,128)S(1)}, u32[]{:S(2)}, u32[]{:S(2)}) %collective-permute-start.4) | collective-permute-done | bytes 65568 | tf_op jit(solution)/shard_map/ppermute | solution.py:28
  78.9 4.0 %collective-permute-start.5 = (f32[16,1024]{1,0:T(8,128)S(1)}, f32[16,1024]{1,0:T(8,128)S(1)}, u32[]{:S(2)}, u32[]{:S(2)}) collective-permute-start(f32[16,1024]{1,0:T(8,128)S(1)} %add.100), channel_id=1, source_target_pairs={{0,6},{6,0},{1,7},{7,1},{2,4},{4,2},{3,5},{5,3},{8,14},{14,8},{9,1... | collective-permute-start | bytes 196616 | tf_op jit(solution)/shard_map/ppermute | solution.py:28
  82.9 0.6 pad_maximum_fusion.2
  83.5 1.9 %collective-permute-done.5 = f32[16,1024]{1,0:T(8,128)S(1)} collective-permute-done((f32[16,1024]{1,0:T(8,128)S(1)}, f32[16,1024]{1,0:T(8,128)S(1)}, u32[]{:S(2)}, u32[]{:S(2)}) %collective-permute-start.5) | collective-permute-done | bytes 65568 | tf_op jit(solution)/shard_map/ppermute | solution.py:28
  85.4 0.6 fusion.30
  (48 shorter events, 1.3 us)
Async XLA Ops:
  0.6 66.0 %copy-start = (bf16[1024,2,512]{2,1,0:T(2,128)(2,1)S(1)}, bf16[1024,2,512]{2,1,0:T(2,128)(2,1)}, u32[]{:S(2)}) copy-start(bf16[1024,2,512]{2,1,0:T(2,128)(2,1)} %param.16) | copy-start | bytes 6291460
  4.1 14.2 %all-to-all-start = ((bf16[32,16,128]{2,1,0:T(8,128)(2,1)}), bf16[32,16,128]{2,1,0:T(8,128)(2,1)S(1)}, u32[]{:S(2)}, u32[]{:S(2)}) async-start(bf16[32,16,128]{2,1,0:T(8,128)(2,1)} %broadcast_in_dim.131), calls=%async_computation | async-start | bytes 262144 | tf_op jit(solution)/shard_map/all_to_all | solution.py:36
  23.6 5.3 %copy-start.2 = (s32[128]{0:T(128)S(1)}, s32[128]{0:T(128)}, u32[]{:S(2)}) copy-start(s32[128]{0:T(128)} %param.20) | copy-start | bytes 1540
  28.7 37.8 %copy-start.1 = (bf16[16,1024]{1,0:T(8,128)(2,1)S(1)}, bf16[16,1024]{1,0:T(8,128)(2,1)}, u32[]{:S(2)}) copy-start(bf16[16,1024]{1,0:T(8,128)(2,1)} %param.11) | copy-start | bytes 98308
  28.9 37.8 %copy-start.3 = (f32[1024]{0:T(1024)S(1)}, f32[1024]{0:T(1024)}, u32[]{:S(2)}) copy-start(f32[1024]{0:T(1024)} %param.15) | copy-start | bytes 12292
  48.0 4.6 %collective-permute-start = (f32[16,1024]{1,0:T(8,128)S(1)}, f32[16,1024]{1,0:T(8,128)S(1)}, u32[]{:S(2)}, u32[]{:S(2)}) collective-permute-start(f32[16,1024]{1,0:T(8,128)S(1)} %fusion.49), channel_id=1, source_target_pairs={{0,1},{1,0},{2,3},{3,2},{4,5},{5,4},{6,7},{7,6},{8,9},{9,8},{10,11... | collective-permute-start | bytes 196616 | tf_op jit(solution)/shard_map/ppermute | solution.py:28
  52.6 7.0 %collective-permute-start.1 = (f32[16,1024]{1,0:T(8,128)S(1)}, f32[16,1024]{1,0:T(8,128)S(1)}, u32[]{:S(2)}, u32[]{:S(2)}) collective-permute-start(f32[16,1024]{1,0:T(8,128)S(1)} %add.93), channel_id=1, source_target_pairs={{0,2},{1,3},{2,0},{3,1},{4,6},{5,7},{6,4},{7,5},{8,10},{9,11},{10,... | collective-permute-start | bytes 196616 | tf_op jit(solution)/shard_map/ppermute | solution.py:28
  59.7 6.8 %collective-permute-start.2 = (f32[16,1024]{1,0:T(8,128)S(1)}, f32[16,1024]{1,0:T(8,128)S(1)}, u32[]{:S(2)}, u32[]{:S(2)}) collective-permute-start(f32[16,1024]{1,0:T(8,128)S(1)} %add.94), channel_id=1, source_target_pairs={{0,6},{6,0},{1,7},{7,1},{2,4},{4,2},{3,5},{5,3},{8,14},{14,8},{9,1... | collective-permute-start | bytes 196616 | tf_op jit(solution)/shard_map/ppermute | solution.py:28
  68.6 4.4 %collective-permute-start.3 = (f32[16,1024]{1,0:T(8,128)S(1)}, f32[16,1024]{1,0:T(8,128)S(1)}, u32[]{:S(2)}, u32[]{:S(2)}) collective-permute-start(f32[16,1024]{1,0:T(8,128)S(1)} %fusion.44), channel_id=1, source_target_pairs={{0,1},{1,0},{2,3},{3,2},{4,5},{5,4},{6,7},{7,6},{8,9},{9,8},{10,11... | collective-permute-start | bytes 196616 | tf_op jit(solution)/shard_map/ppermute | solution.py:28
  73.0 5.9 %collective-permute-start.4 = (f32[16,1024]{1,0:T(8,128)S(1)}, f32[16,1024]{1,0:T(8,128)S(1)}, u32[]{:S(2)}, u32[]{:S(2)}) collective-permute-start(f32[16,1024]{1,0:T(8,128)S(1)} %add.99), channel_id=1, source_target_pairs={{0,2},{1,3},{2,0},{3,1},{4,6},{5,7},{6,4},{7,5},{8,10},{9,11},{10,... | collective-permute-start | bytes 196616 | tf_op jit(solution)/shard_map/ppermute | solution.py:28
  78.9 6.5 %collective-permute-start.5 = (f32[16,1024]{1,0:T(8,128)S(1)}, f32[16,1024]{1,0:T(8,128)S(1)}, u32[]{:S(2)}, u32[]{:S(2)}) collective-permute-start(f32[16,1024]{1,0:T(8,128)S(1)} %add.100), channel_id=1, source_target_pairs={{0,6},{6,0},{1,7},{7,1},{2,4},{4,2},{3,5},{5,3},{8,14},{14,8},{9,1... | collective-permute-start | bytes 196616 | tf_op jit(solution)/shard_map/ppermute | solution.py:28
